TPU v7x, 128 devices: a whole 4x4x4 slice. The times are simulated.
128 devices in a mesh: rep: 4 (over x), shard: 32 (over z, y, core).
Axes of the slice: x: 4, y: 4, z: 4, core: 2. Of those that a mesh axis runs over, the one named last changes fastest.
Arguments:
- features: bfloat16 [65536, 1024], P(('rep', 'shard')), may hold values from -6 to 6
- cotangent: bfloat16 [65536, 1024], P(('rep', 'shard')), may hold values from -6 to 6
- cross_weight: bfloat16 [1024, 1024], replicated, may hold values from -0.1875 to 0.1875
- cross_bias: float32 [1024], replicated, may hold values from -3 to 3
- emb_table: float32 [131072, 128], P('shard'), may hold values from -6 to 6
- row_accum: float32 [131072], P('shard'), may hold values from 0.5 to 50
- send_bags: int32 [128, 32, 256], P(('rep', 'shard')), may hold values from 0 to 3583, as said below
- slot_counts: int32 [128, 32], P(('rep', 'shard')), may hold values from 64 to 256, as said below
- recv_rows: int32 [128, 32, 256], P(('rep', 'shard')), may hold values from 0 to 4095, as said below
- touched_rows: int32 [32, 2048], P('shard'), may hold values from 0 to 4095, as said below
Outputs:
- weight_grad: float32 [1024, 1024], replicated
- bias_grad: float32 [1024], replicated
- dense_grad: bfloat16 [65536, 128], P(('rep', 'shard'))
- new_table: float32 [131072, 128], P('shard')
- new_accum: float32 [131072], P('shard')
Inputs may be any that keep to these rules, and one draw needn't show every extreme that they name: `send_bags`: bag b * 7 + f of a device is feature f of its sample b. The first slot_counts[d, s] slots of a block are live; in each replica group some shard receives 256 live slots from every device of the group. `recv_rows`: every slot, live or not, names a row listed in touched_rows for the owner's shard. `touched_rows`: ascending and distinct.
All inputs are finite; a program needn't handle non-finite values.
Results may differ from a plain program's by a relative error of at most 0.0055.
Values may be sent and summed in bfloat16 or wider, within the bound.
No kernel may reach another device: no remote copies, remote signals or barrier semaphores. Data moves between devices by JAX's collectives and lax.ppermute only.
A program may use at most 128 MiB of HBM per device.

v0:
```python
import math

import jax
import jax.numpy as jnp
from jax import lax
from jax.sharding import PartitionSpec as P

learn_rate = 0.5
keep_rate = 0.9


def adagrad_rows(table_rows, accum_rows, grads):
    new_accum = accum_rows + jnp.mean(grads * grads, axis=1)
    new_rows = keep_rate * table_rows - learn_rate * grads / jnp.sqrt(new_accum)[:, None]
    return (new_rows, new_accum)


def blocked(count, fn):
    step_rows = math.gcd(count, 512)
    index_blocks = jnp.arange(count, dtype=jnp.int32).reshape(-1, step_rows)
    result = lax.map(fn, index_blocks)
    return result.reshape((count,) + result.shape[2:])


def per_device(
    features,
    cotangent,
    cross_weight,
    cross_bias,
    emb_table,
    row_accum,
    send_bags,
    slot_counts,
    recv_rows,
    touched_rows,
):
    width = emb_table.shape[1]
    shard_rows = emb_table.shape[0]
    total_tokens = features.shape[0] * lax.axis_size("rep") * lax.axis_size("shard")
    scale = 1.0 / jnp.sqrt(jnp.float32(total_tokens))
    linear = jnp.dot(features, cross_weight, preferred_element_type=jnp.float32) + cross_bias
    cot_f = cotangent.astype(jnp.float32)
    gated = (cot_f * features.astype(jnp.float32)).astype(jnp.bfloat16)
    weight_part = lax.dot_general(
        features, gated, (((0,), (0,)), ((), ())), preferred_element_type=jnp.float32
    )
    bias_part = jnp.sum(gated.astype(jnp.float32), axis=0)
    backprop = lax.dot_general(
        gated, cross_weight, (((1,), (1,)), ((), ())), preferred_element_type=jnp.float32
    )
    input_grad = cot_f * linear + backprop + cot_f
    dense_grad = input_grad[:, :width].astype(jnp.bfloat16)
    pooled = input_grad[:, width:].astype(jnp.bfloat16).reshape(-1, width)
    bag_ids = send_bags[0]
    shard_count = bag_ids.shape[0]
    slot_total = bag_ids.shape[1]
    live_mask = jnp.arange(slot_total, dtype=jnp.int32)[None, :] < slot_counts[0][:, None]
    flat_bags = jnp.where(live_mask, bag_ids, -1).reshape(-1)
    bag_range = jnp.arange(pooled.shape[0], dtype=jnp.int32)

    def pick_bags(positions):
        select = (flat_bags[positions][:, None] == bag_range[None, :]).astype(jnp.bfloat16)
        return jnp.dot(select, pooled, preferred_element_type=jnp.float32).astype(jnp.bfloat16)

    outgoing = blocked(shard_count * slot_total, pick_bags).reshape(shard_count, slot_total, width)
    incoming = lax.all_to_all(outgoing, "shard", split_axis=0, concat_axis=0, tiled=True)
    weight_sum, bias_sum = lax.psum((weight_part, bias_part), ("rep", "shard"))
    weight_grad = weight_sum * scale
    bias_grad = bias_sum * scale
    incoming_rows = incoming.reshape(-1, width)
    slot_rows = recv_rows[0].reshape(-1)
    touched = touched_rows[0]
    row_range = jnp.arange(shard_rows, dtype=jnp.int32)
    marks = jnp.any(row_range[:, None] == touched[None, :], axis=1)

    def row_block(row_ids):
        select = (row_ids[:, None] == slot_rows[None, :]).astype(jnp.bfloat16)
        return jnp.dot(select, incoming_rows, preferred_element_type=jnp.float32)

    local_sums = blocked(shard_rows, row_block)
    row_grads = lax.psum(local_sums.astype(jnp.bfloat16), "rep").astype(jnp.float32)
    upd_table, upd_accum = adagrad_rows(emb_table, row_accum, row_grads)
    new_table = jnp.where(marks[:, None], upd_table, emb_table)
    new_accum = jnp.where(marks, upd_accum, row_accum)
    return (weight_grad, bias_grad, dense_grad, new_table, new_accum)


def solution(mesh):
    in_specs = (
        P(("rep", "shard"), None),
        P(("rep", "shard"), None),
        P(),
        P(),
        P("shard", None),
        P("shard"),
        P(("rep", "shard"), None, None),
        P(("rep", "shard"), None),
        P(("rep", "shard"), None, None),
        P("shard", None),
    )
    out_specs = (P(), P(), P(("rep", "shard"), None), P("shard", None), P("shard"))
    return jax.shard_map(
        per_device, mesh=mesh, in_specs=in_specs, out_specs=out_specs, check_vma=False
    )
```

profile of v0, /device:TPU:0, one launch (start us, length us, event | category | flops | bytes accessed | tf_op | source)
XLA Modules:
  0.0 358.1 jit_solution(6436038658471441879)
XLA Ops:
  7.2 0.9 iota_compare_fusion.9
  8.1 0.8 copy.19
  8.9 2.6 fusion.29
  11.6 1.5 fusion.24
  13.1 1.0 copy-done.3
  14.1 1.0 slice.13
  15.1 2.7 reshape.80
  17.8 102.1 %while.22 = (s32[]{:T(128)}, bf16[16,512,128]{2,1,0:T(8,128)(2,1)}, s32[16,512]{1,0:T(8,128)S(1)}, s32[8192]{0:T(1024)S(1)}, bf16[3584,128]{1,0:T(8,128)(2,1)}, /*index=5*/s32[]{:T(128)}) while((s32[]{:T(128)}, bf16[16,512,128]{2,1,0:T(8,128)(2,1)}, s32[16,512]{1,0:T(8,128)S(1)}, s32[8192]{0:T(1024)S(1)}, ...), condition=%wide.region_5.6_spmd.clone, body=%wide.region_4.5_spmd.clone.sunk | while | flops 471665152 | bytes 1067093 | solution.py:21
  17.8 3.1 gather_fusion
  21.0 3.2 fusion.45
  24.2 3.1 gather_fusion
  27.4 3.2 fusion.45
  30.6 3.1 gather_fusion
  33.8 3.2 fusion.45
  37.0 3.1 gather_fusion
  40.1 3.2 fusion.45
  43.4 3.1 gather_fusion
  46.5 3.2 fusion.45
  49.8 3.1 gather_fusion
  52.9 3.2 fusion.45
  56.1 3.1 gather_fusion
  59.3 3.2 fusion.45
  62.5 3.1 gather_fusion
  65.7 3.2 fusion.45
  68.9 3.1 gather_fusion
  72.1 3.2 fusion.45
  75.3 3.1 gather_fusion
  78.4 3.2 fusion.45
  81.7 3.1 gather_fusion
  84.8 3.2 fusion.45
  88.1 3.1 gather_fusion
  91.2 3.2 fusion.45
  94.4 3.1 gather_fusion
  97.6 3.2 fusion.45
  100.8 3.1 gather_fusion
  104.0 3.2 fusion.45
  107.2 3.1 gather_fusion
  110.4 3.2 fusion.45
  113.6 3.1 gather_fusion
  116.7 3.2 fusion.45
  120.0 8.6 %all-to-all-start = ((bf16[32,256,128]{2,1,0:T(8,128)(2,1)}), bf16[32,256,128]{2,1,0:T(8,128)(2,1)}, u32[]{:S(2)}, u32[]{:S(2)}) async-start(bf16[32,256,128]{2,1,0:T(8,128)(2,1)} %bitcast.47), calls=%async_computation | async-start | bytes 4194304 | tf_op jit(solution)/shard_map/all_to_all | solution.py:66
  128.5 0.0 all-reduce.3.cloned.1.call-start
  128.6 4.5 %convolution_bitcast_fusion = f32[1024,1024]{0,1:T(8,128)} fusion(bf16[512,1024]{1,0:T(8,128)(2,1)S(1)} %copy-done.1, bf16[512,1024]{1,0:T(8,128)(2,1)} %param.15), kind=kOutput, calls=%fused_computation.24 | convolution fusion | flops 1075838976 | bytes 6291456 | tf_op jit(solution)/shard_map/dot_general | solution.py:44
  133.2 1.6 convert_reduce_fusion
  134.8 79.4 %psum.22 = f32[1024]{0:T(1024)S(1)} all-reduce(f32[1024]{0:T(1024)S(1)} %convert_reduce_fusion), channel_id=1, replica_groups=mesh['rep'=4,'shard'=32] {'rep','shard'}, use_global_device_ids=true, to_apply=%region_2.3 | all-reduce | flops 1024 | bytes 8192 | tf_op jit(solution)/shard_map/psum | solution.py:67
  214.2 37.5 %while.21 = (s32[]{:T(128)}, bf16[8,512,128]{2,1,0:T(8,128)(2,1)}, s32[8,512]{1,0:T(8,128)S(1)}, s32[1,32,256]{2,1,0:T(8,128)S(1)}, bf16[8192,128]{1,0:T(8,128)(2,1)}, /*index=5*/s32[]{:T(128)}) while((s32[]{:T(128)}, bf16[8,512,128]{2,1,0:T(8,128)(2,1)}, s32[8,512]{1,0:T(8,128)S(1)}, s32[1,32,256]{2,1,0:T(8,128)S(1)}, ...), condition=%wide.region_7.8_spmd, body=%wide.region_6.7_spmd.sunk | while | flops 1077936128 | bytes 2463829 | solution.py:21
  214.3 4.6 %fusion.43 = bf16[8,512,128]{2,1,0:T(8,128)(2,1)} fusion(bf16[8,512,128]{2,1,0:T(8,128)(2,1)} %get-tuple-element.202, s32[]{:T(128)S(6)} %copy.33, bf16[8192,128]{1,0:T(8,128)(2,1)} %get-tuple-element.211, s32[8192]{0:T(1024)S(1)} %bitcast.50, s32[512]{0:T(512)S(1)} %bitcast.53), kind=kOutput, calls=%fused_computation.7.clone.1 | convolution fusion | flops 1077936128 | bytes 2394116 | tf_op jit(solution)/shard_map/while/body/eval_jaxpr/dot_general | solution.py:78
  219.0 4.6 %fusion.43 = bf16[8,512,128]{2,1,0:T(8,128)(2,1)} fusion(bf16[8,512,128]{2,1,0:T(8,128)(2,1)} %get-tuple-element.202, s32[]{:T(128)S(6)} %copy.33, bf16[8192,128]{1,0:T(8,128)(2,1)} %get-tuple-element.211, s32[8192]{0:T(1024)S(1)} %bitcast.50, s32[512]{0:T(512)S(1)} %bitcast.53), kind=kOutput, calls=%fused_computation.7.clone.1 | convolution fusion | flops 1077936128 | bytes 2394116 | tf_op jit(solution)/shard_map/while/body/eval_jaxpr/dot_general | solution.py:78
  223.6 4.6 %fusion.43 = bf16[8,512,128]{2,1,0:T(8,128)(2,1)} fusion(bf16[8,512,128]{2,1,0:T(8,128)(2,1)} %get-tuple-element.202, s32[]{:T(128)S(6)} %copy.33, bf16[8192,128]{1,0:T(8,128)(2,1)} %get-tuple-element.211, s32[8192]{0:T(1024)S(1)} %bitcast.50, s32[512]{0:T(512)S(1)} %bitcast.53), kind=kOutput, calls=%fused_computation.7.clone.1 | convolution fusion | flops 1077936128 | bytes 2394116 | tf_op jit(solution)/shard_map/while/body/eval_jaxpr/dot_general | solution.py:78
  228.3 4.6 %fusion.43 = bf16[8,512,128]{2,1,0:T(8,128)(2,1)} fusion(bf16[8,512,128]{2,1,0:T(8,128)(2,1)} %get-tuple-element.202, s32[]{:T(128)S(6)} %copy.33, bf16[8192,128]{1,0:T(8,128)(2,1)} %get-tuple-element.211, s32[8192]{0:T(1024)S(1)} %bitcast.50, s32[512]{0:T(512)S(1)} %bitcast.53), kind=kOutput, calls=%fused_computation.7.clone.1 | convolution fusion | flops 1077936128 | bytes 2394116 | tf_op jit(solution)/shard_map/while/body/eval_jaxpr/dot_general | solution.py:78
  233.0 4.6 %fusion.43 = bf16[8,512,128]{2,1,0:T(8,128)(2,1)} fusion(bf16[8,512,128]{2,1,0:T(8,128)(2,1)} %get-tuple-element.202, s32[]{:T(128)S(6)} %copy.33, bf16[8192,128]{1,0:T(8,128)(2,1)} %get-tuple-element.211, s32[8192]{0:T(1024)S(1)} %bitcast.50, s32[512]{0:T(512)S(1)} %bitcast.53), kind=kOutput, calls=%fused_computation.7.clone.1 | convolution fusion | flops 1077936128 | bytes 2394116 | tf_op jit(solution)/shard_map/while/body/eval_jaxpr/dot_general | solution.py:78
  237.7 4.6 %fusion.43 = bf16[8,512,128]{2,1,0:T(8,128)(2,1)} fusion(bf16[8,512,128]{2,1,0:T(8,128)(2,1)} %get-tuple-element.202, s32[]{:T(128)S(6)} %copy.33, bf16[8192,128]{1,0:T(8,128)(2,1)} %get-tuple-element.211, s32[8192]{0:T(1024)S(1)} %bitcast.50, s32[512]{0:T(512)S(1)} %bitcast.53), kind=kOutput, calls=%fused_computation.7.clone.1 | convolution fusion | flops 1077936128 | bytes 2394116 | tf_op jit(solution)/shard_map/while/body/eval_jaxpr/dot_general | solution.py:78
  242.3 4.6 %fusion.43 = bf16[8,512,128]{2,1,0:T(8,128)(2,1)} fusion(bf16[8,512,128]{2,1,0:T(8,128)(2,1)} %get-tuple-element.202, s32[]{:T(128)S(6)} %copy.33, bf16[8192,128]{1,0:T(8,128)(2,1)} %get-tuple-element.211, s32[8192]{0:T(1024)S(1)} %bitcast.50, s32[512]{0:T(512)S(1)} %bitcast.53), kind=kOutput, calls=%fused_computation.7.clone.1 | convolution fusion | flops 1077936128 | bytes 2394116 | tf_op jit(solution)/shard_map/while/body/eval_jaxpr/dot_general | solution.py:78
  247.0 4.7 %fusion.43 = bf16[8,512,128]{2,1,0:T(8,128)(2,1)} fusion(bf16[8,512,128]{2,1,0:T(8,128)(2,1)} %get-tuple-element.202, s32[]{:T(128)S(6)} %copy.33, bf16[8192,128]{1,0:T(8,128)(2,1)} %get-tuple-element.211, s32[8192]{0:T(1024)S(1)} %bitcast.50, s32[512]{0:T(512)S(1)} %bitcast.53), kind=kOutput, calls=%fused_computation.7.clone.1 | convolution fusion | flops 1077936128 | bytes 2394116 | tf_op jit(solution)/shard_map/while/body/eval_jaxpr/dot_general | solution.py:78
  251.7 0.6 broadcast_multiply_fusion.1
  252.3 1.6 slice.12
  253.9 4.1 %fusion.17 = pred[4096]{0:T(1024)(128)(4,1)S(1)} fusion(s32[2048]{0:T(1024)S(1)} %bitcast.56), kind=kLoop, calls=%fused_computation.18 | loop fusion | flops 16773120 | bytes 12288 | tf_op jit(solution)/shard_map/reduce_or | solution.py:74
  258.0 39.7 %all-reduce.3.cloned.1.call-done = f32[1024,1024]{0,1:T(8,128)} async-done(((f32[1024,1024]{0,1:T(8,128)}), f32[1024,1024]{0,1:T(8,128)}) %all-reduce.3.cloned.1.call-update) | async-done | bytes 4194320 | tf_op jit(solution)/shard_map/psum | solution.py:67
  297.7 5.0 %broadcast_multiply_fusion = f32[1024,1024]{0,1:T(8,128)} fusion(f32[1024,1024]{0,1:T(8,128)} %all-reduce.3.cloned.1.call-done), kind=kLoop, calls=%fused_computation.33 | loop fusion | flops 1048576 | bytes 8388608 | tf_op jit(solution)/shard_map/mul | solution.py:68
  302.7 5.4 %copy.17 = f32[1024,1024]{1,0:T(8,128)} copy(f32[1024,1024]{0,1:T(8,128)} %broadcast_multiply_fusion) | data formatting | bytes 8388608
  308.0 36.2 %all-reduce.5.cloned.1.call-done = bf16[4096,128]{1,0:T(8,128)(2,1)} async-done(((bf16[4096,128]{1,0:T(8,128)(2,1)}), bf16[4096,128]{1,0:T(8,128)(2,1)}) %all-reduce.5.cloned.1.call-update) | async-done | bytes 1048592 | tf_op jit(solution)/shard_map/psum | solution.py:81
  344.3 1.8 fusion.21
  346.1 0.6 fusion.27
  346.8 4.5 %fusion.20 = f32[4096,128]{1,0:T(8,128)} fusion(f32[4096,128]{1,0:T(8,128)} %param.18, bf16[4096,128]{1,0:T(8,128)(2,1)} %all-reduce.5.cloned.1.call-done, f32[4096]{0:T(1024)S(1)} %get-tuple-element.114, pred[4096]{0:T(1024)(128)(4,1)S(1)} %fusion.17), kind=kLoop, calls=%fused_computation.27 | loop fusion | flops 3145728 | bytes 5263360 | tf_op jit(solution)/shard_map/jit(_where)/select_n | solution.py:83
  (73 shorter events, 0.6 us)
Async XLA Ops:
  7.2 1.7 copy-start
  8.9 2.7 copy-start.1
  8.9 2.7 copy-start.2
  8.9 2.7 copy-start.7
  13.1 1.0 copy-start.3
  120.0 94.2 %all-to-all-start = ((bf16[32,256,128]{2,1,0:T(8,128)(2,1)}), bf16[32,256,128]{2,1,0:T(8,128)(2,1)}, u32[]{:S(2)}, u32[]{:S(2)}) async-start(bf16[32,256,128]{2,1,0:T(8,128)(2,1)} %bitcast.47), calls=%async_computation | async-start | bytes 4194304 | tf_op jit(solution)/shard_map/all_to_all | solution.py:66
  128.5 169.1 %all-reduce.3.cloned.1.call-start = ((), (), s32[]{:S(2)}) async-start(), calls=%async_computation.1 | async-start | bytes 8388608 | tf_op jit(solution)/shard_map/psum | solution.py:67
  133.2 81.0 %copy-start.4 = (s32[1,32,256]{2,1,0:T(8,128)S(1)}, s32[1,32,256]{2,1,0:T(8,128)}, u32[]{:S(2)}) copy-start(s32[1,32,256]{2,1,0:T(8,128)} %param.22) | copy-start | bytes 98308
  133.2 211.1 %all-reduce.5.cloned.1.call-start = ((), (), s32[]{:S(2)}) async-start(), calls=%async_computation.2 | async-start | bytes 2097152 | tf_op jit(solution)/shard_map/psum | solution.py:81
  214.2 39.7 %copy-start.6 = (s32[1,2048]{1,0:T(1,128)S(1)}, s32[1,2048]{1,0:T(1,128)}, u32[]{:S(2)}) copy-start(s32[1,2048]{1,0:T(1,128)} %param.23) | copy-start | bytes 24580
  302.7 43.5 %copy-start.5 = (f32[4096]{0:T(1024)S(1)}, f32[4096]{0:T(1024)}, u32[]{:S(2)}) copy-start(f32[4096]{0:T(1024)} %param.19) | copy-start | bytes 49156
Sparse Core Ops, SparseCore 0:
  134.8 162.7 all-reduce.2
  300.0 44.2 all-reduce.4
where the time goes:
time: 360 us; the launch traced here: 358 us
  matrix products  97.1 us (27%)
  blocking collectives  79.4 us (22%)
  waiting for transfers between devices  76 us (21%)
  local copies, waits for them, and re-layouts  63 us (18%)
  other arithmetic  19.4 us (5%)
  between operations  14.2 us (4%)
  starting transfers between devices  8.65 us (2%)
    psum x1, blocking collectives, per_device(): weight_sum, bias_sum = lax.psum((weight_part, bias_part), ('rep', 'shard'))  79.4 us
    dot_general x16, matrix products, pick_bags(): jnp.dot(select, pooled, preferred_element_type=jnp.float32)  51.3 us
    gather x16, local copies, waits for them, and re-layouts, pick_bags(): flat_bags[positions][:, None] == bag_range[None, :]  50.3 us
    psum x1, waiting for transfers between devices, per_device(): weight_sum, bias_sum = lax.psum((weight_part, bias_part), ('rep', 'shard'))  39.7 us
    dot_general x8, matrix products, row_block(): return jnp.dot(select, incoming_rows, preferred_element_type=jnp.float32)  37.1 us
    psum x1, waiting for transfers between devices, per_device(): lax.psum(local_sums.astype(jnp.bfloat16), 'rep').astype(jnp.float32)  36.2 us
    all_to_all x1, starting transfers between devices, per_device(): lax.all_to_all(outgoing, 'shard', split_axis=0, concat_axis=0, tiled=True)  8.57 us
  transfers between devices with their start and end apart: 3, of which 2 were waited for; matrix products, arithmetic and copies ran while one was open for 17% of the time, Pallas kernels for 0%

commit v1 on v0

v1 whole, which is shorter than its diff:
```python
import jax
import jax.numpy as jnp
from jax import lax
from jax.sharding import PartitionSpec as P

learn_rate = 0.5
keep_rate = 0.9


def adagrad_rows(table_rows, accum_rows, grads):
    new_accum = accum_rows + jnp.mean(grads * grads, axis=1)
    new_rows = keep_rate * table_rows - learn_rate * grads / jnp.sqrt(new_accum)[:, None]
    return (new_rows, new_accum)


def rep_sum(local, rep):
    rows = local.shape[0]
    parts = local.astype(jnp.bfloat16).reshape(rep, rows // rep, -1)
    got = lax.all_to_all(parts, "rep", 0, 0, tiled=True)
    mine = jnp.sum(got.astype(jnp.float32), axis=0).astype(jnp.bfloat16)
    spread = jnp.broadcast_to(mine[None], parts.shape)
    full = lax.all_to_all(spread, "rep", 0, 0, tiled=True)
    return full.reshape(rows, -1).astype(jnp.float32)


def per_device(
    features,
    cotangent,
    cross_weight,
    cross_bias,
    emb_table,
    row_accum,
    send_bags,
    slot_counts,
    recv_rows,
    touched_rows,
):
    width = emb_table.shape[1]
    shard_rows = emb_table.shape[0]
    dim = features.shape[1]
    rep = lax.axis_size("rep")
    total_tokens = features.shape[0] * rep * lax.axis_size("shard")
    scale = 1.0 / jnp.sqrt(jnp.float32(total_tokens))
    linear = jnp.dot(features, cross_weight, preferred_element_type=jnp.float32) + cross_bias
    cot_f = cotangent.astype(jnp.float32)
    gated = (cot_f * features.astype(jnp.float32)).astype(jnp.bfloat16)
    ones = jnp.ones((features.shape[0], 8), jnp.bfloat16)
    feats_aug = jnp.concatenate([features, ones], axis=1)
    grads_part = lax.dot_general(
        feats_aug, gated, (((0,), (0,)), ((), ())), preferred_element_type=jnp.float32
    )
    backprop = lax.dot_general(
        gated, cross_weight, (((1,), (1,)), ((), ())), preferred_element_type=jnp.float32
    )
    input_grad = cot_f * linear + backprop + cot_f
    dense_grad = input_grad[:, :width].astype(jnp.bfloat16)
    pooled = input_grad[:, width:].astype(jnp.bfloat16).reshape(-1, width)
    bag_ids = send_bags[0]
    shard_count = bag_ids.shape[0]
    slot_total = bag_ids.shape[1]
    live_mask = jnp.arange(slot_total, dtype=jnp.int32)[None, :] < slot_counts[0][:, None]
    picked = pooled.at[bag_ids.reshape(-1)].get(mode="promise_in_bounds")
    picked = picked.reshape(shard_count, slot_total, width)
    outgoing = jnp.where(live_mask[:, :, None], picked, jnp.zeros((), jnp.bfloat16))
    incoming = lax.all_to_all(outgoing, "shard", split_axis=0, concat_axis=0, tiled=True)
    grads_sum = lax.psum(grads_part, ("rep", "shard"))
    weight_grad = grads_sum[:dim] * scale
    bias_grad = grads_sum[dim] * scale
    incoming_rows = incoming.reshape(-1, width)
    slot_rows = recv_rows[0].reshape(-1)
    touched = touched_rows[0]
    row_range = jnp.arange(shard_rows, dtype=jnp.int32)
    marks = jnp.any(row_range[:, None] == touched[None, :], axis=1)
    select = (row_range[:, None] == slot_rows[None, :]).astype(jnp.bfloat16)
    local_sums = jnp.dot(select, incoming_rows, preferred_element_type=jnp.float32)
    row_grads = rep_sum(local_sums, rep)
    upd_table, upd_accum = adagrad_rows(emb_table, row_accum, row_grads)
    new_table = jnp.where(marks[:, None], upd_table, emb_table)
    new_accum = jnp.where(marks, upd_accum, row_accum)
    return (weight_grad, bias_grad, dense_grad, new_table, new_accum)


def solution(mesh):
    in_specs = (
        P(("rep", "shard"), None),
        P(("rep", "shard"), None),
        P(),
        P(),
        P("shard", None),
        P("shard"),
        P(("rep", "shard"), None, None),
        P(("rep", "shard"), None),
        P(("rep", "shard"), None, None),
        P("shard", None),
    )
    out_specs = (P(), P(), P(("rep", "shard"), None), P("shard", None), P("shard"))
    return jax.shard_map(
        per_device, mesh=mesh, in_specs=in_specs, out_specs=out_specs, check_vma=False
    )
```

time: 360 us -> 252 us (0.70)
  matrix products: 97.1 us -> 31.5 us
  blocking collectives: 79.4 us -> 20.5 us
  waiting for transfers between devices: 76 us -> 113 us
  local copies, waits for them, and re-layouts: 63 us -> 38.8 us
  starting transfers between devices: 8.65 us -> 12.3 us
    psum x1 -> x0, blocking collectives: 79.4 us -> none  [per_device(): weight_sum, bias_sum = lax.psum((weight_part, bias_part), ('rep', 'shard'))]
    dot_general x25 -> x2, matrix products: 93 us -> 27.4 us  [the longest x1 22.9 us: per_device(): jnp.dot(select, incoming_rows, preferred_element_type=jnp.float32)]
    all_to_all x1, waiting for transfers between devices: 0.01 us -> 25.3 us  [per_device(): lax.all_to_all(outgoing, 'shard', split_axis=0, concat_axis=0, tiled=True)]
    gather x16 -> x1, local copies, waits for them, and re-layouts: 50.3 us -> 29.5 us  [per_device(): picked = pooled.at[bag_ids.reshape(-1)].get(mode='promise_in_bounds')]
    all_to_all x0 -> x1, blocking collectives: none -> 20.5 us  [rep_sum(): got = lax.all_to_all(parts, 'rep', 0, 0, tiled=True)]
    psum x2 -> x1, waiting for transfers between devices: 75.9 us -> 87.8 us  [per_device(): grads_sum = lax.psum(grads_part, ('rep', 'shard'))]
    select_n x17 -> x2, other arithmetic: 0.13 us -> 4.43 us  [the longest x1 4.39 us: per_device(): jnp.where(live_mask[:, :, None], picked, jnp.zeros((), jnp.bfloat16))]
  transfers between devices with their start and end apart: 3 -> 3, of which waited for: 2 -> 2; matrix products, arithmetic and copies ran while one was open for 17% -> 16% of each run, Pallas kernels for 0% -> 0%
where the time goes in v1:
time: 252 us; the launch traced here: 251 us
  waiting for transfers between devices  113 us (45%)
  local copies, waits for them, and re-layouts  38.8 us (15%)
  matrix products  31.5 us (12%)
  blocking collectives  20.5 us (8%)
  other arithmetic  20.4 us (8%)
  between operations  14.2 us (6%)
  starting transfers between devices  12.3 us (5%)
    psum x1, waiting for transfers between devices, per_device(): grads_sum = lax.psum(grads_part, ('rep', 'shard'))  87.8 us
    gather x1, local copies, waits for them, and re-layouts, per_device(): picked = pooled.at[bag_ids.reshape(-1)].get(mode='promise_in_bounds')  29.5 us
    all_to_all x1, waiting for transfers between devices, per_device(): lax.all_to_all(outgoing, 'shard', split_axis=0, concat_axis=0, tiled=True)  25.3 us
    dot_general x1, matrix products, per_device(): jnp.dot(select, incoming_rows, preferred_element_type=jnp.float32)  22.9 us
    all_to_all x1, blocking collectives, rep_sum(): got = lax.all_to_all(parts, 'rep', 0, 0, tiled=True)  20.5 us
    all_to_all x1, starting transfers between devices, per_device(): lax.all_to_all(outgoing, 'shard', split_axis=0, concat_axis=0, tiled=True)  8.71 us
    mul x1, other arithmetic, per_device(): weight_grad = grads_sum[:dim] * scale  5.04 us
  transfers between devices with their start and end apart: 3, of which 2 were waited for; matrix products, arithmetic and copies ran while one was open for 16% of the time, Pallas kernels for 0%

profile of v1, /device:TPU:0, one launch (start us, length us, event | category | flops | bytes accessed | tf_op | source)
XLA Modules:
  0.0 250.8 jit_solution(14496884450403018348)
XLA Ops:
  7.2 0.0 copy-start
  7.2 0.0 copy-start.7
  7.2 0.0 copy-start.9
  7.2 0.0 copy-start.11
  7.2 1.5 copy-done
  8.8 2.5 fusion.17
  11.2 0.0 copy-done.7
  11.2 0.0 copy-done.9
  11.3 0.0 copy-done.11
  11.3 1.6 fusion.7
  12.9 0.0 copy-start.2
  12.9 1.0 copy-done.2
  13.8 0.0 copy-start.3
  13.8 0.0 copy-start.6
  13.8 1.0 slice.23
  14.8 2.0 reshape.88
  16.8 0.0 copy-done.3
  16.9 0.0 copy-done.6
  17.0 0.1 iota_compare_fusion.5
  17.0 29.5 %gather_fusion = bf16[8192,128]{1,0:T(8,128)(2,1)} fusion(bf16[3584,128]{1,0:T(8,128)(2,1)S(1)} %reshape.88, s32[8192]{0:T(1024)S(1)} %broadcast_clamp_fusion), kind=kCustom, calls=%fused_computation | custom fusion | bytes 4227072 | tf_op jit(solution)/shard_map/gather | solution.py:62
  46.5 4.4 %broadcast_select_fusion = bf16[32,256,128]{2,1,0:T(8,128)(2,1)} fusion(bf16[32,256,128]{2,1,0:T(8,128)(2,1)} %bitcast.30, pred[32,256]{1,0:T(8,128)(4,1)S(1)} %iota_compare_fusion.5), kind=kLoop, calls=%fused_computation.20 | loop fusion | flops 1048576 | bytes 4202496 | tf_op jit(solution)/shard_map/jit(_where)/select_n | solution.py:64
  50.9 0.0 copy-start.8
  50.9 8.7 %all-to-all-start = ((bf16[32,256,128]{2,1,0:T(8,128)(2,1)}), bf16[32,256,128]{2,1,0:T(8,128)(2,1)}, u32[]{:S(2)}, u32[]{:S(2)}) async-start(bf16[32,256,128]{2,1,0:T(8,128)(2,1)} %broadcast_select_fusion), calls=%async_computation | async-start | bytes 4194304 | tf_op jit(solution)/shard_map/all_to_all | solution.py:65
  59.6 0.0 all-reduce.3.cloned.1.call-start
  59.7 0.0 copy-done.8
  59.7 4.5 %fusion.10 = f32[1032,1024]{1,0:T(8,128)} fusion(bf16[512,1024]{1,0:T(8,128)(2,1)S(1)} %copy-done.8, bf16[512,1024]{1,0:T(8,128)(2,1)} %param.11), kind=kOutput, calls=%fused_computation.21 | convolution fusion | flops 1084227584 | bytes 6324224 | tf_op jit(solution)/shard_map/dot_general | solution.py:49
  64.2 0.0 copy-start.4
  64.2 0.0 all-reduce.3.cloned.1.call-update
  64.2 0.7 copy-done.4
  65.0 25.3 %all-to-all-done = bf16[32,256,128]{2,1,0:T(8,128)(2,1)} async-done(((bf16[32,256,128]{2,1,0:T(8,128)(2,1)}), bf16[32,256,128]{2,1,0:T(8,128)(2,1)}, u32[]{:S(2)}, u32[]{:S(2)}) %all-to-all-start) | async-done | bytes 2097184 | tf_op jit(solution)/shard_map/all_to_all | solution.py:65
  90.3 22.9 %fusion.3 = bf16[4096,128]{1,0:T(8,128)(2,1)S(1)} fusion(bf16[8192,128]{1,0:T(8,128)(2,1)} %bitcast.5, s32[8192]{0:T(1024)S(1)} %bitcast.36), kind=kOutput, calls=%fused_computation.6 | convolution fusion | flops 8624013312 | bytes 3178496 | tf_op jit(solution)/shard_map/dot_general | solution.py:75
  113.2 20.5 %all_to_all.15 = bf16[4,1024,128]{2,1,0:T(8,128)(2,1)S(1)} all-to-all(bf16[4,1024,128]{2,1,0:T(8,128)(2,1)S(1)} %bitcast.31), channel_id=1, replica_groups=mesh['rep'=4,'shard'=32] {'rep'}, dimensions={0} | all-to-all | bytes 2097152 | tf_op jit(solution)/shard_map/all_to_all | solution.py:19
  133.7 0.0 copy-start.10
  133.7 0.3 reduce_sum.21
  134.0 1.1 broadcast_in_dim.22
  135.1 3.5 %all-to-all-start.2 = ((bf16[4,1024,128]{2,1,0:T(8,128)(2,1)}), bf16[4,1024,128]{2,1,0:T(8,128)(2,1)S(1)}, u32[]{:S(2)}, u32[]{:S(2)}) async-start(bf16[4,1024,128]{2,1,0:T(8,128)(2,1)} %broadcast_in_dim.22), calls=%async_computation.2 | async-start | bytes 2097152 | tf_op jit(solution)/shard_map/all_to_all | solution.py:22
  138.6 0.0 copy-done.10
  138.6 4.1 %fusion.2 = pred[4096]{0:T(1024)(128)(4,1)S(1)} fusion(s32[2048]{0:T(1024)S(1)} %bitcast.39), kind=kLoop, calls=%fused_computation.5 | loop fusion | flops 16773120 | bytes 12288 | tf_op jit(solution)/shard_map/reduce_or | solution.py:73
  142.8 1.6 slice.22
  144.3 87.8 %all-reduce.3.cloned.1.call-done = f32[1032,1024]{1,0:T(8,128)} async-done(((f32[1032,1024]{1,0:T(8,128)}), f32[1032,1024]{1,0:T(8,128)}) %all-reduce.3.cloned.1.call-update) | async-done | bytes 4227088 | tf_op jit(solution)/shard_map/psum | solution.py:66
  232.1 1.4 slice_multiply_fusion.1
  233.4 5.0 %slice_multiply_fusion = f32[1024,1024]{1,0:T(8,128)} fusion(f32[1032,1024]{1,0:T(8,128)} %all-reduce.3.cloned.1.call-done), kind=kLoop, calls=%fused_computation.7 | loop fusion | flops 1048576 | bytes 8388608 | tf_op jit(solution)/shard_map/mul | solution.py:67
  238.5 0.0 copy-start.5
  238.5 0.0 all-to-all-done.2
  238.5 0.0 copy-start.1
  238.5 0.6 fusion.4
  239.1 0.1 copy-done.5
  239.2 0.6 fusion.14
  239.8 0.3 copy-done.1
  240.1 3.9 %fusion.9 = f32[4096,128]{1,0:T(8,128)} fusion(f32[4096,128]{1,0:T(8,128)S(1)} %copy-done.1, f32[4,1024,128]{2,1,0:T(8,128)S(1)} %get-tuple-element.6, f32[4096]{0:T(1024)S(1)} %get-tuple-element.8, pred[4096]{0:T(1024)(128)(4,1)S(1)} %fusion.2), kind=kLoop, calls=%fused_computation.19 | loop fusion | flops 2097152 | bytes 6311936 | tf_op jit(solution)/shard_map/jit(_where)/select_n | solution.py:78
  (5 shorter events, 0.1 us)
Async XLA Ops:
  7.2 1.6 copy-start
  7.2 4.1 %copy-start.7 = (bf16[512,1024]{1,0:T(8,128)(2,1)S(1)}, bf16[512,1024]{1,0:T(8,128)(2,1)}, u32[]{:S(2)}) copy-start(bf16[512,1024]{1,0:T(8,128)(2,1)} %param.10) | copy-start | bytes 3145732
  7.2 4.1 %copy-start.9 = (bf16[512,1024]{1,0:T(8,128)(2,1)S(1)}, bf16[512,1024]{1,0:T(8,128)(2,1)}, u32[]{:S(2)}) copy-start(bf16[512,1024]{1,0:T(8,128)(2,1)} %param.11) | copy-start | bytes 3145732
  7.2 4.1 %copy-start.11 = (f32[1024]{0:T(1024)S(1)}, f32[1024]{0:T(1024)}, u32[]{:S(2)}) copy-start(f32[1024]{0:T(1024)} %param.13) | copy-start | bytes 12292
  12.9 1.0 copy-start.2
  13.8 3.0 %copy-start.3 = (s32[1,32,256]{2,1,0:T(8,128)S(1)}, s32[1,32,256]{2,1,0:T(8,128)}, u32[]{:S(2)}) copy-start(s32[1,32,256]{2,1,0:T(8,128)} %param.16) | copy-start | bytes 98308
  13.8 3.1 %copy-start.6 = (s32[1,32]{1,0:T(1,128)S(1)}, s32[1,32]{1,0:T(1,128)}, u32[]{:S(2)}) copy-start(s32[1,32]{1,0:T(1,128)} %param.17) | copy-start | bytes 388
  50.9 8.8 %copy-start.8 = (bf16[512,1024]{1,0:T(8,128)(2,1)S(1)}, bf16[512,1024]{1,0:T(8,128)(2,1)}, u32[]{:S(2)}) copy-start(bf16[512,1024]{1,0:T(8,128)(2,1)} %param.10) | copy-start | bytes 3145732
  50.9 39.4 %all-to-all-start = ((bf16[32,256,128]{2,1,0:T(8,128)(2,1)}), bf16[32,256,128]{2,1,0:T(8,128)(2,1)}, u32[]{:S(2)}, u32[]{:S(2)}) async-start(bf16[32,256,128]{2,1,0:T(8,128)(2,1)} %broadcast_select_fusion), calls=%async_computation | async-start | bytes 4194304 | tf_op jit(solution)/shard_map/all_to_all | solution.py:65
  59.6 172.4 %all-reduce.3.cloned.1.call-start = ((), (), s32[]{:S(2)}) async-start(), calls=%async_computation.3 | async-start | bytes 8454144 | tf_op jit(solution)/shard_map/psum | solution.py:66
  64.2 0.8 copy-start.4
  133.7 4.9 %copy-start.10 = (s32[1,2048]{1,0:T(1,128)S(1)}, s32[1,2048]{1,0:T(1,128)}, u32[]{:S(2)}) copy-start(s32[1,2048]{1,0:T(1,128)} %param.19) | copy-start | bytes 24580
  135.1 103.4 %all-to-all-start.2 = ((bf16[4,1024,128]{2,1,0:T(8,128)(2,1)}), bf16[4,1024,128]{2,1,0:T(8,128)(2,1)S(1)}, u32[]{:S(2)}, u32[]{:S(2)}) async-start(bf16[4,1024,128]{2,1,0:T(8,128)(2,1)} %broadcast_in_dim.22), calls=%async_computation.2 | async-start | bytes 2097152 | tf_op jit(solution)/shard_map/all_to_all | solution.py:22
  238.5 0.7 copy-start.5
  238.5 1.6 copy-start.1
Sparse Core Ops, SparseCore 0:
  65.4 166.6 all-reduce.2

commit v2 on v1

--- a/solution.py
+++ b/solution.py
@@ -23,6 +23,14 @@
     return full.reshape(rows, -1).astype(jnp.float32)
 
 
+def pack_grads(weight_part, bias_part, devices):
+    dim = weight_part.shape[0]
+    block = dim // devices
+    bias_cols = jnp.pad(bias_part.reshape(devices, block, 1), ((0, 0), (0, 0), (0, 127)))
+    packed = jnp.concatenate([weight_part.reshape(devices, block, dim), bias_cols], axis=2)
+    return packed.astype(jnp.bfloat16)
+
+
 def per_device(
     features,
     cotangent,
@@ -35,20 +43,24 @@
     recv_rows,
     touched_rows,
 ):
+    axes = ("rep", "shard")
     width = emb_table.shape[1]
     shard_rows = emb_table.shape[0]
     dim = features.shape[1]
     rep = lax.axis_size("rep")
-    total_tokens = features.shape[0] * rep * lax.axis_size("shard")
+    devices = lax.axis_size(axes)
+    total_tokens = features.shape[0] * devices
     scale = 1.0 / jnp.sqrt(jnp.float32(total_tokens))
     linear = jnp.dot(features, cross_weight, preferred_element_type=jnp.float32) + cross_bias
     cot_f = cotangent.astype(jnp.float32)
     gated = (cot_f * features.astype(jnp.float32)).astype(jnp.bfloat16)
-    ones = jnp.ones((features.shape[0], 8), jnp.bfloat16)
-    feats_aug = jnp.concatenate([features, ones], axis=1)
-    grads_part = lax.dot_general(
-        feats_aug, gated, (((0,), (0,)), ((), ())), preferred_element_type=jnp.float32
+    weight_part = lax.dot_general(
+        features, gated, (((0,), (0,)), ((), ())), preferred_element_type=jnp.float32
     )
+    bias_part = jnp.sum(gated.astype(jnp.float32), axis=0)
+    packed = pack_grads(weight_part, bias_part, devices)
+    got_w = lax.all_to_all(packed, axes, 0, 0, tiled=True)
+
     backprop = lax.dot_general(
         gated, cross_weight, (((1,), (1,)), ((), ())), preferred_element_type=jnp.float32
     )
@@ -62,10 +74,17 @@
     picked = pooled.at[bag_ids.reshape(-1)].get(mode="promise_in_bounds")
     picked = picked.reshape(shard_count, slot_total, width)
     outgoing = jnp.where(live_mask[:, :, None], picked, jnp.zeros((), jnp.bfloat16))
+
+    got_w, outgoing = lax.optimization_barrier((got_w, outgoing))
     incoming = lax.all_to_all(outgoing, "shard", split_axis=0, concat_axis=0, tiled=True)
-    grads_sum = lax.psum(grads_part, ("rep", "shard"))
-    weight_grad = grads_sum[:dim] * scale
-    bias_grad = grads_sum[dim] * scale
+    ones = jnp.ones((devices,), jnp.bfloat16)
+    mine_w = lax.dot_general(
+        ones, got_w, (((0,), (0,)), ((), ())), preferred_element_type=jnp.float32
+    ).astype(jnp.bfloat16)
+    spread = jnp.broadcast_to(mine_w[None], got_w.shape)
+    spread, incoming = lax.optimization_barrier((spread, incoming))
+    full_w = lax.all_to_all(spread, axes, 0, 0, tiled=True)
+
     incoming_rows = incoming.reshape(-1, width)
     slot_rows = recv_rows[0].reshape(-1)
     touched = touched_rows[0]
@@ -73,7 +92,12 @@
     marks = jnp.any(row_range[:, None] == touched[None, :], axis=1)
     select = (row_range[:, None] == slot_rows[None, :]).astype(jnp.bfloat16)
     local_sums = jnp.dot(select, incoming_rows, preferred_element_type=jnp.float32)
+    full_w, local_sums = lax.optimization_barrier((full_w, local_sums))
     row_grads = rep_sum(local_sums, rep)
+
+    full_w = full_w.astype(jnp.float32)
+    weight_grad = full_w[:, :, :dim].reshape(dim, dim) * scale
+    bias_grad = full_w[:, :, dim].reshape(dim) * scale
     upd_table, upd_accum = adagrad_rows(emb_table, row_accum, row_grads)
     new_table = jnp.where(marks[:, None], upd_table, emb_table)
     new_accum = jnp.where(marks, upd_accum, row_accum)

time: 252 us -> 186 us (0.74)
  waiting for transfers between devices: 113 us -> 36.9 us
  starting transfers between devices: 12.3 us -> 29.1 us
  between operations: 14.2 us -> 0.88 us
  other arithmetic: 20.4 us -> 26.5 us
  local copies, waits for them, and re-layouts: 38.8 us -> 41.7 us
    psum x1 -> x0, waiting for transfers between devices: 87.8 us -> none  [per_device(): grads_sum = lax.psum(grads_part, ('rep', 'shard'))]
    all_to_all x0 -> x2, starting transfers between devices: none -> 18.2 us  [the longest x1 11.6 us: per_device(): got_w = lax.all_to_all(packed, axes, 0, 0, tiled=True)]
    all_to_all x0 -> x2, waiting for transfers between devices: none -> 9.02 us  [the longest x1 9.02 us: per_device(): full_w = lax.all_to_all(spread, axes, 0, 0, tiled=True)]
    concatenate x0 -> x1, other arithmetic: none -> 3.21 us  [pack_grads(): jnp.concatenate([weight_part.reshape(devices, block, dim), bias_cols], ax...]
    all_to_all x1, waiting for transfers between devices: 25.3 us -> 27.9 us  [per_device(): lax.all_to_all(outgoing, 'shard', split_axis=0, concat_axis=0, tiled=True)]
  transfers between devices with their start and end apart: 3 -> 4, of which waited for: 2 -> 2; matrix products, arithmetic and copies ran while one was open for 16% -> 43% of each run, Pallas kernels for 0% -> 0%
where the time goes in v2:
time: 186 us; the launch traced here: 185 us
  local copies, waits for them, and re-layouts  41.7 us (22%)
  waiting for transfers between devices  36.9 us (20%)
  matrix products  31.2 us (17%)
  starting transfers between devices  29.1 us (16%)
  other arithmetic  26.5 us (14%)
  blocking collectives  18.3 us (10%)
    gather x1, local copies, waits for them, and re-layouts, per_device(): picked = pooled.at[bag_ids.reshape(-1)].get(mode='promise_in_bounds')  29.5 us
    all_to_all x1, waiting for transfers between devices, per_device(): lax.all_to_all(outgoing, 'shard', split_axis=0, concat_axis=0, tiled=True)  27.9 us
    dot_general x1, matrix products, per_device(): jnp.dot(select, incoming_rows, preferred_element_type=jnp.float32)  23.6 us
    all_to_all x1, blocking collectives, rep_sum(): got = lax.all_to_all(parts, 'rep', 0, 0, tiled=True)  18.3 us
    all_to_all x1, starting transfers between devices, per_device(): got_w = lax.all_to_all(packed, axes, 0, 0, tiled=True)  11.6 us
    all_to_all x1, waiting for transfers between devices, per_device(): full_w = lax.all_to_all(spread, axes, 0, 0, tiled=True)  9.02 us
    all_to_all x1, starting transfers between devices, per_device(): lax.all_to_all(outgoing, 'shard', split_axis=0, concat_axis=0, tiled=True)  7.12 us
    all_to_all x1, starting transfers between devices, per_device(): full_w = lax.all_to_all(spread, axes, 0, 0, tiled=True)  6.58 us
  transfers between devices with their start and end apart: 4, of which 2 were waited for; matrix products, arithmetic and copies ran while one was open for 43% of the time, Pallas kernels for 0%

profile of v2, /device:TPU:0, one launch (start us, length us, event | category | flops | bytes accessed | tf_op | source)
XLA Modules:
  0.0 184.5 jit_solution(1939825095499399592)
XLA Ops:
  0.6 0.0 copy-start
  0.6 0.0 copy-start.3
  0.7 0.0 copy-start.4
  0.7 2.1 %fusion.16 = bf16[1024]{0:T(1024)(128)(2,1)S(1)} fusion(bf16[512,1024]{1,0:T(8,128)(2,1)} %param.10, bf16[512,1024]{1,0:T(8,128)(2,1)} %param.11), kind=kLoop, calls=%fused_computation.29 | loop fusion | flops 2620416 | bytes 2099200 | tf_op jit(solution)/shard_map/reduce_sum | solution.py:60
  2.7 0.0 copy-done.3
  2.7 0.2 copy-done.4
  3.0 2.6 %convert_bitcast_fusion = bf16[128,8,1024]{2,1,0:T(8,128)(2,1)} fusion(bf16[512,1024]{1,0:T(8,128)(2,1)S(1)} %copy-done.3, bf16[512,1024]{1,0:T(8,128)(2,1)S(1)} %copy-done.4), kind=kOutput, calls=%fused_computation.25 | convolution fusion | flops 1076887552 | bytes 4194304 | tf_op jit(solution)/shard_map/dot_general | solution.py:57
  5.6 0.4 reshape.116
  6.0 3.2 %fusion.5 = bf16[128,8,1152]{2,1,0:T(8,128)(2,1)} fusion(bf16[128,8,1]{2,1,0:T(8,128)(2,1)S(1)} %reshape.116, bf16[128,8,1024]{2,1,0:T(8,128)(2,1)} %convert_bitcast_fusion), kind=kLoop, calls=%fused_computation.15 | loop fusion | flops 7077888 | bytes 4458496 | tf_op jit(solution)/shard_map/concatenate | solution.py:30
  9.2 11.6 %all-to-all-start = ((bf16[128,8,1152]{2,1,0:T(8,128)(2,1)}), bf16[128,8,1152]{2,1,0:T(8,128)(2,1)}, u32[]{:S(2)}, u32[]{:S(2)}) async-start(bf16[128,8,1152]{2,1,0:T(8,128)(2,1)} %fusion.5), calls=%async_computation | async-start | bytes 4718592 | tf_op jit(solution)/shard_map/all_to_all | solution.py:62
  20.9 0.0 copy-done
  20.9 0.0 copy-start.5
  20.9 0.0 copy-start.12
  20.9 1.3 fusion.22
  22.2 0.0 copy-done.5
  22.2 0.0 copy-done.12
  22.2 1.5 fusion.11
  23.7 0.0 copy-start.6
  23.7 1.0 copy-done.6
  24.7 0.0 copy-start.7
  24.7 1.0 slice.20
  25.7 2.0 %reshape.102 = bf16[3584,128]{1,0:T(8,128)(2,1)S(1)} reshape(bf16[512,896]{1,0:T(8,128)(2,1)} %slice.20) | data formatting | bytes 1835008 | tf_op jit(solution)/shard_map/reshape | solution.py:69
  27.7 0.0 copy-done.7
  27.9 0.0 copy-start.10
  27.9 29.5 %gather_fusion = bf16[8192,128]{1,0:T(8,128)(2,1)} fusion(bf16[3584,128]{1,0:T(8,128)(2,1)S(1)} %reshape.102, s32[8192]{0:T(1024)S(1)} %broadcast_clamp_fusion), kind=kCustom, calls=%fused_computation | custom fusion | bytes 4227072 | tf_op jit(solution)/shard_map/gather | solution.py:74
  57.4 0.0 copy-done.10
  57.4 0.1 iota_compare_fusion.4
  57.4 4.4 %broadcast_select_fusion = bf16[32,256,128]{2,1,0:T(8,128)(2,1)} fusion(bf16[32,256,128]{2,1,0:T(8,128)(2,1)} %bitcast.39, pred[32,256]{1,0:T(8,128)(4,1)S(1)} %iota_compare_fusion.4), kind=kLoop, calls=%fused_computation.26 | loop fusion | flops 1048576 | bytes 4202496 | tf_op jit(solution)/shard_map/jit(_where)/select_n | solution.py:76
  61.8 0.0 all-to-all-done
  61.8 7.1 %all-to-all-start.1 = ((bf16[32,256,128]{2,1,0:T(8,128)(2,1)}), bf16[32,256,128]{2,1,0:T(8,128)(2,1)}, u32[]{:S(2)}, u32[]{:S(2)}) async-start(bf16[32,256,128]{2,1,0:T(8,128)(2,1)} %broadcast_select_fusion), calls=%async_computation.1 | async-start | bytes 4194304 | tf_op jit(solution)/shard_map/all_to_all | solution.py:79
  69.0 2.2 %fusion.6 = bf16[1,8,1152]{2,0,1:T(2,128)(2,1)S(1)} fusion(bf16[128,8,1152]{2,1,0:T(8,128)(2,1)} %all-to-all-done), kind=kOutput, calls=%fused_computation.16 | convolution fusion | flops 2359296 | bytes 2377728 | tf_op jit(solution)/shard_map/dot_general | solution.py:81
  71.1 27.9 %all-to-all-done.1 = bf16[32,256,128]{2,1,0:T(8,128)(2,1)} async-done(((bf16[32,256,128]{2,1,0:T(8,128)(2,1)}), bf16[32,256,128]{2,1,0:T(8,128)(2,1)}, u32[]{:S(2)}, u32[]{:S(2)}) %all-to-all-start.1) | async-done | bytes 2097184 | tf_op jit(solution)/shard_map/all_to_all | solution.py:79
  99.0 1.6 broadcast_in_dim.26
  100.6 0.0 copy-start.8
  100.6 6.6 %all-to-all-start.2 = ((bf16[128,8,1152]{2,1,0:T(8,128)(2,1)}), bf16[128,8,1152]{2,1,0:T(8,128)(2,1)}, u32[]{:S(2)}, u32[]{:S(2)}) async-start(bf16[128,8,1152]{2,1,0:T(8,128)(2,1)} %broadcast_in_dim.26), calls=%async_computation.2 | async-start | bytes 4718592 | tf_op jit(solution)/shard_map/all_to_all | solution.py:86
  107.2 0.0 copy-done.8
  107.2 23.6 %fusion = bf16[4096,128]{1,0:T(8,128)(2,1)} fusion(bf16[8192,128]{1,0:T(8,128)(2,1)} %bitcast.6, s32[8192]{0:T(1024)S(1)} %bitcast.46), kind=kOutput, calls=%fused_computation.2 | convolution fusion | flops 8623489024 | bytes 3178496 | tf_op jit(solution)/shard_map/dot_general | solution.py:94
  130.8 9.0 %all-to-all-done.2 = bf16[128,8,1152]{2,1,0:T(8,128)(2,1)} async-done(((bf16[128,8,1152]{2,1,0:T(8,128)(2,1)}), bf16[128,8,1152]{2,1,0:T(8,128)(2,1)}, u32[]{:S(2)}, u32[]{:S(2)}) %all-to-all-start.2) | async-done | bytes 2359328 | tf_op jit(solution)/shard_map/all_to_all | solution.py:86
  139.8 18.3 %all_to_all.25 = bf16[4,1024,128]{2,1,0:T(8,128)(2,1)S(1)} all-to-all(bf16[4,1024,128]{2,1,0:T(8,128)(2,1)} %bitcast.40), channel_id=1, replica_groups=mesh['rep'=4,'shard'=32] {'rep'}, dimensions={0} | all-to-all | bytes 2097152 | tf_op jit(solution)/shard_map/all_to_all | solution.py:19
  158.1 0.0 copy-start.11
  158.1 0.3 reduce_sum.31
  158.4 1.1 broadcast_in_dim.48
  159.5 3.7 %all-to-all-start.4 = ((bf16[4,1024,128]{2,1,0:T(8,128)(2,1)}), bf16[4,1024,128]{2,1,0:T(8,128)(2,1)S(1)}, u32[]{:S(2)}, u32[]{:S(2)}) async-start(bf16[4,1024,128]{2,1,0:T(8,128)(2,1)} %broadcast_in_dim.48), calls=%async_computation.4 | async-start | bytes 2097152 | tf_op jit(solution)/shard_map/all_to_all | solution.py:22
  163.2 0.0 copy-done.11
  163.3 4.1 %fusion.2 = pred[4096]{0:T(1024)(128)(4,1)S(1)} fusion(s32[2048]{0:T(1024)S(1)} %bitcast.48), kind=kLoop, calls=%fused_computation.5 | loop fusion | flops 16773120 | bytes 12288 | tf_op jit(solution)/shard_map/reduce_or | solution.py:92
  167.4 1.6 slice.23
  169.0 2.0 %convert_element_type.39 = f32[128,8,1152]{2,1,0:T(8,128)S(1)} convert(bf16[128,8,1152]{2,1,0:T(8,128)(2,1)} %all-to-all-done.2) | non-fusion elementwise | flops 1179648 | bytes 7077888 | tf_op jit(solution)/shard_map/convert_element_type | solution.py:98
  170.9 0.0 copy-start.1
  170.9 2.1 %copy-done.1 = f32[128,8,1152]{2,1,0:T(8,128)} copy-done((f32[128,8,1152]{2,1,0:T(8,128)}, f32[128,8,1152]{2,1,0:T(8,128)S(1)}, u32[]{:S(2)}) %copy-start.1) | copy-done | bytes 4718616
  173.1 0.2 fusion.14
  173.3 0.7 mul.50
  174.0 5.0 %fusion.4 = f32[1024,1024]{1,0:T(8,128)} fusion(f32[128,8,1152]{2,1,0:T(8,128)} %copy-done.1), kind=kLoop, calls=%fused_computation.9 | loop fusion | flops 1048576 | bytes 8388608 | tf_op jit(solution)/shard_map/mul | solution.py:99
  179.0 0.0 copy-start.9
  179.0 0.0 all-to-all-done.4
  179.0 0.0 copy-start.2
  179.0 0.6 fusion.8
  179.7 0.1 copy-done.9
  179.7 0.6 fusion.18
  180.3 0.3 copy-done.2
  180.6 3.9 %fusion.13 = f32[4096,128]{1,0:T(8,128)} fusion(f32[4096,128]{1,0:T(8,128)S(1)} %copy-done.2, f32[4,1024,128]{2,1,0:T(8,128)S(1)} %get-tuple-element.18, f32[4096]{0:T(1024)S(1)} %get-tuple-element.20, pred[4096]{0:T(1024)(128)(4,1)S(1)} %fusion.2), kind=kLoop, calls=%fused_computation.24 | loop fusion | flops 2097152 | bytes 6311936 | tf_op jit(solution)/shard_map/jit(_where)/select_n | solution.py:102
  (6 shorter events, 0.1 us)
Async XLA Ops:
  0.6 20.3 %copy-start = (bf16[1024,1024]{1,0:T(8,128)(2,1)S(1)}, bf16[1024,1024]{1,0:T(8,128)(2,1)}, u32[]{:S(2)}) copy-start(bf16[1024,1024]{1,0:T(8,128)(2,1)} %param.12) | copy-start | bytes 6291460
  0.6 2.1 %copy-start.3 = (bf16[512,1024]{1,0:T(8,128)(2,1)S(1)}, bf16[512,1024]{1,0:T(8,128)(2,1)}, u32[]{:S(2)}) copy-start(bf16[512,1024]{1,0:T(8,128)(2,1)} %param.10) | copy-start | bytes 3145732
  0.7 2.3 %copy-start.4 = (bf16[512,1024]{1,0:T(8,128)(2,1)S(1)}, bf16[512,1024]{1,0:T(8,128)(2,1)}, u32[]{:S(2)}) copy-start(bf16[512,1024]{1,0:T(8,128)(2,1)} %param.11) | copy-start | bytes 3145732
  9.2 52.6 %all-to-all-start = ((bf16[128,8,1152]{2,1,0:T(8,128)(2,1)}), bf16[128,8,1152]{2,1,0:T(8,128)(2,1)}, u32[]{:S(2)}, u32[]{:S(2)}) async-start(bf16[128,8,1152]{2,1,0:T(8,128)(2,1)} %fusion.5), calls=%async_computation | async-start | bytes 4718592 | tf_op jit(solution)/shard_map/all_to_all | solution.py:62
  20.9 1.3 copy-start.5
  20.9 1.3 copy-start.12
  23.7 1.0 copy-start.6
  24.7 3.0 %copy-start.7 = (s32[1,32,256]{2,1,0:T(8,128)S(1)}, s32[1,32,256]{2,1,0:T(8,128)}, u32[]{:S(2)}) copy-start(s32[1,32,256]{2,1,0:T(8,128)} %param.16) | copy-start | bytes 98308
  27.9 29.5 %copy-start.10 = (s32[1,32]{1,0:T(1,128)S(1)}, s32[1,32]{1,0:T(1,128)}, u32[]{:S(2)}) copy-start(s32[1,32]{1,0:T(1,128)} %param.17) | copy-start | bytes 388
  61.8 37.2 %all-to-all-start.1 = ((bf16[32,256,128]{2,1,0:T(8,128)(2,1)}), bf16[32,256,128]{2,1,0:T(8,128)(2,1)}, u32[]{:S(2)}, u32[]{:S(2)}) async-start(bf16[32,256,128]{2,1,0:T(8,128)(2,1)} %broadcast_select_fusion), calls=%async_computation.1 | async-start | bytes 4194304 | tf_op jit(solution)/shard_map/all_to_all | solution.py:79
  100.6 6.6 %copy-start.8 = (s32[1,32,256]{2,1,0:T(8,128)S(1)}, s32[1,32,256]{2,1,0:T(8,128)}, u32[]{:S(2)}) copy-start(s32[1,32,256]{2,1,0:T(8,128)} %param.18) | copy-start | bytes 98308
  100.6 39.3 %all-to-all-start.2 = ((bf16[128,8,1152]{2,1,0:T(8,128)(2,1)}), bf16[128,8,1152]{2,1,0:T(8,128)(2,1)}, u32[]{:S(2)}, u32[]{:S(2)}) async-start(bf16[128,8,1152]{2,1,0:T(8,128)(2,1)} %broadcast_in_dim.26), calls=%async_computation.2 | async-start | bytes 4718592 | tf_op jit(solution)/shard_map/all_to_all | solution.py:86
  158.1 5.1 %copy-start.11 = (s32[1,2048]{1,0:T(1,128)S(1)}, s32[1,2048]{1,0:T(1,128)}, u32[]{:S(2)}) copy-start(s32[1,2048]{1,0:T(1,128)} %param.19) | copy-start | bytes 24580
  159.5 19.5 %all-to-all-start.4 = ((bf16[4,1024,128]{2,1,0:T(8,128)(2,1)}), bf16[4,1024,128]{2,1,0:T(8,128)(2,1)S(1)}, u32[]{:S(2)}, u32[]{:S(2)}) async-start(bf16[4,1024,128]{2,1,0:T(8,128)(2,1)} %broadcast_in_dim.48), calls=%async_computation.4 | async-start | bytes 2097152 | tf_op jit(solution)/shard_map/all_to_all | solution.py:22
  170.9 2.1 %copy-start.1 = (f32[128,8,1152]{2,1,0:T(8,128)}, f32[128,8,1152]{2,1,0:T(8,128)S(1)}, u32[]{:S(2)}) copy-start(f32[128,8,1152]{2,1,0:T(8,128)S(1)} %convert_element_type.39) | copy-start | bytes 14155780
  179.0 0.7 copy-start.9
  179.0 1.6 copy-start.2

commit v3 on v2

--- a/solution.py
+++ b/solution.py
@@ -71,9 +71,11 @@
     shard_count = bag_ids.shape[0]
     slot_total = bag_ids.shape[1]
     live_mask = jnp.arange(slot_total, dtype=jnp.int32)[None, :] < slot_counts[0][:, None]
-    picked = pooled.at[bag_ids.reshape(-1)].get(mode="promise_in_bounds")
-    picked = picked.reshape(shard_count, slot_total, width)
-    outgoing = jnp.where(live_mask[:, :, None], picked, jnp.zeros((), jnp.bfloat16))
+    flat_bags = jnp.where(live_mask, bag_ids, -1).reshape(-1)
+    bag_range = jnp.arange(pooled.shape[0], dtype=jnp.int32)
+    pick = (flat_bags[:, None] == bag_range[None, :]).astype(jnp.bfloat16)
+    picked = jnp.dot(pick, pooled, preferred_element_type=jnp.float32).astype(jnp.bfloat16)
+    outgoing = picked.reshape(shard_count, slot_total, width)
 
     got_w, outgoing = lax.optimization_barrier((got_w, outgoing))
     incoming = lax.all_to_all(outgoing, "shard", split_axis=0, concat_axis=0, tiled=True)
@@ -88,12 +90,16 @@
     incoming_rows = incoming.reshape(-1, width)
     slot_rows = recv_rows[0].reshape(-1)
     touched = touched_rows[0]
-    row_range = jnp.arange(shard_rows, dtype=jnp.int32)
-    marks = jnp.any(row_range[:, None] == touched[None, :], axis=1)
-    select = (row_range[:, None] == slot_rows[None, :]).astype(jnp.bfloat16)
+    select = (touched[:, None] == slot_rows[None, :]).astype(jnp.bfloat16)
     local_sums = jnp.dot(select, incoming_rows, preferred_element_type=jnp.float32)
     full_w, local_sums = lax.optimization_barrier((full_w, local_sums))
-    row_grads = rep_sum(local_sums, rep)
+    touched_grads = rep_sum(local_sums, rep).astype(jnp.bfloat16)
+    row_range = jnp.arange(shard_rows, dtype=jnp.int32)
+    place = (row_range[:, None] == touched[None, :]).astype(jnp.bfloat16)
+    with_marks = jnp.concatenate([touched_grads, jnp.ones_like(touched_grads)], axis=1)
+    spread_rows = jnp.dot(place, with_marks, preferred_element_type=jnp.float32)
+    row_grads = spread_rows[:, :width]
+    marks = spread_rows[:, width] > 0.5
 
     full_w = full_w.astype(jnp.float32)
     weight_grad = full_w[:, :, :dim].reshape(dim, dim) * scale

time: 186 us -> 170 us (0.914)
  local copies, waits for them, and re-layouts: 41.7 us -> 17 us
  matrix products: 31.2 us -> 50 us
  waiting for transfers between devices: 36.9 us -> 55.6 us
  blocking collectives: 18.3 us -> 0 us
  other arithmetic: 26.5 us -> 15.3 us
    dot_general x0 -> x2, matrix products: none -> 30.1 us  [the longest x1 23.1 us: per_device(): jnp.dot(pick, pooled, preferred_element_type=jnp.float32)]
    gather x1 -> x0, local copies, waits for them, and re-layouts: 29.5 us -> none  [per_device(): picked = pooled.at[bag_ids.reshape(-1)].get(mode='promise_in_bounds')]
    all_to_all x1 -> x0, blocking collectives: 18.3 us -> none  [rep_sum(): got = lax.all_to_all(parts, 'rep', 0, 0, tiled=True)]
    all_to_all x1, waiting for transfers between devices: 9.02 us -> 20.5 us  [per_device(): full_w = lax.all_to_all(spread, axes, 0, 0, tiled=True)]
    dot_general x1, matrix products: 23.6 us -> 12.3 us  [per_device(): jnp.dot(select, incoming_rows, preferred_element_type=jnp.float32)]
    unnamed x28 -> x30, local copies, waits for them, and re-layouts: 3.82 us -> 9.94 us
    select_n x2 -> x1, other arithmetic: 4.43 us -> 0.01 us  [per_device(): flat_bags = jnp.where(live_mask, bag_ids, -1).reshape(-1)]
    reduce_or x1 -> x0, other arithmetic: 4.13 us -> none  [per_device(): marks = jnp.any(row_range[:, None] == touched[None, :], axis=1)]
  transfers between devices with their start and end apart: 4 -> 5, of which waited for: 2 -> 4; matrix products, arithmetic and copies ran while one was open for 43% -> 32% of each run, Pallas kernels for 0% -> 0%
where the time goes in v3:
time: 170 us
  waiting for transfers between devices  55.6 us (33%)
  matrix products  50 us (29%)
  starting transfers between devices  30.9 us (18%)
  local copies, waits for them, and re-layouts  17 us (10%)
  other arithmetic  15.3 us (9%)
    all_to_all x1, waiting for transfers between devices, per_device(): lax.all_to_all(outgoing, 'shard', split_axis=0, concat_axis=0, tiled=True)  27.9 us
    dot_general x1, matrix products, per_device(): jnp.dot(pick, pooled, preferred_element_type=jnp.float32)  23.1 us
    all_to_all x1, waiting for transfers between devices, per_device(): full_w = lax.all_to_all(spread, axes, 0, 0, tiled=True)  20.5 us
    dot_general x1, matrix products, per_device(): jnp.dot(select, incoming_rows, preferred_element_type=jnp.float32)  12.3 us
    all_to_all x1, starting transfers between devices, per_device(): got_w = lax.all_to_all(packed, axes, 0, 0, tiled=True)  11.8 us
    unnamed x30, local copies, waits for them, and re-layouts  9.94 us
    dot_general x1, matrix products, per_device(): spread_rows = jnp.dot(place, with_marks, preferred_element_type=jnp.float32)  6.96 us
    all_to_all x1, starting transfers between devices, per_device(): full_w = lax.all_to_all(spread, axes, 0, 0, tiled=True)  6.07 us
  transfers between devices with their start and end apart: 5, of which 4 were waited for; matrix products, arithmetic and copies ran while one was open for 32% of the time, Pallas kernels for 0%

profile of v3, /device:TPU:0, one launch (start us, length us, event | category | flops | bytes accessed | tf_op | source)
XLA Modules:
  0.0 169.7 jit_solution(716418163227517376)
XLA Ops:
  0.6 0.0 copy-start
  0.6 0.0 copy-start.3
  0.7 0.0 copy-start.4
  0.7 2.1 %fusion.20 = bf16[1024]{0:T(1024)(128)(2,1)S(1)} fusion(bf16[512,1024]{1,0:T(8,128)(2,1)} %param.10, bf16[512,1024]{1,0:T(8,128)(2,1)} %param.11), kind=kLoop, calls=%fused_computation.30 | loop fusion | flops 2620416 | bytes 2099200 | tf_op jit(solution)/shard_map/reduce_sum | solution.py:60
  2.7 0.0 copy-done.3
  2.7 0.2 copy-done.4
  3.0 2.6 %convert_bitcast_fusion = bf16[128,8,1024]{2,1,0:T(8,128)(2,1)} fusion(bf16[512,1024]{1,0:T(8,128)(2,1)S(1)} %copy-done.3, bf16[512,1024]{1,0:T(8,128)(2,1)S(1)} %copy-done.4), kind=kOutput, calls=%fused_computation.26 | convolution fusion | flops 1076887552 | bytes 4194304 | tf_op jit(solution)/shard_map/dot_general | solution.py:57
  5.6 0.4 reshape.75
  6.0 3.2 %fusion.11 = bf16[128,8,1152]{2,1,0:T(8,128)(2,1)} fusion(bf16[128,8,1]{2,1,0:T(8,128)(2,1)S(1)} %reshape.75, bf16[128,8,1024]{2,1,0:T(8,128)(2,1)} %convert_bitcast_fusion), kind=kLoop, calls=%fused_computation.18 | loop fusion | flops 7077888 | bytes 4458496 | tf_op jit(solution)/shard_map/concatenate | solution.py:30
  9.2 11.8 %all-to-all-start = ((bf16[128,8,1152]{2,1,0:T(8,128)(2,1)}), bf16[128,8,1152]{2,1,0:T(8,128)(2,1)}, u32[]{:S(2)}, u32[]{:S(2)}) async-start(bf16[128,8,1152]{2,1,0:T(8,128)(2,1)} %fusion.11), calls=%async_computation | async-start | bytes 4718592 | tf_op jit(solution)/shard_map/all_to_all | solution.py:62
  21.1 0.0 copy-done
  21.1 0.0 copy-start.5
  21.1 0.0 copy-start.12
  21.1 1.3 fusion.27
  22.4 0.0 copy-done.5
  22.4 0.0 copy-done.12
  22.4 1.5 fusion.16
  23.9 0.0 copy-start.6
  23.9 1.0 copy-done.6
  24.9 0.0 copy-start.10
  24.9 0.0 copy-start.7
  24.9 0.1 slice.26
  25.0 1.8 %reshape.68 = bf16[3584,128]{1,0:T(8,128)(2,1)} reshape(bf16[512,896]{1,0:T(8,128)(2,1)S(1)} %slice.26) | data formatting | bytes 1835008 | tf_op jit(solution)/shard_map/reshape | solution.py:69
  26.8 0.0 copy-done.10
  26.8 0.1 iota_compare_fusion.7
  26.9 0.0 copy-done.7
  26.9 23.1 %fusion.8 = bf16[8192,128]{1,0:T(8,128)(2,1)} fusion(bf16[3584,128]{1,0:T(8,128)(2,1)} %reshape.68, s32[8192]{0:T(1024)S(1)} %broadcast_select_fusion), kind=kOutput, calls=%fused_computation.10 | convolution fusion | flops 7546601472 | bytes 3047424 | tf_op jit(solution)/shard_map/dot_general | solution.py:77
  50.1 3.7 %all-to-all-done = bf16[128,8,1152]{2,1,0:T(8,128)(2,1)} async-done(((bf16[128,8,1152]{2,1,0:T(8,128)(2,1)}), bf16[128,8,1152]{2,1,0:T(8,128)(2,1)}, u32[]{:S(2)}, u32[]{:S(2)}) %all-to-all-start) | async-done | bytes 2359328 | tf_op jit(solution)/shard_map/all_to_all | solution.py:62
  53.7 4.8 %all-to-all-start.1 = ((bf16[32,256,128]{2,1,0:T(8,128)(2,1)}), bf16[32,256,128]{2,1,0:T(8,128)(2,1)}, u32[]{:S(2)}, u32[]{:S(2)}) async-start(bf16[32,256,128]{2,1,0:T(8,128)(2,1)} %bitcast.25), calls=%async_computation.1 | async-start | bytes 4194304 | tf_op jit(solution)/shard_map/all_to_all | solution.py:81
  58.5 2.2 %fusion.12 = bf16[1,8,1152]{2,0,1:T(2,128)(2,1)S(1)} fusion(bf16[128,8,1152]{2,1,0:T(8,128)(2,1)} %all-to-all-done), kind=kOutput, calls=%fused_computation.19 | convolution fusion | flops 2359296 | bytes 2377728 | tf_op jit(solution)/shard_map/dot_general | solution.py:83
  60.7 27.9 %all-to-all-done.1 = bf16[32,256,128]{2,1,0:T(8,128)(2,1)} async-done(((bf16[32,256,128]{2,1,0:T(8,128)(2,1)}), bf16[32,256,128]{2,1,0:T(8,128)(2,1)}, u32[]{:S(2)}, u32[]{:S(2)}) %all-to-all-start.1) | async-done | bytes 2097184 | tf_op jit(solution)/shard_map/all_to_all | solution.py:81
  88.6 1.6 broadcast_in_dim.19
  90.2 0.0 copy-start.8
  90.2 0.0 copy-start.11
  90.2 6.1 %all-to-all-start.2 = ((bf16[128,8,1152]{2,1,0:T(8,128)(2,1)}), bf16[128,8,1152]{2,1,0:T(8,128)(2,1)}, u32[]{:S(2)}, u32[]{:S(2)}) async-start(bf16[128,8,1152]{2,1,0:T(8,128)(2,1)} %broadcast_in_dim.19), calls=%async_computation.2 | async-start | bytes 4718592 | tf_op jit(solution)/shard_map/all_to_all | solution.py:88
  96.3 0.0 copy-done.8
  96.3 0.0 copy-done.11
  96.3 12.3 %fusion.1 = bf16[2048,128]{1,0:T(8,128)(2,1)} fusion(bf16[8192,128]{1,0:T(8,128)(2,1)} %bitcast.6, s32[8192]{0:T(1024)S(1)} %bitcast.31, s32[2048]{0:T(1024)S(1)} %bitcast.33), kind=kOutput, calls=%fused_computation.2 | convolution fusion | flops 4311744512 | bytes 2662400 | tf_op jit(solution)/shard_map/dot_general | solution.py:94
  108.7 20.5 %all-to-all-done.2 = bf16[128,8,1152]{2,1,0:T(8,128)(2,1)} async-done(((bf16[128,8,1152]{2,1,0:T(8,128)(2,1)}), bf16[128,8,1152]{2,1,0:T(8,128)(2,1)}, u32[]{:S(2)}, u32[]{:S(2)}) %all-to-all-start.2) | async-done | bytes 2359328 | tf_op jit(solution)/shard_map/all_to_all | solution.py:88
  129.1 3.5 %all-to-all-start.3 = ((bf16[4,512,128]{2,1,0:T(8,128)(2,1)}), bf16[4,512,128]{2,1,0:T(8,128)(2,1)S(1)}, u32[]{:S(2)}, u32[]{:S(2)}) async-start(bf16[4,512,128]{2,1,0:T(8,128)(2,1)} %bitcast.8), calls=%async_computation.3 | async-start | bytes 1048576 | tf_op jit(solution)/shard_map/all_to_all | solution.py:19
  132.6 1.6 slice.29
  134.2 2.9 %copy.24 = f32[4096,128]{0,1:T(8,128)} copy(f32[4096,128]{1,0:T(8,128)} %param.14) | data formatting | bytes 4194304 | tf_op args[4]
  137.0 2.0 %convert_element_type.42 = f32[128,8,1152]{2,1,0:T(8,128)S(1)} convert(bf16[128,8,1152]{2,1,0:T(8,128)(2,1)} %all-to-all-done.2) | non-fusion elementwise | flops 1179648 | bytes 7077888 | tf_op jit(solution)/shard_map/convert_element_type | solution.py:104
  139.0 0.0 copy-start.1
  139.0 2.1 %copy-done.1 = f32[128,8,1152]{2,1,0:T(8,128)} copy-done((f32[128,8,1152]{2,1,0:T(8,128)}, f32[128,8,1152]{2,1,0:T(8,128)S(1)}, u32[]{:S(2)}) %copy-start.1) | copy-done | bytes 4718616
  141.2 0.2 fusion.18
  141.4 0.7 mul.46
  142.1 0.0 all-to-all-done.3
  142.1 0.1 reduce_sum.31
  142.1 0.9 broadcast_in_dim.20
  143.0 4.8 %all-to-all-start.4 = ((bf16[4,512,128]{2,1,0:T(8,128)(2,1)}), bf16[4,512,128]{2,1,0:T(8,128)(2,1)S(1)}, u32[]{:S(2)}, u32[]{:S(2)}) async-start(bf16[4,512,128]{2,1,0:T(8,128)(2,1)} %broadcast_in_dim.20), calls=%async_computation.4 | async-start | bytes 1048576 | tf_op jit(solution)/shard_map/all_to_all | solution.py:22
  147.8 5.0 %fusion.10 = f32[1024,1024]{1,0:T(8,128)} fusion(f32[128,8,1152]{2,1,0:T(8,128)} %copy-done.1), kind=kLoop, calls=%fused_computation.14 | loop fusion | flops 1048576 | bytes 8388608 | tf_op jit(solution)/shard_map/mul | solution.py:105
  152.8 3.6 %all-to-all-done.4 = bf16[4,512,128]{2,1,0:T(8,128)(2,1)S(1)} async-done(((bf16[4,512,128]{2,1,0:T(8,128)(2,1)}), bf16[4,512,128]{2,1,0:T(8,128)(2,1)S(1)}, u32[]{:S(2)}, u32[]{:S(2)}) %all-to-all-start.4) | async-done | bytes 524320 | tf_op jit(solution)/shard_map/all_to_all | solution.py:22
  156.4 7.0 %fusion.6 = f32[4096,256]{0,1:T(8,128)S(1)} fusion(s32[2048]{0:T(1024)S(1)} %bitcast.34, bf16[2048,128]{1,0:T(8,128)(2,1)S(1)} %bitcast.26), kind=kOutput, calls=%fused_computation.8 | convolution fusion | flops 4303355904 | bytes 4726784 | tf_op jit(solution)/shard_map/dot_general | solution.py:100
  163.4 0.0 copy-start.9
  163.4 0.0 copy-start.2
  163.4 0.1 compare_reduce_fusion
  163.4 0.2 multiply_reduce_fusion
  163.6 0.5 copy-done.9
  164.1 0.6 fusion.22
  164.7 0.3 copy-done.2
  165.0 1.8 %subtract_select_fusion = f32[4096,128]{0,1:T(8,128)} fusion(f32[4096,128]{0,1:T(8,128)S(1)} %copy-done.2, f32[4096,256]{0,1:T(8,128)S(1)} %fusion.6, f32[4096]{0:T(1024)S(1)} %get-tuple-element.33, pred[4096]{0:T(1024)(128)(4,1)S(1)} %compare_reduce_fusion), kind=kLoop, calls=%fused_computation.24 | loop fusion | flops 2621440 | bytes 6311936 | tf_op jit(solution)/shard_map/jit(_where)/select_n | solution.py:108
  166.8 2.9 %copy.26 = f32[4096,128]{1,0:T(8,128)} copy(f32[4096,128]{0,1:T(8,128)} %subtract_select_fusion) | data formatting | bytes 4194304
  (5 shorter events, 0.1 us)
Async XLA Ops:
  0.6 20.4 %copy-start = (bf16[1024,1024]{1,0:T(8,128)(2,1)S(1)}, bf16[1024,1024]{1,0:T(8,128)(2,1)}, u32[]{:S(2)}) copy-start(bf16[1024,1024]{1,0:T(8,128)(2,1)} %param.12) | copy-start | bytes 6291460
  0.6 2.1 %copy-start.3 = (bf16[512,1024]{1,0:T(8,128)(2,1)S(1)}, bf16[512,1024]{1,0:T(8,128)(2,1)}, u32[]{:S(2)}) copy-start(bf16[512,1024]{1,0:T(8,128)(2,1)} %param.10) | copy-start | bytes 3145732
  0.7 2.3 %copy-start.4 = (bf16[512,1024]{1,0:T(8,128)(2,1)S(1)}, bf16[512,1024]{1,0:T(8,128)(2,1)}, u32[]{:S(2)}) copy-start(bf16[512,1024]{1,0:T(8,128)(2,1)} %param.11) | copy-start | bytes 3145732
  9.2 44.5 %all-to-all-start = ((bf16[128,8,1152]{2,1,0:T(8,128)(2,1)}), bf16[128,8,1152]{2,1,0:T(8,128)(2,1)}, u32[]{:S(2)}, u32[]{:S(2)}) async-start(bf16[128,8,1152]{2,1,0:T(8,128)(2,1)} %fusion.11), calls=%async_computation | async-start | bytes 4718592 | tf_op jit(solution)/shard_map/all_to_all | solution.py:62
  21.1 1.3 copy-start.5
  21.1 1.3 copy-start.12
  23.9 1.0 copy-start.6
  24.9 1.9 %copy-start.10 = (s32[1,32]{1,0:T(1,128)S(1)}, s32[1,32]{1,0:T(1,128)}, u32[]{:S(2)}) copy-start(s32[1,32]{1,0:T(1,128)} %param.17) | copy-start | bytes 388
  24.9 2.0 %copy-start.7 = (s32[1,32,256]{2,1,0:T(8,128)S(1)}, s32[1,32,256]{2,1,0:T(8,128)}, u32[]{:S(2)}) copy-start(s32[1,32,256]{2,1,0:T(8,128)} %param.16) | copy-start | bytes 98308
  53.7 34.9 %all-to-all-start.1 = ((bf16[32,256,128]{2,1,0:T(8,128)(2,1)}), bf16[32,256,128]{2,1,0:T(8,128)(2,1)}, u32[]{:S(2)}, u32[]{:S(2)}) async-start(bf16[32,256,128]{2,1,0:T(8,128)(2,1)} %bitcast.25), calls=%async_computation.1 | async-start | bytes 4194304 | tf_op jit(solution)/shard_map/all_to_all | solution.py:81
  90.2 6.1 %copy-start.8 = (s32[1,32,256]{2,1,0:T(8,128)S(1)}, s32[1,32,256]{2,1,0:T(8,128)}, u32[]{:S(2)}) copy-start(s32[1,32,256]{2,1,0:T(8,128)} %param.18) | copy-start | bytes 98308
  90.2 6.1 %copy-start.11 = (s32[1,2048]{1,0:T(1,128)S(1)}, s32[1,2048]{1,0:T(1,128)}, u32[]{:S(2)}) copy-start(s32[1,2048]{1,0:T(1,128)} %param.19) | copy-start | bytes 24580
  90.2 38.9 %all-to-all-start.2 = ((bf16[128,8,1152]{2,1,0:T(8,128)(2,1)}), bf16[128,8,1152]{2,1,0:T(8,128)(2,1)}, u32[]{:S(2)}, u32[]{:S(2)}) async-start(bf16[128,8,1152]{2,1,0:T(8,128)(2,1)} %broadcast_in_dim.19), calls=%async_computation.2 | async-start | bytes 4718592 | tf_op jit(solution)/shard_map/all_to_all | solution.py:88
  129.1 12.9 %all-to-all-start.3 = ((bf16[4,512,128]{2,1,0:T(8,128)(2,1)}), bf16[4,512,128]{2,1,0:T(8,128)(2,1)S(1)}, u32[]{:S(2)}, u32[]{:S(2)}) async-start(bf16[4,512,128]{2,1,0:T(8,128)(2,1)} %bitcast.8), calls=%async_computation.3 | async-start | bytes 1048576 | tf_op jit(solution)/shard_map/all_to_all | solution.py:19
  139.0 2.1 %copy-start.1 = (f32[128,8,1152]{2,1,0:T(8,128)}, f32[128,8,1152]{2,1,0:T(8,128)S(1)}, u32[]{:S(2)}) copy-start(f32[128,8,1152]{2,1,0:T(8,128)S(1)} %convert_element_type.42) | copy-start | bytes 14155780
  143.0 13.4 %all-to-all-start.4 = ((bf16[4,512,128]{2,1,0:T(8,128)(2,1)}), bf16[4,512,128]{2,1,0:T(8,128)(2,1)S(1)}, u32[]{:S(2)}, u32[]{:S(2)}) async-start(bf16[4,512,128]{2,1,0:T(8,128)(2,1)} %broadcast_in_dim.20), calls=%async_computation.4 | async-start | bytes 1048576 | tf_op jit(solution)/shard_map/all_to_all | solution.py:22
  163.4 0.7 copy-start.9
  163.4 1.6 copy-start.2

commit v4 on v3

--- a/solution.py
+++ b/solution.py
@@ -83,16 +83,13 @@
     mine_w = lax.dot_general(
         ones, got_w, (((0,), (0,)), ((), ())), preferred_element_type=jnp.float32
     ).astype(jnp.bfloat16)
-    spread = jnp.broadcast_to(mine_w[None], got_w.shape)
-    spread, incoming = lax.optimization_barrier((spread, incoming))
-    full_w = lax.all_to_all(spread, axes, 0, 0, tiled=True)
+    full_w = lax.all_gather(mine_w, axes, axis=0, tiled=False)
 
     incoming_rows = incoming.reshape(-1, width)
     slot_rows = recv_rows[0].reshape(-1)
     touched = touched_rows[0]
     select = (touched[:, None] == slot_rows[None, :]).astype(jnp.bfloat16)
     local_sums = jnp.dot(select, incoming_rows, preferred_element_type=jnp.float32)
-    full_w, local_sums = lax.optimization_barrier((full_w, local_sums))
     touched_grads = rep_sum(local_sums, rep).astype(jnp.bfloat16)
     row_range = jnp.arange(shard_rows, dtype=jnp.int32)
     place = (row_range[:, None] == touched[None, :]).astype(jnp.bfloat16)
@@ -101,7 +98,7 @@
     row_grads = spread_rows[:, :width]
     marks = spread_rows[:, width] > 0.5
 
-    full_w = full_w.astype(jnp.float32)
+    full_w = full_w.astype(jnp.float32).reshape(devices, -1, dim + 128)
     weight_grad = full_w[:, :, :dim].reshape(dim, dim) * scale
     bias_grad = full_w[:, :, dim].reshape(dim) * scale
     upd_table, upd_accum = adagrad_rows(emb_table, row_accum, row_grads)

time: 170 us -> 159 us (0.935); the launches traced: 170 us -> 157 us
  waiting for transfers between devices: 55.6 us -> 35 us
  between operations: 0.88 us -> 14.3 us
  blocking collectives: 0 us -> 11.3 us
  starting transfers between devices: 30.9 us -> 20.3 us
  local copies, waits for them, and re-layouts: 17 us -> 13.9 us
  other arithmetic: 15.3 us -> 12.8 us
    all_to_all x2 -> x0, waiting for transfers between devices: 20.5 us -> none  [the longest x1 20.5 us: per_device(): full_w = lax.all_to_all(spread, axes, 0, 0, tiled=True)]
    all_to_all x0 -> x1, blocking collectives: none -> 11.3 us  [rep_sum(): got = lax.all_to_all(parts, 'rep', 0, 0, tiled=True)]
    all_to_all x2 -> x0, starting transfers between devices: 9.54 us -> none  [the longest x1 6.07 us: per_device(): full_w = lax.all_to_all(spread, axes, 0, 0, tiled=True)]
    mul x1, other arithmetic: 5.04 us -> 2.6 us  [per_device(): weight_grad = full_w[:, :, :dim].reshape(dim, dim) * scale]
    unnamed x30 -> x28, local copies, waits for them, and re-layouts: 9.94 us -> 7.83 us
  transfers between devices with their start and end apart: 5 -> 4, of which waited for: 4 -> 3; matrix products, arithmetic and copies ran while one was open for 32% -> 38% of each run, Pallas kernels for 0% -> 0%
where the time goes in v4:
time: 159 us; the launch traced here: 157 us
  matrix products  49 us (31%)
  waiting for transfers between devices  35 us (22%)
  starting transfers between devices  20.3 us (13%)
  between operations  14.3 us (9%)
  local copies, waits for them, and re-layouts  13.9 us (9%)
  other arithmetic  12.8 us (8%)
  blocking collectives  11.3 us (7%)
    all_to_all x1, waiting for transfers between devices, per_device(): lax.all_to_all(outgoing, 'shard', split_axis=0, concat_axis=0, tiled=True)  27 us
    dot_general x1, matrix products, per_device(): jnp.dot(pick, pooled, preferred_element_type=jnp.float32)  23.1 us
    all_to_all x1, starting transfers between devices, per_device(): got_w = lax.all_to_all(packed, axes, 0, 0, tiled=True)  11.8 us
    dot_general x1, matrix products, per_device(): jnp.dot(select, incoming_rows, preferred_element_type=jnp.float32)  11.3 us
    all_to_all x1, blocking collectives, rep_sum(): got = lax.all_to_all(parts, 'rep', 0, 0, tiled=True)  11.3 us
    unnamed x28, local copies, waits for them, and re-layouts  7.83 us
    dot_general x1, matrix products, per_device(): spread_rows = jnp.dot(place, with_marks, preferred_element_type=jnp.float32)  6.96 us
    all_to_all x1, starting transfers between devices, per_device(): lax.all_to_all(outgoing, 'shard', split_axis=0, concat_axis=0, tiled=True)  4.76 us
  transfers between devices with their start and end apart: 4, of which 3 were waited for; matrix products, arithmetic and copies ran while one was open for 38% of the time, Pallas kernels for 0%

profile of v4, /device:TPU:0, one launch (start us, length us, event | category | flops | bytes accessed | tf_op | source)
XLA Modules:
  0.0 156.6 jit_solution(18300953918418954717)
XLA Ops:
  7.2 0.0 copy-start
  7.2 0.0 copy-start.2
  7.2 0.0 copy-start.3
  7.2 2.1 %fusion.23 = bf16[1024]{0:T(1024)(128)(2,1)S(1)} fusion(bf16[512,1024]{1,0:T(8,128)(2,1)} %param.10, bf16[512,1024]{1,0:T(8,128)(2,1)} %param.11), kind=kLoop, calls=%fused_computation.32 | loop fusion | flops 2620416 | bytes 2099200 | tf_op jit(solution)/shard_map/reduce_sum | solution.py:60
  9.3 0.0 copy-done.2
  9.3 0.2 copy-done.3
  9.5 2.6 %convert_bitcast_fusion = bf16[128,8,1024]{2,1,0:T(8,128)(2,1)} fusion(bf16[512,1024]{1,0:T(8,128)(2,1)S(1)} %copy-done.2, bf16[512,1024]{1,0:T(8,128)(2,1)S(1)} %copy-done.3), kind=kOutput, calls=%fused_computation.28 | convolution fusion | flops 1076887552 | bytes 4194304 | tf_op jit(solution)/shard_map/dot_general | solution.py:57
  12.1 0.4 reshape.76
  12.6 3.2 %fusion.14 = bf16[128,8,1152]{2,1,0:T(8,128)(2,1)} fusion(bf16[128,8,1]{2,1,0:T(8,128)(2,1)S(1)} %reshape.76, bf16[128,8,1024]{2,1,0:T(8,128)(2,1)} %convert_bitcast_fusion), kind=kLoop, calls=%fused_computation.19 | loop fusion | flops 7077888 | bytes 4458496 | tf_op jit(solution)/shard_map/concatenate | solution.py:30
  15.8 0.0 copy-start.9
  15.8 0.0 copy-start.6
  15.8 11.8 %all-to-all-start = ((bf16[128,8,1152]{2,1,0:T(8,128)(2,1)}), bf16[128,8,1152]{2,1,0:T(8,128)(2,1)}, u32[]{:S(2)}, u32[]{:S(2)}) async-start(bf16[128,8,1152]{2,1,0:T(8,128)(2,1)} %fusion.14), calls=%async_computation | async-start | bytes 4718592 | tf_op jit(solution)/shard_map/all_to_all | solution.py:62
  27.6 0.0 copy-done.9
  27.6 0.1 iota_compare_fusion.7
  27.7 0.0 copy-done.6
  27.7 0.0 copy-done
  27.8 0.0 copy-start.4
  27.8 0.0 copy-start.11
  27.8 1.2 fusion.30
  29.0 0.0 copy-done.4
  29.0 0.0 copy-done.11
  29.1 1.5 fusion.19
  30.6 0.0 copy-start.5
  30.6 1.0 copy-done.5
  31.6 0.1 slice.26
  31.6 1.8 %reshape.67 = bf16[3584,128]{1,0:T(8,128)(2,1)} reshape(bf16[512,896]{1,0:T(8,128)(2,1)S(1)} %slice.26) | data formatting | bytes 1835008 | tf_op jit(solution)/shard_map/reshape | solution.py:69
  33.5 23.1 %fusion.8 = bf16[8192,128]{1,0:T(8,128)(2,1)} fusion(bf16[3584,128]{1,0:T(8,128)(2,1)} %reshape.67, s32[8192]{0:T(1024)S(1)} %broadcast_select_fusion), kind=kOutput, calls=%fused_computation.10 | convolution fusion | flops 7546601472 | bytes 3047424 | tf_op jit(solution)/shard_map/dot_general | solution.py:77
  56.6 3.7 %all-to-all-done = bf16[128,8,1152]{2,1,0:T(8,128)(2,1)} async-done(((bf16[128,8,1152]{2,1,0:T(8,128)(2,1)}), bf16[128,8,1152]{2,1,0:T(8,128)(2,1)}, u32[]{:S(2)}, u32[]{:S(2)}) %all-to-all-start) | async-done | bytes 2359328 | tf_op jit(solution)/shard_map/all_to_all | solution.py:62
  60.3 4.8 %all-to-all-start.1 = ((bf16[32,256,128]{2,1,0:T(8,128)(2,1)}), bf16[32,256,128]{2,1,0:T(8,128)(2,1)}, u32[]{:S(2)}, u32[]{:S(2)}) async-start(bf16[32,256,128]{2,1,0:T(8,128)(2,1)} %bitcast.28), calls=%async_computation.1 | async-start | bytes 4194304 | tf_op jit(solution)/shard_map/all_to_all | solution.py:81
  65.1 0.0 copy-start.7
  65.1 0.0 copy-start.10
  65.1 0.3 all-gather.3.cloned.1.call-start
  65.3 2.2 %fusion.15 = bf16[1,8,1152]{2,0,1:T(2,128)(2,1)S(1)} fusion(bf16[128,8,1152]{2,1,0:T(8,128)(2,1)} %all-to-all-done), kind=kOutput, calls=%fused_computation.21 | convolution fusion | flops 2359296 | bytes 2377728 | tf_op jit(solution)/shard_map/dot_general | solution.py:83
  67.5 0.6 copy.35
  68.1 0.0 all-gather.3.cloned.1.call-update
  68.2 0.0 copy-done.7
  68.2 27.0 %all-to-all-done.1 = bf16[32,256,128]{2,1,0:T(8,128)(2,1)} async-done(((bf16[32,256,128]{2,1,0:T(8,128)(2,1)}), bf16[32,256,128]{2,1,0:T(8,128)(2,1)}, u32[]{:S(2)}, u32[]{:S(2)}) %all-to-all-start.1) | async-done | bytes 2097184 | tf_op jit(solution)/shard_map/all_to_all | solution.py:81
  95.2 0.0 copy-done.10
  95.2 11.3 %fusion.11 = bf16[2048,128]{1,0:T(8,128)(2,1)S(1)} fusion(bf16[8192,128]{1,0:T(8,128)(2,1)} %bitcast.9, s32[8192]{0:T(1024)S(1)} %bitcast.35, s32[2048]{0:T(1024)S(1)} %bitcast.37), kind=kOutput, calls=%fused_computation.18 | convolution fusion | flops 4312006656 | bytes 2662400 | tf_op jit(solution)/shard_map/dot_general | solution.py:92
  106.5 11.3 %all_to_all.20 = bf16[4,512,128]{2,1,0:T(8,128)(2,1)S(1)} all-to-all(bf16[4,512,128]{2,1,0:T(8,128)(2,1)S(1)} %bitcast.30), channel_id=1, replica_groups=mesh['rep'=4,'shard'=32] {'rep'}, dimensions={0} | all-to-all | bytes 1048576 | tf_op jit(solution)/shard_map/all_to_all | solution.py:19
  117.8 0.1 reduce_sum.31
  117.9 0.9 broadcast_in_dim.32
  118.8 3.5 %all-to-all-start.3 = ((bf16[4,512,128]{2,1,0:T(8,128)(2,1)}), bf16[4,512,128]{2,1,0:T(8,128)(2,1)S(1)}, u32[]{:S(2)}, u32[]{:S(2)}) async-start(bf16[4,512,128]{2,1,0:T(8,128)(2,1)} %broadcast_in_dim.32), calls=%async_computation.3 | async-start | bytes 1048576 | tf_op jit(solution)/shard_map/all_to_all | solution.py:22
  122.3 1.6 %slice.29 = bf16[512,128]{1,0:T(8,128)(2,1)} slice(bf16[512,1024]{1,0:T(8,128)(2,1)} %copy-done.5), slice={[0:512], [0:128]} | slice | bytes 262144 | tf_op jit(solution)/shard_map/slice | solution.py:68
  123.8 2.9 %copy.24 = f32[4096,128]{0,1:T(8,128)} copy(f32[4096,128]{1,0:T(8,128)} %param.14) | data formatting | bytes 4194304 | tf_op args[4]
  126.7 4.3 %all-to-all-done.3 = bf16[4,512,128]{2,1,0:T(8,128)(2,1)S(1)} async-done(((bf16[4,512,128]{2,1,0:T(8,128)(2,1)}), bf16[4,512,128]{2,1,0:T(8,128)(2,1)S(1)}, u32[]{:S(2)}, u32[]{:S(2)}) %all-to-all-start.3) | async-done | bytes 524320 | tf_op jit(solution)/shard_map/all_to_all | solution.py:22
  131.0 7.0 %fusion.6 = f32[4096,256]{0,1:T(8,128)S(1)} fusion(s32[2048]{0:T(1024)S(1)} %bitcast.38, bf16[2048,128]{1,0:T(8,128)(2,1)S(1)} %bitcast.29), kind=kOutput, calls=%fused_computation.8 | convolution fusion | flops 4303355904 | bytes 4726784 | tf_op jit(solution)/shard_map/dot_general | solution.py:97
  138.0 0.0 copy-start.8
  138.0 0.0 copy-start.1
  138.0 0.1 compare_reduce_fusion
  138.1 0.2 multiply_reduce_fusion
  138.2 0.5 copy-done.8
  138.7 0.6 fusion.25
  139.3 0.3 copy-done.1
  139.6 1.8 %subtract_select_fusion = f32[4096,128]{0,1:T(8,128)} fusion(f32[4096,128]{0,1:T(8,128)S(1)} %copy-done.1, f32[4096,256]{0,1:T(8,128)S(1)} %fusion.6, f32[4096]{0:T(1024)S(1)} %get-tuple-element.25, pred[4096]{0:T(1024)(128)(4,1)S(1)} %compare_reduce_fusion), kind=kLoop, calls=%fused_computation.26 | loop fusion | flops 2621440 | bytes 6311936 | tf_op jit(solution)/shard_map/jit(_where)/select_n | solution.py:105
  141.4 2.9 %copy.26 = f32[4096,128]{1,0:T(8,128)} copy(f32[4096,128]{0,1:T(8,128)} %subtract_select_fusion) | data formatting | bytes 4194304
  144.3 0.0 all-gather.3.cloned.1.call-done
  144.3 2.0 %bitcast_convert_fusion = f32[128,8,1152]{2,1,0:T(8,128)S(1)} fusion(bf16[1024,1152]{1,0:T(8,128)(2,1)} %all-gather.3.cloned.1.call-done), kind=kLoop, calls=%fused_computation.20 | loop fusion | flops 1179648 | bytes 7077888 | tf_op jit(solution)/shard_map/convert_element_type | solution.py:101
  146.3 0.2 fusion.21
  146.5 2.6 %fusion.10 = f32[1024,1024]{1,0:T(8,128)} fusion(f32[128,8,1152]{2,1,0:T(8,128)S(1)} %bitcast_convert_fusion), kind=kLoop, calls=%fused_computation.14 | loop fusion | flops 1048576 | bytes 8388608 | tf_op jit(solution)/shard_map/mul | solution.py:102
  149.1 0.7 mul.46
  (4 shorter events, 0.1 us)
Async XLA Ops:
  7.2 20.6 %copy-start = (bf16[1024,1024]{1,0:T(8,128)(2,1)S(1)}, bf16[1024,1024]{1,0:T(8,128)(2,1)}, u32[]{:S(2)}) copy-start(bf16[1024,1024]{1,0:T(8,128)(2,1)} %param.12) | copy-start | bytes 6291460
  7.2 2.1 %copy-start.2 = (bf16[512,1024]{1,0:T(8,128)(2,1)S(1)}, bf16[512,1024]{1,0:T(8,128)(2,1)}, u32[]{:S(2)}) copy-start(bf16[512,1024]{1,0:T(8,128)(2,1)} %param.10) | copy-start | bytes 3145732
  7.2 2.3 %copy-start.3 = (bf16[512,1024]{1,0:T(8,128)(2,1)S(1)}, bf16[512,1024]{1,0:T(8,128)(2,1)}, u32[]{:S(2)}) copy-start(bf16[512,1024]{1,0:T(8,128)(2,1)} %param.11) | copy-start | bytes 3145732
  15.8 11.8 %copy-start.9 = (s32[1,32]{1,0:T(1,128)S(1)}, s32[1,32]{1,0:T(1,128)}, u32[]{:S(2)}) copy-start(s32[1,32]{1,0:T(1,128)} %param.17) | copy-start | bytes 388
  15.8 11.9 %copy-start.6 = (s32[1,32,256]{2,1,0:T(8,128)S(1)}, s32[1,32,256]{2,1,0:T(8,128)}, u32[]{:S(2)}) copy-start(s32[1,32,256]{2,1,0:T(8,128)} %param.16) | copy-start | bytes 98308
  15.8 44.5 %all-to-all-start = ((bf16[128,8,1152]{2,1,0:T(8,128)(2,1)}), bf16[128,8,1152]{2,1,0:T(8,128)(2,1)}, u32[]{:S(2)}, u32[]{:S(2)}) async-start(bf16[128,8,1152]{2,1,0:T(8,128)(2,1)} %fusion.14), calls=%async_computation | async-start | bytes 4718592 | tf_op jit(solution)/shard_map/all_to_all | solution.py:62
  27.8 1.3 copy-start.4
  27.8 1.3 copy-start.11
  30.6 1.0 copy-start.5
  60.3 34.9 %all-to-all-start.1 = ((bf16[32,256,128]{2,1,0:T(8,128)(2,1)}), bf16[32,256,128]{2,1,0:T(8,128)(2,1)}, u32[]{:S(2)}, u32[]{:S(2)}) async-start(bf16[32,256,128]{2,1,0:T(8,128)(2,1)} %bitcast.28), calls=%async_computation.1 | async-start | bytes 4194304 | tf_op jit(solution)/shard_map/all_to_all | solution.py:81
  65.1 3.1 %copy-start.7 = (s32[1,32,256]{2,1,0:T(8,128)S(1)}, s32[1,32,256]{2,1,0:T(8,128)}, u32[]{:S(2)}) copy-start(s32[1,32,256]{2,1,0:T(8,128)} %param.18) | copy-start | bytes 98308
  65.1 30.1 %copy-start.10 = (s32[1,2048]{1,0:T(1,128)S(1)}, s32[1,2048]{1,0:T(1,128)}, u32[]{:S(2)}) copy-start(s32[1,2048]{1,0:T(1,128)} %param.19) | copy-start | bytes 24580
  65.1 79.2 %all-gather.3.cloned.1.call-start = ((), (), s32[]{:S(2)}) async-start(), calls=%async_computation.4 | async-start | bytes 2377728 | tf_op jit(solution)/shard_map/all_gather | solution.py:86
  118.8 12.2 %all-to-all-start.3 = ((bf16[4,512,128]{2,1,0:T(8,128)(2,1)}), bf16[4,512,128]{2,1,0:T(8,128)(2,1)S(1)}, u32[]{:S(2)}, u32[]{:S(2)}) async-start(bf16[4,512,128]{2,1,0:T(8,128)(2,1)} %broadcast_in_dim.32), calls=%async_computation.3 | async-start | bytes 1048576 | tf_op jit(solution)/shard_map/all_to_all | solution.py:22
  138.0 0.7 copy-start.8
  138.0 1.6 %copy-start.1 = (f32[4096,128]{0,1:T(8,128)S(1)}, f32[4096,128]{0,1:T(8,128)}, u32[]{:S(2)}) copy-start(f32[4096,128]{0,1:T(8,128)} %copy.24) | copy-start | bytes 6291460
Sparse Core Ops, SparseCore 0:
  68.8 70.5 all-gather.2

commit v5 on v4

--- a/solution.py
+++ b/solution.py
@@ -14,13 +14,12 @@
 
 
 def rep_sum(local, rep):
-    rows = local.shape[0]
-    parts = local.astype(jnp.bfloat16).reshape(rep, rows // rep, -1)
+    parts = jnp.broadcast_to(local.astype(jnp.bfloat16)[None], (rep,) + local.shape)
     got = lax.all_to_all(parts, "rep", 0, 0, tiled=True)
-    mine = jnp.sum(got.astype(jnp.float32), axis=0).astype(jnp.bfloat16)
-    spread = jnp.broadcast_to(mine[None], parts.shape)
-    full = lax.all_to_all(spread, "rep", 0, 0, tiled=True)
-    return full.reshape(rows, -1).astype(jnp.float32)
+    total = got[0].astype(jnp.float32)
+    for k in range(1, rep):
+        total = total + got[k].astype(jnp.float32)
+    return total
 
 
 def pack_grads(weight_part, bias_part, devices):

time: 159 us -> 169 us (1.063); the launches traced: 157 us -> 169 us
  waiting for transfers between devices: 35 us -> 54.8 us
  blocking collectives: 11.3 us -> 0 us
  other arithmetic: 12.8 us -> 14.5 us
    all_to_all x1, waiting for transfers between devices: 4.3 us -> 24.1 us  [rep_sum(): got = lax.all_to_all(parts, 'rep', 0, 0, tiled=True)]
    all_to_all x1 -> x0, blocking collectives: 11.3 us -> none  [rep_sum(): got = lax.all_to_all(parts, 'rep', 0, 0, tiled=True)]
    add x0 -> x1, other arithmetic: none -> 1.79 us  [rep_sum(): total = total + got[k].astype(jnp.float32)]
  transfers between devices with their start and end apart: 4 -> 4, of which waited for: 3 -> 3; matrix products, arithmetic and copies ran while one was open for 38% -> 37% of each run, Pallas kernels for 0% -> 0%
where the time goes in v5:
time: 169 us
  waiting for transfers between devices  54.8 us (32%)
  matrix products  49 us (29%)
  starting transfers between devices  21.5 us (13%)
  local copies, waits for them, and re-layouts  14.6 us (9%)
  other arithmetic  14.5 us (9%)
  between operations  14.3 us (8%)
    all_to_all x1, waiting for transfers between devices, per_device(): lax.all_to_all(outgoing, 'shard', split_axis=0, concat_axis=0, tiled=True)  27 us
    all_to_all x1, waiting for transfers between devices, rep_sum(): got = lax.all_to_all(parts, 'rep', 0, 0, tiled=True)  24.1 us
    dot_general x1, matrix products, per_device(): jnp.dot(pick, pooled, preferred_element_type=jnp.float32)  23.1 us
    all_to_all x1, starting transfers between devices, per_device(): got_w = lax.all_to_all(packed, axes, 0, 0, tiled=True)  11.8 us
    dot_general x1, matrix products, per_device(): jnp.dot(select, incoming_rows, preferred_element_type=jnp.float32)  11.3 us
    unnamed x28, local copies, waits for them, and re-layouts  7.82 us
    dot_general x1, matrix products, per_device(): spread_rows = jnp.dot(place, with_marks, preferred_element_type=jnp.float32)  6.99 us
    all_to_all x1, starting transfers between devices, per_device(): lax.all_to_all(outgoing, 'shard', split_axis=0, concat_axis=0, tiled=True)  4.91 us
  transfers between devices with their start and end apart: 4, of which 3 were waited for; matrix products, arithmetic and copies ran while one was open for 37% of the time, Pallas kernels for 0%

profile of v5, /device:TPU:0, one launch (start us, length us, event | category | flops | bytes accessed | tf_op | source)
XLA Modules:
  0.0 168.7 jit_solution(9934744717385527566)
XLA Ops:
  7.2 0.0 copy-start
  7.2 0.0 copy-start.2
  7.2 0.0 copy-start.3
  7.2 2.1 %fusion.24 = bf16[1024]{0:T(1024)(128)(2,1)S(1)} fusion(bf16[512,1024]{1,0:T(8,128)(2,1)} %param.10, bf16[512,1024]{1,0:T(8,128)(2,1)} %param.11), kind=kLoop, calls=%fused_computation.34 | loop fusion | flops 2620416 | bytes 2099200 | tf_op jit(solution)/shard_map/reduce_sum | solution.py:59
  9.3 0.0 copy-done.2
  9.3 0.2 copy-done.3
  9.5 2.6 %convert_bitcast_fusion = bf16[128,8,1024]{2,1,0:T(8,128)(2,1)} fusion(bf16[512,1024]{1,0:T(8,128)(2,1)S(1)} %copy-done.2, bf16[512,1024]{1,0:T(8,128)(2,1)S(1)} %copy-done.3), kind=kOutput, calls=%fused_computation.28 | convolution fusion | flops 1076887552 | bytes 4194304 | tf_op jit(solution)/shard_map/dot_general | solution.py:56
  12.1 0.4 reshape.76
  12.6 3.2 %fusion.14 = bf16[128,8,1152]{2,1,0:T(8,128)(2,1)} fusion(bf16[128,8,1]{2,1,0:T(8,128)(2,1)S(1)} %reshape.76, bf16[128,8,1024]{2,1,0:T(8,128)(2,1)} %convert_bitcast_fusion), kind=kLoop, calls=%fused_computation.19 | loop fusion | flops 7077888 | bytes 4458496 | tf_op jit(solution)/shard_map/concatenate | solution.py:29
  15.8 0.0 copy-start.9
  15.8 0.0 copy-start.6
  15.8 11.8 %all-to-all-start = ((bf16[128,8,1152]{2,1,0:T(8,128)(2,1)}), bf16[128,8,1152]{2,1,0:T(8,128)(2,1)}, u32[]{:S(2)}, u32[]{:S(2)}) async-start(bf16[128,8,1152]{2,1,0:T(8,128)(2,1)} %fusion.14), calls=%async_computation | async-start | bytes 4718592 | tf_op jit(solution)/shard_map/all_to_all | solution.py:61
  27.6 0.0 copy-done.9
  27.6 0.1 iota_compare_fusion.7
  27.7 0.0 copy-done.6
  27.7 0.0 copy-done
  27.8 0.0 copy-start.4
  27.8 0.0 copy-start.11
  27.8 1.2 fusion.31
  29.0 0.0 copy-done.4
  29.0 0.0 copy-done.11
  29.1 1.5 fusion.19
  30.6 0.0 copy-start.5
  30.6 1.0 copy-done.5
  31.6 0.1 slice.42
  31.7 1.8 %reshape.69 = bf16[3584,128]{1,0:T(8,128)(2,1)} reshape(bf16[512,896]{1,0:T(8,128)(2,1)S(1)} %slice.42) | data formatting | bytes 1835008 | tf_op jit(solution)/shard_map/reshape | solution.py:68
  33.5 23.1 %fusion.8 = bf16[8192,128]{1,0:T(8,128)(2,1)} fusion(bf16[3584,128]{1,0:T(8,128)(2,1)} %reshape.69, s32[8192]{0:T(1024)S(1)} %broadcast_select_fusion), kind=kOutput, calls=%fused_computation.10 | convolution fusion | flops 7546601472 | bytes 3047424 | tf_op jit(solution)/shard_map/dot_general | solution.py:76
  56.6 3.7 %all-to-all-done = bf16[128,8,1152]{2,1,0:T(8,128)(2,1)} async-done(((bf16[128,8,1152]{2,1,0:T(8,128)(2,1)}), bf16[128,8,1152]{2,1,0:T(8,128)(2,1)}, u32[]{:S(2)}, u32[]{:S(2)}) %all-to-all-start) | async-done | bytes 2359328 | tf_op jit(solution)/shard_map/all_to_all | solution.py:61
  60.3 0.0 copy-start.7
  60.3 4.9 %all-to-all-start.1 = ((bf16[32,256,128]{2,1,0:T(8,128)(2,1)}), bf16[32,256,128]{2,1,0:T(8,128)(2,1)}, u32[]{:S(2)}, u32[]{:S(2)}) async-start(bf16[32,256,128]{2,1,0:T(8,128)(2,1)} %bitcast.28), calls=%async_computation.1 | async-start | bytes 4194304 | tf_op jit(solution)/shard_map/all_to_all | solution.py:80
  65.2 0.0 copy-start.10
  65.2 0.3 all-gather.3.cloned.1.call-start
  65.5 0.0 copy-done.7
  65.5 2.2 %fusion.15 = bf16[1,8,1152]{2,0,1:T(2,128)(2,1)S(1)} fusion(bf16[128,8,1152]{2,1,0:T(8,128)(2,1)} %all-to-all-done), kind=kOutput, calls=%fused_computation.21 | convolution fusion | flops 2359296 | bytes 2377728 | tf_op jit(solution)/shard_map/dot_general | solution.py:82
  67.7 0.6 copy.35
  68.3 0.0 all-gather.3.cloned.1.call-update
  68.3 27.0 %all-to-all-done.1 = bf16[32,256,128]{2,1,0:T(8,128)(2,1)} async-done(((bf16[32,256,128]{2,1,0:T(8,128)(2,1)}), bf16[32,256,128]{2,1,0:T(8,128)(2,1)}, u32[]{:S(2)}, u32[]{:S(2)}) %all-to-all-start.1) | async-done | bytes 2097184 | tf_op jit(solution)/shard_map/all_to_all | solution.py:80
  95.4 0.0 copy-done.10
  95.4 11.3 %fusion.11 = bf16[2048,128]{1,0:T(8,128)(2,1)S(1)} fusion(bf16[8192,128]{1,0:T(8,128)(2,1)} %bitcast.9, s32[8192]{0:T(1024)S(1)} %bitcast.33, s32[2048]{0:T(1024)S(1)} %bitcast.35), kind=kOutput, calls=%fused_computation.18 | convolution fusion | flops 4312006656 | bytes 2662400 | tf_op jit(solution)/shard_map/dot_general | solution.py:91
  106.7 1.6 broadcast_in_dim.32
  108.3 4.5 %all-to-all-start.2 = ((bf16[4,2048,128]{2,1,0:T(8,128)(2,1)}), bf16[4,2048,128]{2,1,0:T(8,128)(2,1)}, u32[]{:S(2)}, u32[]{:S(2)}) async-start(bf16[4,2048,128]{2,1,0:T(8,128)(2,1)} %broadcast_in_dim.32), calls=%async_computation.2 | async-start | bytes 4194304 | tf_op jit(solution)/shard_map/all_to_all | solution.py:18
  112.7 1.6 slice.45
  114.3 2.9 %copy.24 = f32[4096,128]{0,1:T(8,128)} copy(f32[4096,128]{1,0:T(8,128)} %param.14) | data formatting | bytes 4194304 | tf_op args[4]
  117.2 24.1 %all-to-all-done.2 = bf16[4,2048,128]{2,1,0:T(8,128)(2,1)} async-done(((bf16[4,2048,128]{2,1,0:T(8,128)(2,1)}), bf16[4,2048,128]{2,1,0:T(8,128)(2,1)}, u32[]{:S(2)}, u32[]{:S(2)}) %all-to-all-start.2) | async-done | bytes 2097184 | tf_op jit(solution)/shard_map/all_to_all | solution.py:18
  141.3 1.8 %fusion.21 = bf16[2048,128]{1,0:T(8,128)(2,1)S(1)} fusion(bf16[4,2048,128]{2,1,0:T(8,128)(2,1)} %all-to-all-done.2), kind=kLoop, calls=%fused_computation.31 | loop fusion | flops 2097152 | bytes 2621440 | tf_op jit(solution)/shard_map/add | solution.py:21
  143.1 7.0 %fusion.6 = f32[4096,256]{0,1:T(8,128)S(1)} fusion(s32[2048]{0:T(1024)S(1)} %bitcast.36, bf16[2048,128]{1,0:T(8,128)(2,1)S(1)} %fusion.21), kind=kOutput, calls=%fused_computation.8 | convolution fusion | flops 4303355904 | bytes 4726784 | tf_op jit(solution)/shard_map/dot_general | solution.py:96
  150.1 0.0 copy-start.8
  150.1 0.0 copy-start.1
  150.1 0.1 compare_reduce_fusion
  150.2 0.2 multiply_reduce_fusion
  150.4 0.5 copy-done.8
  150.8 0.6 fusion.26
  151.4 0.3 copy-done.1
  151.7 1.8 %subtract_select_fusion = f32[4096,128]{0,1:T(8,128)} fusion(f32[4096,128]{0,1:T(8,128)S(1)} %copy-done.1, f32[4096,256]{0,1:T(8,128)S(1)} %fusion.6, f32[4096]{0:T(1024)S(1)} %get-tuple-element.25, pred[4096]{0:T(1024)(128)(4,1)S(1)} %compare_reduce_fusion), kind=kLoop, calls=%fused_computation.26 | loop fusion | flops 2621440 | bytes 6311936 | tf_op jit(solution)/shard_map/jit(_where)/select_n | solution.py:104
  153.5 2.9 %copy.26 = f32[4096,128]{1,0:T(8,128)} copy(f32[4096,128]{0,1:T(8,128)} %subtract_select_fusion) | data formatting | bytes 4194304
  156.4 0.0 all-gather.3.cloned.1.call-done
  156.4 2.0 %bitcast_convert_fusion = f32[128,8,1152]{2,1,0:T(8,128)S(1)} fusion(bf16[1024,1152]{1,0:T(8,128)(2,1)} %all-gather.3.cloned.1.call-done), kind=kLoop, calls=%fused_computation.20 | loop fusion | flops 1179648 | bytes 7077888 | tf_op jit(solution)/shard_map/convert_element_type | solution.py:100
  158.4 0.2 fusion.22
  158.6 2.6 %fusion.10 = f32[1024,1024]{1,0:T(8,128)} fusion(f32[128,8,1152]{2,1,0:T(8,128)S(1)} %bitcast_convert_fusion), kind=kLoop, calls=%fused_computation.14 | loop fusion | flops 1048576 | bytes 8388608 | tf_op jit(solution)/shard_map/mul | solution.py:101
  161.2 0.7 mul.46
  (4 shorter events, 0.1 us)
Async XLA Ops:
  7.2 20.6 %copy-start = (bf16[1024,1024]{1,0:T(8,128)(2,1)S(1)}, bf16[1024,1024]{1,0:T(8,128)(2,1)}, u32[]{:S(2)}) copy-start(bf16[1024,1024]{1,0:T(8,128)(2,1)} %param.12) | copy-start | bytes 6291460
  7.2 2.1 %copy-start.2 = (bf16[512,1024]{1,0:T(8,128)(2,1)S(1)}, bf16[512,1024]{1,0:T(8,128)(2,1)}, u32[]{:S(2)}) copy-start(bf16[512,1024]{1,0:T(8,128)(2,1)} %param.10) | copy-start | bytes 3145732
  7.2 2.3 %copy-start.3 = (bf16[512,1024]{1,0:T(8,128)(2,1)S(1)}, bf16[512,1024]{1,0:T(8,128)(2,1)}, u32[]{:S(2)}) copy-start(bf16[512,1024]{1,0:T(8,128)(2,1)} %param.11) | copy-start | bytes 3145732
  15.8 11.8 %copy-start.9 = (s32[1,32]{1,0:T(1,128)S(1)}, s32[1,32]{1,0:T(1,128)}, u32[]{:S(2)}) copy-start(s32[1,32]{1,0:T(1,128)} %param.17) | copy-start | bytes 388
  15.8 11.9 %copy-start.6 = (s32[1,32,256]{2,1,0:T(8,128)S(1)}, s32[1,32,256]{2,1,0:T(8,128)}, u32[]{:S(2)}) copy-start(s32[1,32,256]{2,1,0:T(8,128)} %param.16) | copy-start | bytes 98308
  15.8 44.5 %all-to-all-start = ((bf16[128,8,1152]{2,1,0:T(8,128)(2,1)}), bf16[128,8,1152]{2,1,0:T(8,128)(2,1)}, u32[]{:S(2)}, u32[]{:S(2)}) async-start(bf16[128,8,1152]{2,1,0:T(8,128)(2,1)} %fusion.14), calls=%async_computation | async-start | bytes 4718592 | tf_op jit(solution)/shard_map/all_to_all | solution.py:61
  27.8 1.3 copy-start.4
  27.8 1.3 copy-start.11
  30.6 1.0 copy-start.5
  60.3 5.2 %copy-start.7 = (s32[1,32,256]{2,1,0:T(8,128)S(1)}, s32[1,32,256]{2,1,0:T(8,128)}, u32[]{:S(2)}) copy-start(s32[1,32,256]{2,1,0:T(8,128)} %param.18) | copy-start | bytes 98308
  60.3 35.1 %all-to-all-start.1 = ((bf16[32,256,128]{2,1,0:T(8,128)(2,1)}), bf16[32,256,128]{2,1,0:T(8,128)(2,1)}, u32[]{:S(2)}, u32[]{:S(2)}) async-start(bf16[32,256,128]{2,1,0:T(8,128)(2,1)} %bitcast.28), calls=%async_computation.1 | async-start | bytes 4194304 | tf_op jit(solution)/shard_map/all_to_all | solution.py:80
  65.2 30.1 %copy-start.10 = (s32[1,2048]{1,0:T(1,128)S(1)}, s32[1,2048]{1,0:T(1,128)}, u32[]{:S(2)}) copy-start(s32[1,2048]{1,0:T(1,128)} %param.19) | copy-start | bytes 24580
  65.2 91.2 %all-gather.3.cloned.1.call-start = ((), (), s32[]{:S(2)}) async-start(), calls=%async_computation.3 | async-start | bytes 2377728 | tf_op jit(solution)/shard_map/all_gather | solution.py:85
  108.3 33.0 %all-to-all-start.2 = ((bf16[4,2048,128]{2,1,0:T(8,128)(2,1)}), bf16[4,2048,128]{2,1,0:T(8,128)(2,1)}, u32[]{:S(2)}, u32[]{:S(2)}) async-start(bf16[4,2048,128]{2,1,0:T(8,128)(2,1)} %broadcast_in_dim.32), calls=%async_computation.2 | async-start | bytes 4194304 | tf_op jit(solution)/shard_map/all_to_all | solution.py:18
  150.1 0.7 copy-start.8
  150.1 1.6 copy-start.1
Sparse Core Ops, SparseCore 0:
  69.0 72.6 all-gather.2

commit v6 on v4

--- a/solution.py
+++ b/solution.py
@@ -1,6 +1,9 @@
+import functools
+
 import jax
 import jax.numpy as jnp
 from jax import lax
+from jax.experimental import pallas as pl
 from jax.sharding import PartitionSpec as P
 
 learn_rate = 0.5
@@ -21,6 +24,44 @@
     spread = jnp.broadcast_to(mine[None], parts.shape)
     full = lax.all_to_all(spread, "rep", 0, 0, tiled=True)
     return full.reshape(rows, -1).astype(jnp.float32)
+
+
+def pick_kernel(feats, t_ref, f_ref, p_ref, o_ref):
+    tile = t_ref.shape[0]
+    samples = p_ref.shape[0]
+    width = o_ref.shape[1]
+    sample_ids = lax.broadcasted_iota(jnp.int32, (tile, samples), 1)
+    onehot = (t_ref[...] == sample_ids).astype(jnp.bfloat16)
+    f_ids = f_ref[...]
+    acc = jnp.zeros((tile, width), jnp.float32)
+    for f in range(feats):
+        block = p_ref[:, f * width:(f + 1) * width]
+        part = jnp.dot(onehot, block, preferred_element_type=jnp.float32)
+        acc = jnp.where(f_ids == f, part, acc)
+    o_ref[...] = acc.astype(o_ref.dtype)
+
+
+def pick_rows(pooled_cols, t_ids, f_ids, feats, tile=512):
+    samples, cols = pooled_cols.shape
+    width = cols // feats
+    slots = t_ids.shape[0]
+    cost = pl.CostEstimate(
+        flops=2 * slots * samples * cols,
+        transcendentals=0,
+        bytes_accessed=samples * cols * 2 + slots * 8 + slots * width * 2,
+    )
+    return pl.pallas_call(
+        functools.partial(pick_kernel, feats),
+        grid=(slots // tile,),
+        in_specs=[
+            pl.BlockSpec((tile, 1), lambda i: (i, 0)),
+            pl.BlockSpec((tile, 1), lambda i: (i, 0)),
+            pl.BlockSpec((samples, cols), lambda i: (0, 0)),
+        ],
+        out_specs=pl.BlockSpec((tile, width), lambda i: (i, 0)),
+        out_shape=jax.ShapeDtypeStruct((slots, width), jnp.bfloat16),
+        cost_estimate=cost,
+    )(t_ids, f_ids, pooled_cols)
 
 
 def pack_grads(weight_part, bias_part, devices):
@@ -66,15 +107,15 @@
     )
     input_grad = cot_f * linear + backprop + cot_f
     dense_grad = input_grad[:, :width].astype(jnp.bfloat16)
-    pooled = input_grad[:, width:].astype(jnp.bfloat16).reshape(-1, width)
+    pooled_cols = input_grad[:, width:].astype(jnp.bfloat16)
+    feats = pooled_cols.shape[1] // width
     bag_ids = send_bags[0]
     shard_count = bag_ids.shape[0]
     slot_total = bag_ids.shape[1]
     live_mask = jnp.arange(slot_total, dtype=jnp.int32)[None, :] < slot_counts[0][:, None]
-    flat_bags = jnp.where(live_mask, bag_ids, -1).reshape(-1)
-    bag_range = jnp.arange(pooled.shape[0], dtype=jnp.int32)
-    pick = (flat_bags[:, None] == bag_range[None, :]).astype(jnp.bfloat16)
-    picked = jnp.dot(pick, pooled, preferred_element_type=jnp.float32).astype(jnp.bfloat16)
+    t_ids = jnp.where(live_mask, bag_ids // feats, -1).reshape(-1, 1)
+    f_ids = (bag_ids % feats).reshape(-1, 1)
+    picked = pick_rows(pooled_cols, t_ids, f_ids, feats)
     outgoing = picked.reshape(shard_count, slot_total, width)
 
     got_w, outgoing = lax.optimization_barrier((got_w, outgoing))

time: 159 us -> 173 us (1.088)
  Pallas kernels: 0 us -> 21.1 us
  matrix products: 49 us -> 29.2 us
  local copies, waits for them, and re-layouts: 13.9 us -> 23.2 us
  other arithmetic: 12.8 us -> 16.8 us
  waiting for transfers between devices: 35 us -> 31.5 us
  starting transfers between devices: 20.3 us -> 22.6 us
    dot_general x1 -> x0, matrix products: 23.1 us -> none  [per_device(): jnp.dot(pick, pooled, preferred_element_type=jnp.float32)]
    pallas_call x0 -> x1, Pallas kernels: none -> 21.1 us  [pick_rows(): pl.pallas_call(functools.partial(pick_kernel, feats), grid=(slots // tile...]
    unnamed x28 -> x43, local copies, waits for them, and re-layouts: 7.83 us -> 17.9 us
    select_n x1, other arithmetic: 0.01 us -> 5.48 us  [per_device(): f_ids = (bag_ids % feats).reshape(-1, 1)]
    all_to_all x1, waiting for transfers between devices: 3.73 us -> 0.01 us  [per_device(): got_w = lax.all_to_all(packed, axes, 0, 0, tiled=True)]
    all_to_all x1, starting transfers between devices: 4.76 us -> 7.27 us  [per_device(): lax.all_to_all(outgoing, 'shard', split_axis=0, concat_axis=0, tiled=True)]
    dot_general x1, matrix products: 2.63 us -> 4.63 us  [per_device(): lax.dot_general(features, gated, (((0,), (0,)), ((), ())), preferred_elem...]
    reshape x1 -> x0, local copies, waits for them, and re-layouts: 1.81 us -> none  [per_device(): pooled = input_grad[:, width:].astype(jnp.bfloat16).reshape(-1, width)]
  transfers between devices with their start and end apart: 4 -> 4, of which waited for: 3 -> 2; matrix products, arithmetic and copies ran while one was open for 38% -> 30% of each run, Pallas kernels for 0% -> 12%
where the time goes in v6:
time: 173 us; the launch traced here: 172 us
  waiting for transfers between devices  31.5 us (18%)
  matrix products  29.2 us (17%)
  local copies, waits for them, and re-layouts  23.2 us (13%)
  starting transfers between devices  22.6 us (13%)
  Pallas kernels  21.1 us (12%)
  other arithmetic  16.8 us (10%)
  between operations  14.3 us (8%)
  blocking collectives  12.9 us (7%)
    all_to_all x1, waiting for transfers between devices, per_device(): lax.all_to_all(outgoing, 'shard', split_axis=0, concat_axis=0, tiled=True)  27 us
    pallas_call x1, Pallas kernels, pick_rows(): pl.pallas_call(functools.partial(pick_kernel, feats), grid=(slots // tile...  21.1 us
    unnamed x43, local copies, waits for them, and re-layouts  17.9 us
    all_to_all x1, blocking collectives, rep_sum(): got = lax.all_to_all(parts, 'rep', 0, 0, tiled=True)  12.9 us
    all_to_all x1, starting transfers between devices, per_device(): got_w = lax.all_to_all(packed, axes, 0, 0, tiled=True)  11.6 us
    dot_general x1, matrix products, per_device(): jnp.dot(select, incoming_rows, preferred_element_type=jnp.float32)  11.3 us
    all_to_all x1, starting transfers between devices, per_device(): lax.all_to_all(outgoing, 'shard', split_axis=0, concat_axis=0, tiled=True)  7.27 us
    dot_general x1, matrix products, per_device(): spread_rows = jnp.dot(place, with_marks, preferred_element_type=jnp.float32)  6.96 us
  transfers between devices with their start and end apart: 4, of which 2 were waited for; matrix products, arithmetic and copies ran while one was open for 30% of the time, Pallas kernels for 12%

profile of v6, /device:TPU:0, one launch (start us, length us, event | category | flops | bytes accessed | tf_op | source)
XLA Modules:
  0.0 171.5 jit_solution(15035392273040880217)
XLA Ops:
  7.2 0.0 copy-start
  7.2 0.0 copy-start.5
  7.2 0.0 copy-start.7
  7.2 4.6 %convert_bitcast_fusion = bf16[128,8,1024]{2,1,0:T(8,128)(2,1)} fusion(bf16[512,1024]{1,0:T(8,128)(2,1)} %param.10, bf16[512,1024]{1,0:T(8,128)(2,1)} %param.11), kind=kOutput, calls=%fused_computation.31 | convolution fusion | flops 1076887552 | bytes 4194304 | tf_op jit(solution)/shard_map/dot_general | solution.py:98
  11.8 0.0 copy-done.5
  11.8 0.0 copy-done.7
  11.8 0.4 fusion.22
  12.3 0.4 reshape.146
  12.7 3.3 %fusion.13 = bf16[128,8,1152]{2,1,0:T(8,128)(2,1)} fusion(bf16[128,8,1]{2,1,0:T(8,128)(2,1)S(1)} %reshape.146, bf16[128,8,1024]{2,1,0:T(8,128)(2,1)} %convert_bitcast_fusion), kind=kLoop, calls=%fused_computation.22 | loop fusion | flops 7077888 | bytes 4458496 | tf_op jit(solution)/shard_map/concatenate | solution.py:71
  16.0 11.6 %all-to-all-start = ((bf16[128,8,1152]{2,1,0:T(8,128)(2,1)}), bf16[128,8,1152]{2,1,0:T(8,128)(2,1)}, u32[]{:S(2)}, u32[]{:S(2)}) async-start(bf16[128,8,1152]{2,1,0:T(8,128)(2,1)} %fusion.13), calls=%async_computation | async-start | bytes 4718592 | tf_op jit(solution)/shard_map/all_to_all | solution.py:103
  27.6 0.0 copy-done.10
  27.8 2.7 %copy.51 = s32[1,8192]{0,1:T(8,128)} copy(s32[1,8192]{1,0:T(1,128)S(1)} %bitcast.61) | data formatting | bytes 65536
  30.5 2.6 %copy.53 = s32[1,8192]{0,1:T(8,128)} copy(s32[1,8192]{1,0:T(1,128)S(1)} %bitcast.62) | data formatting | bytes 65536
  33.1 0.0 copy-done.13
  33.1 0.1 fusion.24
  33.2 1.7 %copy.47 = pred[1,8192]{0,1:T(8,128)(4,1)S(1)} copy(pred[1,8192]{1,0:T(4,128)(4,1)S(1)} %bitcast.63) | data formatting | bytes 16384
  35.0 2.2 %copy.49 = pred[1,8192]{0,1:T(8,128)(4,1)} copy(pred[1,8192]{1,0:T(4,128)(4,1)S(1)} %bitcast.64) | data formatting | bytes 16384
  37.2 0.0 copy-done
  37.2 2.6 %fusion.31 = f32[512,1024]{1,0:T(8,128)S(1)} fusion(bf16[512,1024]{1,0:T(8,128)(2,1)} %param.10, bf16[1024,1024]{1,0:T(8,128)(2,1)S(1)} %copy-done), kind=kOutput, calls=%fused_computation.50 | convolution fusion | flops 1073741824 | bytes 5242880 | tf_op jit(solution)/shard_map/dot_general | solution.py:95
  39.8 0.0 copy-done.6
  39.8 0.0 copy-done.8
  39.8 0.0 copy-done.15
  39.8 0.0 copy-start.1
  39.8 0.0 copy-start.2
  39.9 1.5 fusion.18
  41.3 0.0 copy-start.9
  41.3 0.0 copy-start.4
  41.4 1.0 slice.26.p_ref
  42.4 0.0 copy-done.1
  42.4 1.6 copy-done.2
  44.0 0.4 copy-done.4
  44.4 5.5 %add_select_fusion = (s32[8192,1]{1,0:T(8,128)}, s32[8192,1]{1,0:T(8,128)}) fusion(s32[1,8192]{0,1:T(8,128)S(1)} %copy-done.1, s32[1,8192]{0,1:T(8,128)S(1)} %copy-done.2, pred[1,8192]{0,1:T(8,128)(4,1)S(1)} %copy-done.4, pred[1,8192]{0,1:T(8,128)(4,1)S(1)} %copy.47), kind=kLoop, calls=%fused_computation.7 | loop fusion | flops 73728 | bytes 147456 | tf_op jit(solution)/shard_map/jit(remainder)/select_n | solution.py:117
  49.9 0.0 copy-done.9
  49.9 21.1 %shard_map.137 = bf16[8192,128]{1,0:T(8,128)(2,1)} custom-call(s32[8192,1]{1,0:T(8,128)} %get-tuple-element.25.t_ref, s32[8192,1]{1,0:T(8,128)} %get-tuple-element.24.f_ref, bf16[512,896]{1,0:T(8,128)(2,1)} %slice.26.p_ref), custom_call_target="tpu_custom_call" | custom-call | flops 7516192768 | bytes 3080192 | tf_op jit(solution)/shard_map/pallas_call | solution.py:53
  71.0 0.0 all-to-all-done
  71.0 0.0 copy-start.14
  71.0 7.3 %all-to-all-start.1 = ((bf16[32,256,128]{2,1,0:T(8,128)(2,1)}), bf16[32,256,128]{2,1,0:T(8,128)(2,1)}, u32[]{:S(2)}, u32[]{:S(2)}) async-start(bf16[32,256,128]{2,1,0:T(8,128)(2,1)} %bitcast.58), calls=%async_computation.1 | async-start | bytes 4194304 | tf_op jit(solution)/shard_map/all_to_all | solution.py:122
  78.3 0.2 all-gather.3.cloned.1.call-start
  78.5 2.2 %fusion.14 = bf16[1,8,1152]{2,0,1:T(2,128)(2,1)S(1)} fusion(bf16[128,8,1152]{2,1,0:T(8,128)(2,1)} %all-to-all-done), kind=kOutput, calls=%fused_computation.24 | convolution fusion | flops 2359296 | bytes 2377728 | tf_op jit(solution)/shard_map/dot_general | solution.py:124
  80.7 0.6 copy.58
  81.3 0.0 all-gather.3.cloned.1.call-update
  81.3 0.0 copy-done.11
  81.4 27.0 %all-to-all-done.1 = bf16[32,256,128]{2,1,0:T(8,128)(2,1)} async-done(((bf16[32,256,128]{2,1,0:T(8,128)(2,1)}), bf16[32,256,128]{2,1,0:T(8,128)(2,1)}, u32[]{:S(2)}, u32[]{:S(2)}) %all-to-all-start.1) | async-done | bytes 2097184 | tf_op jit(solution)/shard_map/all_to_all | solution.py:122
  108.4 0.0 copy-done.14
  108.4 11.3 %fusion.10 = bf16[2048,128]{1,0:T(8,128)(2,1)S(1)} fusion(bf16[8192,128]{1,0:T(8,128)(2,1)} %bitcast.9, s32[8192]{0:T(1024)S(1)} %bitcast.67, s32[2048]{0:T(1024)S(1)} %bitcast.69), kind=kOutput, calls=%fused_computation.21 | convolution fusion | flops 4312006656 | bytes 2662400 | tf_op jit(solution)/shard_map/dot_general | solution.py:133
  119.7 12.9 %all_to_all.20 = bf16[4,512,128]{2,1,0:T(8,128)(2,1)S(1)} all-to-all(bf16[4,512,128]{2,1,0:T(8,128)(2,1)S(1)} %bitcast.60), channel_id=1, replica_groups=mesh['rep'=4,'shard'=32] {'rep'}, dimensions={0} | all-to-all | bytes 1048576 | tf_op jit(solution)/shard_map/all_to_all | solution.py:22
  132.6 0.1 reduce_sum.31
  132.7 0.9 broadcast_in_dim.14
  133.6 3.5 %all-to-all-start.3 = ((bf16[4,512,128]{2,1,0:T(8,128)(2,1)}), bf16[4,512,128]{2,1,0:T(8,128)(2,1)S(1)}, u32[]{:S(2)}, u32[]{:S(2)}) async-start(bf16[4,512,128]{2,1,0:T(8,128)(2,1)} %broadcast_in_dim.14), calls=%async_computation.3 | async-start | bytes 1048576 | tf_op jit(solution)/shard_map/all_to_all | solution.py:25
  137.0 1.6 slice.29
  138.7 2.9 %copy.40 = f32[4096,128]{0,1:T(8,128)} copy(f32[4096,128]{1,0:T(8,128)} %param.14) | data formatting | bytes 4194304 | tf_op args[4]
  141.6 4.4 %all-to-all-done.3 = bf16[4,512,128]{2,1,0:T(8,128)(2,1)S(1)} async-done(((bf16[4,512,128]{2,1,0:T(8,128)(2,1)}), bf16[4,512,128]{2,1,0:T(8,128)(2,1)S(1)}, u32[]{:S(2)}, u32[]{:S(2)}) %all-to-all-start.3) | async-done | bytes 524320 | tf_op jit(solution)/shard_map/all_to_all | solution.py:25
  146.0 7.0 %fusion.4 = f32[4096,256]{0,1:T(8,128)S(1)} fusion(s32[2048]{0:T(1024)S(1)} %bitcast.70, bf16[2048,128]{1,0:T(8,128)(2,1)S(1)} %bitcast.59), kind=kOutput, calls=%fused_computation.5 | convolution fusion | flops 4303355904 | bytes 4726784 | tf_op jit(solution)/shard_map/dot_general | solution.py:138
  153.0 0.0 copy-start.3
  153.0 0.1 compare_reduce_fusion
  153.0 0.2 multiply_reduce_fusion
  153.2 0.6 fusion.26
  153.8 0.7 copy-done.3
  154.6 1.8 %subtract_select_fusion = f32[4096,128]{0,1:T(8,128)} fusion(f32[4096,128]{0,1:T(8,128)S(1)} %copy-done.3, f32[4096,256]{0,1:T(8,128)S(1)} %fusion.4, f32[4096]{0:T(1024)S(1)} %get-tuple-element.27, pred[4096]{0:T(1024)(128)(4,1)S(1)} %compare_reduce_fusion), kind=kLoop, calls=%fused_computation.29 | loop fusion | flops 2621440 | bytes 6311936 | tf_op jit(solution)/shard_map/jit(_where)/select_n | solution.py:146
  156.3 2.9 %copy.42 = f32[4096,128]{1,0:T(8,128)} copy(f32[4096,128]{0,1:T(8,128)} %subtract_select_fusion) | data formatting | bytes 4194304
  159.2 2.0 %bitcast_convert_fusion = f32[128,8,1152]{2,1,0:T(8,128)S(1)} fusion(bf16[1024,1152]{1,0:T(8,128)(2,1)} %all-gather.3.cloned.1.call-done), kind=kLoop, calls=%fused_computation.23 | loop fusion | flops 1179648 | bytes 7077888 | tf_op jit(solution)/shard_map/convert_element_type | solution.py:142
  161.2 2.6 %fusion.8 = f32[1024,1024]{1,0:T(8,128)} fusion(f32[128,8,1152]{2,1,0:T(8,128)S(1)} %bitcast_convert_fusion), kind=kLoop, calls=%fused_computation.15 | loop fusion | flops 1048576 | bytes 8388608 | tf_op jit(solution)/shard_map/mul | solution.py:143
  163.8 0.2 fusion.20
  164.0 0.7 mul.46
  (16 shorter events, 0.2 us)
Async XLA Ops:
  7.2 30.0 %copy-start = (bf16[1024,1024]{1,0:T(8,128)(2,1)S(1)}, bf16[1024,1024]{1,0:T(8,128)(2,1)}, u32[]{:S(2)}) copy-start(bf16[1024,1024]{1,0:T(8,128)(2,1)} %param.12) | copy-start | bytes 6291460
  7.2 4.7 %copy-start.5 = (bf16[512,1024]{1,0:T(8,128)(2,1)S(1)}, bf16[512,1024]{1,0:T(8,128)(2,1)}, u32[]{:S(2)}) copy-start(bf16[512,1024]{1,0:T(8,128)(2,1)} %param.10) | copy-start | bytes 3145732
  7.2 4.7 %copy-start.7 = (bf16[512,1024]{1,0:T(8,128)(2,1)S(1)}, bf16[512,1024]{1,0:T(8,128)(2,1)}, u32[]{:S(2)}) copy-start(bf16[512,1024]{1,0:T(8,128)(2,1)} %param.11) | copy-start | bytes 3145732
  16.0 11.6 %copy-start.10 = (s32[1,32,256]{2,1,0:T(8,128)S(1)}, s32[1,32,256]{2,1,0:T(8,128)}, u32[]{:S(2)}) copy-start(s32[1,32,256]{2,1,0:T(8,128)} %param.16) | copy-start | bytes 98308
  16.0 55.0 %all-to-all-start = ((bf16[128,8,1152]{2,1,0:T(8,128)(2,1)}), bf16[128,8,1152]{2,1,0:T(8,128)(2,1)}, u32[]{:S(2)}, u32[]{:S(2)}) async-start(bf16[128,8,1152]{2,1,0:T(8,128)(2,1)} %fusion.13), calls=%async_computation | async-start | bytes 4718592 | tf_op jit(solution)/shard_map/all_to_all | solution.py:103
  30.4 2.7 %copy-start.13 = (s32[1,32]{1,0:T(1,128)S(1)}, s32[1,32]{1,0:T(1,128)}, u32[]{:S(2)}) copy-start(s32[1,32]{1,0:T(1,128)} %param.17) | copy-start | bytes 388
  37.2 2.6 %copy-start.6 = (bf16[512,1024]{1,0:T(8,128)(2,1)S(1)}, bf16[512,1024]{1,0:T(8,128)(2,1)}, u32[]{:S(2)}) copy-start(bf16[512,1024]{1,0:T(8,128)(2,1)} %param.10) | copy-start | bytes 3145732
  37.2 2.6 %copy-start.8 = (bf16[512,1024]{1,0:T(8,128)(2,1)S(1)}, bf16[512,1024]{1,0:T(8,128)(2,1)}, u32[]{:S(2)}) copy-start(bf16[512,1024]{1,0:T(8,128)(2,1)} %param.11) | copy-start | bytes 3145732
  37.2 2.7 %copy-start.15 = (f32[1024]{0:T(1024)S(1)}, f32[1024]{0:T(1024)}, u32[]{:S(2)}) copy-start(f32[1024]{0:T(1024)} %param.13) | copy-start | bytes 12292
  39.8 2.5 %copy-start.1 = (s32[1,8192]{0,1:T(8,128)S(1)}, s32[1,8192]{0,1:T(8,128)}, u32[]{:S(2)}) copy-start(s32[1,8192]{0,1:T(8,128)} %copy.51) | copy-start | bytes 98308
  39.8 4.2 %copy-start.2 = (s32[1,8192]{0,1:T(8,128)S(1)}, s32[1,8192]{0,1:T(8,128)}, u32[]{:S(2)}) copy-start(s32[1,8192]{0,1:T(8,128)} %copy.53) | copy-start | bytes 98308
  41.3 8.5 %copy-start.9 = (bf16[512,1024]{1,0:T(8,128)(2,1)}, bf16[512,1024]{1,0:T(8,128)(2,1)S(1)}, u32[]{:S(2)}) copy-start(bf16[512,1024]{1,0:T(8,128)(2,1)S(1)} %fusion.18) | copy-start | bytes 3145732
  41.3 3.0 %copy-start.4 = (pred[1,8192]{0,1:T(8,128)(4,1)S(1)}, pred[1,8192]{0,1:T(8,128)(4,1)}, u32[]{:S(2)}) copy-start(pred[1,8192]{0,1:T(8,128)(4,1)} %copy.49) | copy-start | bytes 24580
  71.0 10.3 %copy-start.11 = (s32[1,32,256]{2,1,0:T(8,128)S(1)}, s32[1,32,256]{2,1,0:T(8,128)}, u32[]{:S(2)}) copy-start(s32[1,32,256]{2,1,0:T(8,128)} %param.18) | copy-start | bytes 98308
  71.0 37.4 %copy-start.14 = (s32[1,2048]{1,0:T(1,128)S(1)}, s32[1,2048]{1,0:T(1,128)}, u32[]{:S(2)}) copy-start(s32[1,2048]{1,0:T(1,128)} %param.19) | copy-start | bytes 24580
  71.0 37.4 %all-to-all-start.1 = ((bf16[32,256,128]{2,1,0:T(8,128)(2,1)}), bf16[32,256,128]{2,1,0:T(8,128)(2,1)}, u32[]{:S(2)}, u32[]{:S(2)}) async-start(bf16[32,256,128]{2,1,0:T(8,128)(2,1)} %bitcast.58), calls=%async_computation.1 | async-start | bytes 4194304 | tf_op jit(solution)/shard_map/all_to_all | solution.py:122
  78.3 80.9 %all-gather.3.cloned.1.call-start = ((), (), s32[]{:S(2)}) async-start(), calls=%async_computation.4 | async-start | bytes 2377728 | tf_op jit(solution)/shard_map/all_gather | solution.py:127
  133.6 12.4 %all-to-all-start.3 = ((bf16[4,512,128]{2,1,0:T(8,128)(2,1)}), bf16[4,512,128]{2,1,0:T(8,128)(2,1)S(1)}, u32[]{:S(2)}, u32[]{:S(2)}) async-start(bf16[4,512,128]{2,1,0:T(8,128)(2,1)} %broadcast_in_dim.14), calls=%async_computation.3 | async-start | bytes 1048576 | tf_op jit(solution)/shard_map/all_to_all | solution.py:25
  146.0 7.2 %copy-start.12 = (f32[4096]{0:T(1024)S(1)}, f32[4096]{0:T(1024)}, u32[]{:S(2)}) copy-start(f32[4096]{0:T(1024)} %param.15) | copy-start | bytes 49156
  153.0 1.6 copy-start.3
Sparse Core Ops, SparseCore 0:
  82.1 71.7 all-gather.2

commit v7 on v4

--- a/solution.py
+++ b/solution.py
@@ -83,7 +83,7 @@
     mine_w = lax.dot_general(
         ones, got_w, (((0,), (0,)), ((), ())), preferred_element_type=jnp.float32
     ).astype(jnp.bfloat16)
-    full_w = lax.all_gather(mine_w, axes, axis=0, tiled=False)
+    full_w = lax.all_gather(mine_w, axes, axis=0, tiled=True)
 
     incoming_rows = incoming.reshape(-1, width)
     slot_rows = recv_rows[0].reshape(-1)
@@ -98,9 +98,8 @@
     row_grads = spread_rows[:, :width]
     marks = spread_rows[:, width] > 0.5
 
-    full_w = full_w.astype(jnp.float32).reshape(devices, -1, dim + 128)
-    weight_grad = full_w[:, :, :dim].reshape(dim, dim) * scale
-    bias_grad = full_w[:, :, dim].reshape(dim) * scale
+    weight_grad = full_w[:, :dim].astype(jnp.float32) * scale
+    bias_grad = full_w[:, dim].astype(jnp.float32) * scale
     upd_table, upd_accum = adagrad_rows(emb_table, row_accum, row_grads)
     new_table = jnp.where(marks[:, None], upd_table, emb_table)
     new_accum = jnp.where(marks, upd_accum, row_accum)

time: 159 us -> 160 us (level)
  matrix products: 49 us -> 51 us
    mul x2, other arithmetic: 2.81 us -> 5.95 us  [the longest x1 4.2 us: per_device(): weight_grad = full_w[:, :dim].astype(jnp.float32) * scale]
    dot_general x1, matrix products: 2.63 us -> 4.64 us  [per_device(): lax.dot_general(features, gated, (((0,), (0,)), ((), ())), preferred_elem...]
    convert_element_type x1 -> x0, other arithmetic: 1.97 us -> none  [per_device(): full_w = full_w.astype(jnp.float32).reshape(devices, -1, dim + 128)]
    reduce_sum x1, other arithmetic: 2.05 us -> 0.42 us  [per_device(): bias_part = jnp.sum(gated.astype(jnp.float32), axis=0)]
where the time goes in v7:
time: 160 us; the launch traced here: 157 us
  matrix products  51 us (32%)
  waiting for transfers between devices  35.1 us (22%)
  starting transfers between devices  20.3 us (13%)
  between operations  14.3 us (9%)
  local copies, waits for them, and re-layouts  13 us (8%)
  other arithmetic  12.4 us (8%)
  blocking collectives  11.3 us (7%)
    all_to_all x1, waiting for transfers between devices, per_device(): lax.all_to_all(outgoing, 'shard', split_axis=0, concat_axis=0, tiled=True)  27 us
    dot_general x1, matrix products, per_device(): jnp.dot(pick, pooled, preferred_element_type=jnp.float32)  23.1 us
    all_to_all x1, starting transfers between devices, per_device(): got_w = lax.all_to_all(packed, axes, 0, 0, tiled=True)  11.8 us
    dot_general x1, matrix products, per_device(): jnp.dot(select, incoming_rows, preferred_element_type=jnp.float32)  11.3 us
    all_to_all x1, blocking collectives, rep_sum(): got = lax.all_to_all(parts, 'rep', 0, 0, tiled=True)  11.3 us
    unnamed x28, local copies, waits for them, and re-layouts  7.59 us
    dot_general x1, matrix products, per_device(): spread_rows = jnp.dot(place, with_marks, preferred_element_type=jnp.float32)  6.96 us
    all_to_all x1, starting transfers between devices, per_device(): lax.all_to_all(outgoing, 'shard', split_axis=0, concat_axis=0, tiled=True)  4.76 us
  transfers between devices with their start and end apart: 4, of which 3 were waited for; matrix products, arithmetic and copies ran while one was open for 38% of the time, Pallas kernels for 0%

profile of v7, /device:TPU:0, one launch (start us, length us, event | category | flops | bytes accessed | tf_op | source)
XLA Modules:
  0.0 157.3 jit_solution(9641062284247347073)
XLA Ops:
  7.2 0.0 copy-start
  7.2 0.0 copy-start.2
  7.2 0.0 copy-start.3
  7.2 4.6 %convert_bitcast_fusion = bf16[128,8,1024]{2,1,0:T(8,128)(2,1)} fusion(bf16[512,1024]{1,0:T(8,128)(2,1)} %param.10, bf16[512,1024]{1,0:T(8,128)(2,1)} %param.11), kind=kOutput, calls=%fused_computation.26 | convolution fusion | flops 1076887552 | bytes 4194304 | tf_op jit(solution)/shard_map/dot_general | solution.py:57
  11.8 0.0 copy-done.2
  11.8 0.0 copy-done.3
  11.8 0.4 fusion.21
  12.3 0.4 reshape.72
  12.7 3.2 %fusion.13 = bf16[128,8,1152]{2,1,0:T(8,128)(2,1)} fusion(bf16[128,8,1]{2,1,0:T(8,128)(2,1)S(1)} %reshape.72, bf16[128,8,1024]{2,1,0:T(8,128)(2,1)} %convert_bitcast_fusion), kind=kLoop, calls=%fused_computation.18 | loop fusion | flops 7077888 | bytes 4458496 | tf_op jit(solution)/shard_map/concatenate | solution.py:30
  15.9 11.8 %all-to-all-start = ((bf16[128,8,1152]{2,1,0:T(8,128)(2,1)}), bf16[128,8,1152]{2,1,0:T(8,128)(2,1)}, u32[]{:S(2)}, u32[]{:S(2)}) async-start(bf16[128,8,1152]{2,1,0:T(8,128)(2,1)} %fusion.13), calls=%async_computation | async-start | bytes 4718592 | tf_op jit(solution)/shard_map/all_to_all | solution.py:62
  27.7 0.0 copy-done
  27.8 0.0 copy-start.4
  27.8 0.0 copy-start.11
  27.8 1.3 fusion.28
  29.0 0.0 copy-done.4
  29.0 0.0 copy-done.11
  29.1 1.5 fusion.18
  30.6 0.0 copy-start.5
  30.6 1.0 copy-done.5
  31.6 0.0 copy-start.6
  31.6 0.0 copy-start.9
  31.6 0.1 slice.26
  31.7 1.8 %reshape.65 = bf16[3584,128]{1,0:T(8,128)(2,1)} reshape(bf16[512,896]{1,0:T(8,128)(2,1)S(1)} %slice.26) | data formatting | bytes 1835008 | tf_op jit(solution)/shard_map/reshape | solution.py:69
  33.5 0.0 copy-done.6
  33.5 0.0 copy-done.9
  33.5 0.1 iota_compare_fusion.7
  33.6 23.1 %fusion.8 = bf16[8192,128]{1,0:T(8,128)(2,1)} fusion(bf16[3584,128]{1,0:T(8,128)(2,1)} %reshape.65, s32[8192]{0:T(1024)S(1)} %broadcast_select_fusion), kind=kOutput, calls=%fused_computation.10 | convolution fusion | flops 7546601472 | bytes 3047424 | tf_op jit(solution)/shard_map/dot_general | solution.py:77
  56.7 3.7 %all-to-all-done = bf16[128,8,1152]{2,1,0:T(8,128)(2,1)} async-done(((bf16[128,8,1152]{2,1,0:T(8,128)(2,1)}), bf16[128,8,1152]{2,1,0:T(8,128)(2,1)}, u32[]{:S(2)}, u32[]{:S(2)}) %all-to-all-start) | async-done | bytes 2359328 | tf_op jit(solution)/shard_map/all_to_all | solution.py:62
  60.4 4.8 %all-to-all-start.1 = ((bf16[32,256,128]{2,1,0:T(8,128)(2,1)}), bf16[32,256,128]{2,1,0:T(8,128)(2,1)}, u32[]{:S(2)}, u32[]{:S(2)}) async-start(bf16[32,256,128]{2,1,0:T(8,128)(2,1)} %bitcast.23), calls=%async_computation.1 | async-start | bytes 4194304 | tf_op jit(solution)/shard_map/all_to_all | solution.py:81
  65.2 0.0 copy-start.7
  65.2 0.0 copy-start.10
  65.2 0.3 all-gather.2.cloned.1.call-start
  65.5 2.2 %fusion.14 = bf16[1,8,1152]{2,0,1:T(2,128)(2,1)S(1)} fusion(bf16[128,8,1152]{2,1,0:T(8,128)(2,1)} %all-to-all-done), kind=kOutput, calls=%fused_computation.19 | convolution fusion | flops 2359296 | bytes 2377728 | tf_op jit(solution)/shard_map/dot_general | solution.py:83
  67.7 0.6 copy.30
  68.3 0.0 all-gather.2.cloned.1.call-update
  68.3 0.0 copy-done.7
  68.3 27.0 %all-to-all-done.1 = bf16[32,256,128]{2,1,0:T(8,128)(2,1)} async-done(((bf16[32,256,128]{2,1,0:T(8,128)(2,1)}), bf16[32,256,128]{2,1,0:T(8,128)(2,1)}, u32[]{:S(2)}, u32[]{:S(2)}) %all-to-all-start.1) | async-done | bytes 2097184 | tf_op jit(solution)/shard_map/all_to_all | solution.py:81
  95.3 0.0 copy-done.10
  95.3 11.3 %fusion.10 = bf16[2048,128]{1,0:T(8,128)(2,1)S(1)} fusion(bf16[8192,128]{1,0:T(8,128)(2,1)} %bitcast.6, s32[8192]{0:T(1024)S(1)} %bitcast.30, s32[2048]{0:T(1024)S(1)} %bitcast.32), kind=kOutput, calls=%fused_computation.17 | convolution fusion | flops 4312006656 | bytes 2662400 | tf_op jit(solution)/shard_map/dot_general | solution.py:92
  106.7 11.3 %all_to_all.20 = bf16[4,512,128]{2,1,0:T(8,128)(2,1)S(1)} all-to-all(bf16[4,512,128]{2,1,0:T(8,128)(2,1)S(1)} %bitcast.25), channel_id=1, replica_groups=mesh['rep'=4,'shard'=32] {'rep'}, dimensions={0} | all-to-all | bytes 1048576 | tf_op jit(solution)/shard_map/all_to_all | solution.py:19
  118.0 0.1 reduce_sum.31
  118.1 0.9 broadcast_in_dim.32
  118.9 3.5 %all-to-all-start.3 = ((bf16[4,512,128]{2,1,0:T(8,128)(2,1)}), bf16[4,512,128]{2,1,0:T(8,128)(2,1)S(1)}, u32[]{:S(2)}, u32[]{:S(2)}) async-start(bf16[4,512,128]{2,1,0:T(8,128)(2,1)} %broadcast_in_dim.32), calls=%async_computation.3 | async-start | bytes 1048576 | tf_op jit(solution)/shard_map/all_to_all | solution.py:22
  122.4 1.6 %slice.29 = bf16[512,128]{1,0:T(8,128)(2,1)} slice(bf16[512,1024]{1,0:T(8,128)(2,1)} %copy-done.5), slice={[0:512], [0:128]} | slice | bytes 262144 | tf_op jit(solution)/shard_map/slice | solution.py:68
  124.0 2.9 %copy.19 = f32[4096,128]{0,1:T(8,128)} copy(f32[4096,128]{1,0:T(8,128)} %param.14) | data formatting | bytes 4194304 | tf_op args[4]
  126.9 4.3 %all-to-all-done.3 = bf16[4,512,128]{2,1,0:T(8,128)(2,1)S(1)} async-done(((bf16[4,512,128]{2,1,0:T(8,128)(2,1)}), bf16[4,512,128]{2,1,0:T(8,128)(2,1)S(1)}, u32[]{:S(2)}, u32[]{:S(2)}) %all-to-all-start.3) | async-done | bytes 524320 | tf_op jit(solution)/shard_map/all_to_all | solution.py:22
  131.2 7.0 %fusion.6 = f32[4096,256]{0,1:T(8,128)S(1)} fusion(s32[2048]{0:T(1024)S(1)} %bitcast.33, bf16[2048,128]{1,0:T(8,128)(2,1)S(1)} %bitcast.24), kind=kOutput, calls=%fused_computation.8 | convolution fusion | flops 4303355904 | bytes 4726784 | tf_op jit(solution)/shard_map/dot_general | solution.py:97
  138.2 0.0 copy-start.8
  138.2 0.0 copy-start.1
  138.2 0.1 compare_reduce_fusion
  138.3 0.2 multiply_reduce_fusion
  138.5 0.5 copy-done.8
  138.9 0.6 fusion.23
  139.5 0.3 copy-done.1
  139.8 1.8 %subtract_select_fusion = f32[4096,128]{0,1:T(8,128)} fusion(f32[4096,128]{0,1:T(8,128)S(1)} %copy-done.1, f32[4096,256]{0,1:T(8,128)S(1)} %fusion.6, f32[4096]{0:T(1024)S(1)} %get-tuple-element.20, pred[4096]{0:T(1024)(128)(4,1)S(1)} %compare_reduce_fusion), kind=kLoop, calls=%fused_computation.24 | loop fusion | flops 2621440 | bytes 6311936 | tf_op jit(solution)/shard_map/jit(_where)/select_n | solution.py:104
  141.6 2.9 %copy.21 = f32[4096,128]{1,0:T(8,128)} copy(f32[4096,128]{0,1:T(8,128)} %subtract_select_fusion) | data formatting | bytes 4194304
  144.5 0.0 all-gather.2.cloned.1.call-done
  144.5 4.2 %convert_multiply_fusion = f32[1024,1024]{1,0:T(8,128)} fusion(bf16[1024,1152]{1,0:T(8,128)(2,1)} %all-gather.2.cloned.1.call-done), kind=kLoop, calls=%fused_computation.13 | loop fusion | flops 2097152 | bytes 6291456 | tf_op jit(solution)/shard_map/mul | solution.py:101
  148.7 1.8 %multiply_reduce_fusion.1 = f32[1024]{0:T(1024)} fusion(bf16[1024,1152]{1,0:T(8,128)(2,1)} %all-gather.2.cloned.1.call-done), kind=kLoop, calls=%fused_computation.28 | loop fusion | flops 2048 | bytes 6144 | tf_op jit(solution)/shard_map/mul | solution.py:102
  (4 shorter events, 0.1 us)
Async XLA Ops:
  7.2 20.6 %copy-start = (bf16[1024,1024]{1,0:T(8,128)(2,1)S(1)}, bf16[1024,1024]{1,0:T(8,128)(2,1)}, u32[]{:S(2)}) copy-start(bf16[1024,1024]{1,0:T(8,128)(2,1)} %param.12) | copy-start | bytes 6291460
  7.2 4.7 %copy-start.2 = (bf16[512,1024]{1,0:T(8,128)(2,1)S(1)}, bf16[512,1024]{1,0:T(8,128)(2,1)}, u32[]{:S(2)}) copy-start(bf16[512,1024]{1,0:T(8,128)(2,1)} %param.10) | copy-start | bytes 3145732
  7.2 4.7 %copy-start.3 = (bf16[512,1024]{1,0:T(8,128)(2,1)S(1)}, bf16[512,1024]{1,0:T(8,128)(2,1)}, u32[]{:S(2)}) copy-start(bf16[512,1024]{1,0:T(8,128)(2,1)} %param.11) | copy-start | bytes 3145732
  15.9 44.5 %all-to-all-start = ((bf16[128,8,1152]{2,1,0:T(8,128)(2,1)}), bf16[128,8,1152]{2,1,0:T(8,128)(2,1)}, u32[]{:S(2)}, u32[]{:S(2)}) async-start(bf16[128,8,1152]{2,1,0:T(8,128)(2,1)} %fusion.13), calls=%async_computation | async-start | bytes 4718592 | tf_op jit(solution)/shard_map/all_to_all | solution.py:62
  27.8 1.3 copy-start.4
  27.8 1.3 copy-start.11
  30.6 1.0 copy-start.5
  31.6 1.9 %copy-start.6 = (s32[1,32,256]{2,1,0:T(8,128)S(1)}, s32[1,32,256]{2,1,0:T(8,128)}, u32[]{:S(2)}) copy-start(s32[1,32,256]{2,1,0:T(8,128)} %param.16) | copy-start | bytes 98308
  31.6 1.9 %copy-start.9 = (s32[1,32]{1,0:T(1,128)S(1)}, s32[1,32]{1,0:T(1,128)}, u32[]{:S(2)}) copy-start(s32[1,32]{1,0:T(1,128)} %param.17) | copy-start | bytes 388
  60.4 34.9 %all-to-all-start.1 = ((bf16[32,256,128]{2,1,0:T(8,128)(2,1)}), bf16[32,256,128]{2,1,0:T(8,128)(2,1)}, u32[]{:S(2)}, u32[]{:S(2)}) async-start(bf16[32,256,128]{2,1,0:T(8,128)(2,1)} %bitcast.23), calls=%async_computation.1 | async-start | bytes 4194304 | tf_op jit(solution)/shard_map/all_to_all | solution.py:81
  65.2 3.1 %copy-start.7 = (s32[1,32,256]{2,1,0:T(8,128)S(1)}, s32[1,32,256]{2,1,0:T(8,128)}, u32[]{:S(2)}) copy-start(s32[1,32,256]{2,1,0:T(8,128)} %param.18) | copy-start | bytes 98308
  65.2 30.1 %copy-start.10 = (s32[1,2048]{1,0:T(1,128)S(1)}, s32[1,2048]{1,0:T(1,128)}, u32[]{:S(2)}) copy-start(s32[1,2048]{1,0:T(1,128)} %param.19) | copy-start | bytes 24580
  65.2 79.3 %all-gather.2.cloned.1.call-start = ((), (), s32[]{:S(2)}) async-start(), calls=%async_computation.4 | async-start | bytes 2377728 | tf_op jit(solution)/shard_map/all_gather | solution.py:86
  118.9 12.3 %all-to-all-start.3 = ((bf16[4,512,128]{2,1,0:T(8,128)(2,1)}), bf16[4,512,128]{2,1,0:T(8,128)(2,1)S(1)}, u32[]{:S(2)}, u32[]{:S(2)}) async-start(bf16[4,512,128]{2,1,0:T(8,128)(2,1)} %broadcast_in_dim.32), calls=%async_computation.3 | async-start | bytes 1048576 | tf_op jit(solution)/shard_map/all_to_all | solution.py:22
  138.2 0.7 copy-start.8
  138.2 1.6 %copy-start.1 = (f32[4096,128]{0,1:T(8,128)S(1)}, f32[4096,128]{0,1:T(8,128)}, u32[]{:S(2)}) copy-start(f32[4096,128]{0,1:T(8,128)} %copy.19) | copy-start | bytes 6291460
Sparse Core Ops, SparseCore 0:
  69.0 70.4 all-gather.1

commit v8 on v7

--- a/solution.py
+++ b/solution.py
@@ -23,14 +23,6 @@
     return full.reshape(rows, -1).astype(jnp.float32)
 
 
-def pack_grads(weight_part, bias_part, devices):
-    dim = weight_part.shape[0]
-    block = dim // devices
-    bias_cols = jnp.pad(bias_part.reshape(devices, block, 1), ((0, 0), (0, 0), (0, 127)))
-    packed = jnp.concatenate([weight_part.reshape(devices, block, dim), bias_cols], axis=2)
-    return packed.astype(jnp.bfloat16)
-
-
 def per_device(
     features,
     cotangent,
@@ -54,11 +46,14 @@
     linear = jnp.dot(features, cross_weight, preferred_element_type=jnp.float32) + cross_bias
     cot_f = cotangent.astype(jnp.float32)
     gated = (cot_f * features.astype(jnp.float32)).astype(jnp.bfloat16)
-    weight_part = lax.dot_general(
-        features, gated, (((0,), (0,)), ((), ())), preferred_element_type=jnp.float32
+    lanes = 128
+    feats_ones = jnp.concatenate(
+        [features, jnp.ones((features.shape[0], lanes), jnp.bfloat16)], axis=1
     )
-    bias_part = jnp.sum(gated.astype(jnp.float32), axis=0)
-    packed = pack_grads(weight_part, bias_part, devices)
+    terms_t = lax.dot_general(
+        gated, feats_ones, (((0,), (0,)), ((), ())), preferred_element_type=jnp.float32
+    )
+    packed = terms_t.astype(jnp.bfloat16).reshape(devices, dim // devices, dim + lanes)
     got_w = lax.all_to_all(packed, axes, 0, 0, tiled=True)
 
     backprop = lax.dot_general(
@@ -85,20 +80,21 @@
     ).astype(jnp.bfloat16)
     full_w = lax.all_gather(mine_w, axes, axis=0, tiled=True)
 
+    row_range = jnp.arange(shard_rows, dtype=jnp.int32)
+    place = (row_range[:, None] == touched_rows[0][None, :]).astype(jnp.bfloat16)
+    place, incoming = lax.optimization_barrier((place, incoming))
     incoming_rows = incoming.reshape(-1, width)
     slot_rows = recv_rows[0].reshape(-1)
     touched = touched_rows[0]
     select = (touched[:, None] == slot_rows[None, :]).astype(jnp.bfloat16)
     local_sums = jnp.dot(select, incoming_rows, preferred_element_type=jnp.float32)
     touched_grads = rep_sum(local_sums, rep).astype(jnp.bfloat16)
-    row_range = jnp.arange(shard_rows, dtype=jnp.int32)
-    place = (row_range[:, None] == touched[None, :]).astype(jnp.bfloat16)
     with_marks = jnp.concatenate([touched_grads, jnp.ones_like(touched_grads)], axis=1)
     spread_rows = jnp.dot(place, with_marks, preferred_element_type=jnp.float32)
     row_grads = spread_rows[:, :width]
     marks = spread_rows[:, width] > 0.5
 
-    weight_grad = full_w[:, :dim].astype(jnp.float32) * scale
+    weight_grad = full_w[:, :dim].T.astype(jnp.float32) * scale
     bias_grad = full_w[:, dim].astype(jnp.float32) * scale
     upd_table, upd_accum = adagrad_rows(emb_table, row_accum, row_grads)
     new_table = jnp.where(marks[:, None], upd_table, emb_table)

time: 160 us -> 166 us (1.038); the launches traced: 157 us -> 165 us
  waiting for transfers between devices: 35.1 us -> 24.2 us
  other arithmetic: 12.4 us -> 23 us
  local copies, waits for them, and re-layouts: 13 us -> 17.1 us
  matrix products: 51 us -> 54.9 us
    all_to_all x1, waiting for transfers between devices: 27 us -> 16.9 us  [per_device(): lax.all_to_all(outgoing, 'shard', split_axis=0, concat_axis=0, tiled=True)]
    convert_element_type x0 -> x1, other arithmetic: none -> 10 us  [per_device(): (row_range[:, None] == touched_rows[0][None, :]).astype(jnp.bfloat16)]
    unnamed x28 -> x27, local copies, waits for them, and re-layouts: 7.59 us -> 12.2 us
    dot_general x1, matrix products: 6.96 us -> 10.4 us  [per_device(): spread_rows = jnp.dot(place, with_marks, preferred_element_type=jnp.float32)]
    concatenate x1 -> x0, other arithmetic: 3.21 us -> none  [pack_grads(): jnp.concatenate([weight_part.reshape(devices, block, dim), bias_cols], ax...]
  transfers between devices with their start and end apart: 4 -> 4, of which waited for: 3 -> 3; matrix products, arithmetic and copies ran while one was open for 38% -> 47% of each run, Pallas kernels for 0% -> 0%
where the time goes in v8:
time: 166 us; the launch traced here: 165 us
  matrix products  54.9 us (33%)
  waiting for transfers between devices  24.2 us (15%)
  other arithmetic  23 us (14%)
  starting transfers between devices  20.5 us (12%)
  local copies, waits for them, and re-layouts  17.1 us (10%)
  between operations  14.2 us (9%)
  blocking collectives  11.6 us (7%)
    dot_general x1, matrix products, per_device(): jnp.dot(pick, pooled, preferred_element_type=jnp.float32)  23.1 us
    all_to_all x1, waiting for transfers between devices, per_device(): lax.all_to_all(outgoing, 'shard', split_axis=0, concat_axis=0, tiled=True)  16.9 us
    unnamed x27, local copies, waits for them, and re-layouts  12.2 us
    all_to_all x1, starting transfers between devices, per_device(): got_w = lax.all_to_all(packed, axes, 0, 0, tiled=True)  11.8 us
    all_to_all x1, blocking collectives, rep_sum(): got = lax.all_to_all(parts, 'rep', 0, 0, tiled=True)  11.6 us
    dot_general x1, matrix products, per_device(): jnp.dot(select, incoming_rows, preferred_element_type=jnp.float32)  11.4 us
    dot_general x1, matrix products, per_device(): spread_rows = jnp.dot(place, with_marks, preferred_element_type=jnp.float32)  10.4 us
    convert_element_type x1, other arithmetic, per_device(): (row_range[:, None] == touched_rows[0][None, :]).astype(jnp.bfloat16)  10 us
  transfers between devices with their start and end apart: 4, of which 3 were waited for; matrix products, arithmetic and copies ran while one was open for 47% of the time, Pallas kernels for 0%

profile of v8, /device:TPU:0, one launch (start us, length us, event | category | flops | bytes accessed | tf_op | source)
XLA Modules:
  0.0 165.5 jit_solution(10899837366319883968)
XLA Ops:
  7.2 0.0 copy-start
  7.2 5.1 %fusion.8 = bf16[128,8,1152]{2,1,0:T(8,128)(2,1)} fusion(bf16[512,1024]{1,0:T(8,128)(2,1)} %param.10, bf16[512,1024]{1,0:T(8,128)(2,1)} %param.11), kind=kOutput, calls=%fused_computation.12 | convolution fusion | flops 1211236352 | bytes 4456448 | tf_op jit(solution)/shard_map/dot_general | solution.py:53
  12.2 0.0 copy-start.8
  12.2 11.8 %all-to-all-start = ((bf16[128,8,1152]{2,1,0:T(8,128)(2,1)}), bf16[128,8,1152]{2,1,0:T(8,128)(2,1)}, u32[]{:S(2)}, u32[]{:S(2)}) async-start(bf16[128,8,1152]{2,1,0:T(8,128)(2,1)} %fusion.8), calls=%async_computation | async-start | bytes 4718592 | tf_op jit(solution)/shard_map/all_to_all | solution.py:57
  24.1 0.0 copy-done
  24.1 0.0 copy-done.8
  24.1 0.0 copy-start.9
  24.1 0.0 copy-start.10
  24.1 1.2 fusion.28
  25.4 0.0 copy-done.9
  25.4 0.0 copy-done.10
  25.4 1.5 fusion.16
  26.9 0.0 copy-start.2
  26.9 1.0 copy-done.2
  27.9 0.0 copy-start.3
  27.9 0.0 copy-start.7
  27.9 0.0 copy-start.4
  27.9 0.1 slice.26
  28.0 1.8 %reshape.59 = bf16[3584,128]{1,0:T(8,128)(2,1)} reshape(bf16[512,896]{1,0:T(8,128)(2,1)S(1)} %slice.26) | data formatting | bytes 1835008 | tf_op jit(solution)/shard_map/reshape | solution.py:64
  29.8 0.0 copy-done.3
  29.8 0.0 copy-done.7
  29.9 0.1 iota_compare_fusion.5
  30.0 0.0 copy-done.4
  30.0 23.1 %fusion.7 = bf16[8192,128]{1,0:T(8,128)(2,1)} fusion(bf16[3584,128]{1,0:T(8,128)(2,1)} %reshape.59, s32[8192]{0:T(1024)S(1)} %broadcast_select_fusion), kind=kOutput, calls=%fused_computation.9 | convolution fusion | flops 7546601472 | bytes 3047424 | tf_op jit(solution)/shard_map/dot_general | solution.py:72
  53.1 3.6 %all-to-all-done = bf16[128,8,1152]{2,1,0:T(8,128)(2,1)} async-done(((bf16[128,8,1152]{2,1,0:T(8,128)(2,1)}), bf16[128,8,1152]{2,1,0:T(8,128)(2,1)}, u32[]{:S(2)}, u32[]{:S(2)}) %all-to-all-start) | async-done | bytes 2359328 | tf_op jit(solution)/shard_map/all_to_all | solution.py:57
  56.8 0.0 copy-start.6
  56.8 4.9 %all-to-all-start.1 = ((bf16[32,256,128]{2,1,0:T(8,128)(2,1)}), bf16[32,256,128]{2,1,0:T(8,128)(2,1)}, u32[]{:S(2)}, u32[]{:S(2)}) async-start(bf16[32,256,128]{2,1,0:T(8,128)(2,1)} %bitcast.23), calls=%async_computation.1 | async-start | bytes 4194304 | tf_op jit(solution)/shard_map/all_to_all | solution.py:76
  61.7 0.3 all-gather.2.cloned.1.call-start
  61.9 0.0 copy-done.6
  62.0 10.0 %fusion.6 = bf16[4096,2048]{1,0:T(8,128)(2,1)} fusion(s32[2048]{0:T(1024)S(1)} %bitcast.31), kind=kLoop, calls=%fused_computation.8 | loop fusion | flops 16777216 | bytes 16785408 | tf_op jit(solution)/shard_map/convert_element_type | solution.py:84
  72.0 2.2 %fusion.12 = bf16[1,8,1152]{2,0,1:T(2,128)(2,1)S(1)} fusion(bf16[128,8,1152]{2,1,0:T(8,128)(2,1)} %all-to-all-done), kind=kOutput, calls=%fused_computation.17 | convolution fusion | flops 2359296 | bytes 2377728 | tf_op jit(solution)/shard_map/dot_general | solution.py:78
  74.2 0.6 copy.33
  74.8 0.0 all-gather.2.cloned.1.call-update
  74.8 16.9 %all-to-all-done.1 = bf16[32,256,128]{2,1,0:T(8,128)(2,1)} async-done(((bf16[32,256,128]{2,1,0:T(8,128)(2,1)}), bf16[32,256,128]{2,1,0:T(8,128)(2,1)}, u32[]{:S(2)}, u32[]{:S(2)}) %all-to-all-start.1) | async-done | bytes 2097184 | tf_op jit(solution)/shard_map/all_to_all | solution.py:76
  91.7 11.4 %fusion.9 = bf16[2048,128]{1,0:T(8,128)(2,1)S(1)} fusion(bf16[8192,128]{1,0:T(8,128)(2,1)} %bitcast.6, s32[8192]{0:T(1024)S(1)} %bitcast.30, s32[2048]{0:T(1024)S(1)} %bitcast.32), kind=kOutput, calls=%fused_computation.16 | convolution fusion | flops 4312006656 | bytes 2662400 | tf_op jit(solution)/shard_map/dot_general | solution.py:90
  103.1 11.6 %all_to_all.20 = bf16[4,512,128]{2,1,0:T(8,128)(2,1)S(1)} all-to-all(bf16[4,512,128]{2,1,0:T(8,128)(2,1)S(1)} %bitcast.25), channel_id=1, replica_groups=mesh['rep'=4,'shard'=32] {'rep'}, dimensions={0} | all-to-all | bytes 1048576 | tf_op jit(solution)/shard_map/all_to_all | solution.py:19
  114.7 0.1 reduce_sum.21
  114.8 0.9 broadcast_in_dim.17
  115.7 3.5 %all-to-all-start.3 = ((bf16[4,512,128]{2,1,0:T(8,128)(2,1)}), bf16[4,512,128]{2,1,0:T(8,128)(2,1)S(1)}, u32[]{:S(2)}, u32[]{:S(2)}) async-start(bf16[4,512,128]{2,1,0:T(8,128)(2,1)} %broadcast_in_dim.17), calls=%async_computation.3 | async-start | bytes 1048576 | tf_op jit(solution)/shard_map/all_to_all | solution.py:22
  119.2 1.6 slice.29
  120.7 2.9 %copy.22 = f32[4096,128]{0,1:T(8,128)} copy(f32[4096,128]{1,0:T(8,128)} %param.14) | data formatting | bytes 4194304 | tf_op args[4]
  123.6 3.6 %all-to-all-done.3 = bf16[4,512,128]{2,1,0:T(8,128)(2,1)S(1)} async-done(((bf16[4,512,128]{2,1,0:T(8,128)(2,1)}), bf16[4,512,128]{2,1,0:T(8,128)(2,1)S(1)}, u32[]{:S(2)}, u32[]{:S(2)}) %all-to-all-start.3) | async-done | bytes 524320 | tf_op jit(solution)/shard_map/all_to_all | solution.py:22
  127.2 10.4 %fusion.18 = f32[4096,256]{0,1:T(8,128)} fusion(bf16[4096,2048]{1,0:T(8,128)(2,1)} %fusion.6, bf16[2048,128]{1,0:T(8,128)(2,1)S(1)} %bitcast.24), kind=kOutput, calls=%fused_computation.25 | convolution fusion | flops 4294967296 | bytes 21495808 | tf_op jit(solution)/shard_map/dot_general | solution.py:93
  137.6 0.0 copy-start.5
  137.6 0.0 copy-start.1
  137.6 1.1 compare_reduce_fusion
  138.7 1.8 %multiply_reduce_fusion = f32[4096]{0:T(1024)S(1)} fusion(f32[4096,256]{0,1:T(8,128)} %fusion.18), kind=kLoop, calls=%fused_computation.23 | loop fusion | flops 1044480 | bytes 2113536 | tf_op jit(solution)/shard_map/reduce_sum | solution.py:11
  140.5 0.0 copy-done.5
  140.5 0.6 fusion.22
  141.1 0.0 copy-done.1
  141.2 3.4 %subtract_select_fusion = f32[4096,128]{0,1:T(8,128)} fusion(f32[4096,128]{0,1:T(8,128)S(1)} %copy-done.1, f32[4096,256]{0,1:T(8,128)} %fusion.18, f32[4096]{0:T(1024)S(1)} %get-tuple-element.29, pred[4096]{0:T(1024)(128)(4,1)S(1)} %compare_reduce_fusion), kind=kLoop, calls=%fused_computation.22 | loop fusion | flops 2621440 | bytes 6311936 | tf_op jit(solution)/shard_map/jit(_where)/select_n | solution.py:100
  144.5 2.9 %copy.25 = f32[4096,128]{1,0:T(8,128)} copy(f32[4096,128]{0,1:T(8,128)} %subtract_select_fusion) | data formatting | bytes 4194304
  147.4 0.0 all-gather.2.cloned.1.call-done
  147.4 4.1 %multiply_bitcast_fusion = f32[1024,1024]{0,1:T(8,128)} fusion(bf16[1024,1152]{1,0:T(8,128)(2,1)} %all-gather.2.cloned.1.call-done), kind=kLoop, calls=%fused_computation.10 | loop fusion | flops 2097152 | bytes 6291456 | tf_op jit(solution)/shard_map/mul | solution.py:97
  151.6 5.3 %copy.24 = f32[1024,1024]{1,0:T(8,128)} copy(f32[1024,1024]{0,1:T(8,128)} %multiply_bitcast_fusion) | data formatting | bytes 8388608
  156.9 1.8 %multiply_reduce_fusion.1 = f32[1024]{0:T(1024)} fusion(bf16[1024,1152]{1,0:T(8,128)(2,1)} %all-gather.2.cloned.1.call-done), kind=kLoop, calls=%fused_computation.27 | loop fusion | flops 2048 | bytes 6144 | tf_op jit(solution)/shard_map/mul | solution.py:98
  (4 shorter events, 0.1 us)
Async XLA Ops:
  7.2 16.9 %copy-start = (bf16[1024,1024]{1,0:T(8,128)(2,1)S(1)}, bf16[1024,1024]{1,0:T(8,128)(2,1)}, u32[]{:S(2)}) copy-start(bf16[1024,1024]{1,0:T(8,128)(2,1)} %param.12) | copy-start | bytes 6291460
  12.2 11.9 %copy-start.8 = (bf16[512,1024]{1,0:T(8,128)(2,1)S(1)}, bf16[512,1024]{1,0:T(8,128)(2,1)}, u32[]{:S(2)}) copy-start(bf16[512,1024]{1,0:T(8,128)(2,1)} %param.10) | copy-start | bytes 3145732
  12.2 44.5 %all-to-all-start = ((bf16[128,8,1152]{2,1,0:T(8,128)(2,1)}), bf16[128,8,1152]{2,1,0:T(8,128)(2,1)}, u32[]{:S(2)}, u32[]{:S(2)}) async-start(bf16[128,8,1152]{2,1,0:T(8,128)(2,1)} %fusion.8), calls=%async_computation | async-start | bytes 4718592 | tf_op jit(solution)/shard_map/all_to_all | solution.py:57
  24.1 1.3 copy-start.9
  24.1 1.3 copy-start.10
  26.9 1.0 copy-start.2
  27.9 1.9 %copy-start.3 = (s32[1,32,256]{2,1,0:T(8,128)S(1)}, s32[1,32,256]{2,1,0:T(8,128)}, u32[]{:S(2)}) copy-start(s32[1,32,256]{2,1,0:T(8,128)} %param.16) | copy-start | bytes 98308
  27.9 1.9 %copy-start.7 = (s32[1,32]{1,0:T(1,128)S(1)}, s32[1,32]{1,0:T(1,128)}, u32[]{:S(2)}) copy-start(s32[1,32]{1,0:T(1,128)} %param.17) | copy-start | bytes 388
  27.9 2.0 %copy-start.4 = (s32[1,32,256]{2,1,0:T(8,128)S(1)}, s32[1,32,256]{2,1,0:T(8,128)}, u32[]{:S(2)}) copy-start(s32[1,32,256]{2,1,0:T(8,128)} %param.18) | copy-start | bytes 98308
  56.8 5.2 %copy-start.6 = (s32[1,2048]{1,0:T(1,128)S(1)}, s32[1,2048]{1,0:T(1,128)}, u32[]{:S(2)}) copy-start(s32[1,2048]{1,0:T(1,128)} %param.19) | copy-start | bytes 24580
  56.8 35.0 %all-to-all-start.1 = ((bf16[32,256,128]{2,1,0:T(8,128)(2,1)}), bf16[32,256,128]{2,1,0:T(8,128)(2,1)}, u32[]{:S(2)}, u32[]{:S(2)}) async-start(bf16[32,256,128]{2,1,0:T(8,128)(2,1)} %bitcast.23), calls=%async_computation.1 | async-start | bytes 4194304 | tf_op jit(solution)/shard_map/all_to_all | solution.py:76
  61.7 85.7 %all-gather.2.cloned.1.call-start = ((), (), s32[]{:S(2)}) async-start(), calls=%async_computation.4 | async-start | bytes 2377728 | tf_op jit(solution)/shard_map/all_gather | solution.py:81
  115.7 11.5 %all-to-all-start.3 = ((bf16[4,512,128]{2,1,0:T(8,128)(2,1)}), bf16[4,512,128]{2,1,0:T(8,128)(2,1)S(1)}, u32[]{:S(2)}, u32[]{:S(2)}) async-start(bf16[4,512,128]{2,1,0:T(8,128)(2,1)} %broadcast_in_dim.17), calls=%async_computation.3 | async-start | bytes 1048576 | tf_op jit(solution)/shard_map/all_to_all | solution.py:22
  137.6 2.9 %copy-start.5 = (f32[4096]{0:T(1024)S(1)}, f32[4096]{0:T(1024)}, u32[]{:S(2)}) copy-start(f32[4096]{0:T(1024)} %param.15) | copy-start | bytes 49156
  137.6 3.5 %copy-start.1 = (f32[4096,128]{0,1:T(8,128)S(1)}, f32[4096,128]{0,1:T(8,128)}, u32[]{:S(2)}) copy-start(f32[4096,128]{0,1:T(8,128)} %copy.22) | copy-start | bytes 6291460
Sparse Core Ops, SparseCore 0:
  74.9 65.2 all-gather.1

commit v9 on v8

--- a/solution.py
+++ b/solution.py
@@ -80,21 +80,24 @@
     ).astype(jnp.bfloat16)
     full_w = lax.all_gather(mine_w, axes, axis=0, tiled=True)
 
-    row_range = jnp.arange(shard_rows, dtype=jnp.int32)
-    place = (row_range[:, None] == touched_rows[0][None, :]).astype(jnp.bfloat16)
-    place, incoming = lax.optimization_barrier((place, incoming))
     incoming_rows = incoming.reshape(-1, width)
     slot_rows = recv_rows[0].reshape(-1)
     touched = touched_rows[0]
     select = (touched[:, None] == slot_rows[None, :]).astype(jnp.bfloat16)
     local_sums = jnp.dot(select, incoming_rows, preferred_element_type=jnp.float32)
     touched_grads = rep_sum(local_sums, rep).astype(jnp.bfloat16)
+    row_range = jnp.arange(shard_rows, dtype=jnp.int32)
+    place = (row_range[:, None] == touched[None, :]).astype(jnp.bfloat16)
     with_marks = jnp.concatenate([touched_grads, jnp.ones_like(touched_grads)], axis=1)
     spread_rows = jnp.dot(place, with_marks, preferred_element_type=jnp.float32)
     row_grads = spread_rows[:, :width]
     marks = spread_rows[:, width] > 0.5
 
-    weight_grad = full_w[:, :dim].T.astype(jnp.float32) * scale
+    eye = (lax.broadcasted_iota(jnp.int32, (dim, dim), 0) == lax.broadcasted_iota(jnp.int32, (dim, dim), 1)).astype(jnp.bfloat16)
+    weight_t = lax.dot_general(
+        full_w[:, :dim], eye, (((0,), (0,)), ((), ())), preferred_element_type=jnp.float32
+    )
+    weight_grad = weight_t * scale
     bias_grad = full_w[:, dim].astype(jnp.float32) * scale
     upd_table, upd_accum = adagrad_rows(emb_table, row_accum, row_grads)
     new_table = jnp.where(marks[:, None], upd_table, emb_table)

time: 166 us -> 158 us (0.952); the launches traced: 165 us -> 155 us
  other arithmetic: 23 us -> 4.54 us
  waiting for transfers between devices: 24.2 us -> 35 us
  local copies, waits for them, and re-layouts: 17.1 us -> 12.6 us
  matrix products: 54.9 us -> 57.4 us
    all_to_all x1, waiting for transfers between devices: 16.9 us -> 27 us  [per_device(): lax.all_to_all(outgoing, 'shard', split_axis=0, concat_axis=0, tiled=True)]
    convert_element_type x1 -> x0, other arithmetic: 10 us -> none  [per_device(): (row_range[:, None] == touched_rows[0][None, :]).astype(jnp.bfloat16)]
    dot_general x0 -> x1, matrix products: none -> 5.99 us  [per_device(): lax.dot_general(full_w[:, :dim], eye, (((0,), (0,)), ((), ())), preferred...]
    unnamed x27 -> x26, local copies, waits for them, and re-layouts: 12.2 us -> 7.59 us
    mul x1 -> x0, other arithmetic: 4.13 us -> none  [per_device(): weight_grad = full_w[:, :dim].T.astype(jnp.float32) * scale]
    dot_general x1, matrix products: 10.4 us -> 6.96 us  [per_device(): spread_rows = jnp.dot(place, with_marks, preferred_element_type=jnp.float32)]
  transfers between devices with their start and end apart: 4 -> 4, of which waited for: 3 -> 3; matrix products, arithmetic and copies ran while one was open for 47% -> 39% of each run, Pallas kernels for 0% -> 0%
where the time goes in v9:
time: 158 us; the launch traced here: 155 us
  matrix products  57.4 us (36%)
  waiting for transfers between devices  35 us (22%)
  starting transfers between devices  20.3 us (13%)
  between operations  14.2 us (9%)
  local copies, waits for them, and re-layouts  12.6 us (8%)
  blocking collectives  11.3 us (7%)
  other arithmetic  4.54 us (3%)
    all_to_all x1, waiting for transfers between devices, per_device(): lax.all_to_all(outgoing, 'shard', split_axis=0, concat_axis=0, tiled=True)  27 us
    dot_general x1, matrix products, per_device(): jnp.dot(pick, pooled, preferred_element_type=jnp.float32)  23.1 us
    all_to_all x1, starting transfers between devices, per_device(): got_w = lax.all_to_all(packed, axes, 0, 0, tiled=True)  11.8 us
    all_to_all x1, blocking collectives, rep_sum(): got = lax.all_to_all(parts, 'rep', 0, 0, tiled=True)  11.3 us
    dot_general x1, matrix products, per_device(): jnp.dot(select, incoming_rows, preferred_element_type=jnp.float32)  11.3 us
    unnamed x26, local copies, waits for them, and re-layouts  7.59 us
    dot_general x1, matrix products, per_device(): spread_rows = jnp.dot(place, with_marks, preferred_element_type=jnp.float32)  6.96 us
    dot_general x1, matrix products, per_device(): lax.dot_general(full_w[:, :dim], eye, (((0,), (0,)), ((), ())), preferred...  5.99 us
  transfers between devices with their start and end apart: 4, of which 3 were waited for; matrix products, arithmetic and copies ran while one was open for 39% of the time, Pallas kernels for 0%

profile of v9, /device:TPU:0, one launch (start us, length us, event | category | flops | bytes accessed | tf_op | source)
XLA Modules:
  0.0 155.4 jit_solution(13316355522908445612)
XLA Ops:
  7.2 0.0 copy-start
  7.2 5.1 %fusion.10 = bf16[128,8,1152]{2,1,0:T(8,128)(2,1)} fusion(bf16[512,1024]{1,0:T(8,128)(2,1)} %param.10, bf16[512,1024]{1,0:T(8,128)(2,1)} %param.11), kind=kOutput, calls=%fused_computation.14 | convolution fusion | flops 1211236352 | bytes 4456448 | tf_op jit(solution)/shard_map/dot_general | solution.py:53
  12.2 0.0 copy-start.7
  12.2 11.8 %all-to-all-start = ((bf16[128,8,1152]{2,1,0:T(8,128)(2,1)}), bf16[128,8,1152]{2,1,0:T(8,128)(2,1)}, u32[]{:S(2)}, u32[]{:S(2)}) async-start(bf16[128,8,1152]{2,1,0:T(8,128)(2,1)} %fusion.10), calls=%async_computation | async-start | bytes 4718592 | tf_op jit(solution)/shard_map/all_to_all | solution.py:57
  24.1 0.0 copy-done
  24.1 0.0 copy-done.7
  24.1 0.0 copy-start.8
  24.1 0.0 copy-start.10
  24.1 1.2 fusion.31
  25.4 0.0 copy-done.8
  25.4 0.0 copy-done.10
  25.4 1.5 fusion.19
  26.9 0.0 copy-start.2
  26.9 1.0 copy-done.2
  27.9 0.0 copy-start.3
  27.9 0.0 copy-start.6
  27.9 0.1 slice.26
  28.0 1.8 %reshape.59 = bf16[3584,128]{1,0:T(8,128)(2,1)} reshape(bf16[512,896]{1,0:T(8,128)(2,1)S(1)} %slice.26) | data formatting | bytes 1835008 | tf_op jit(solution)/shard_map/reshape | solution.py:64
  29.8 0.0 copy-done.3
  29.8 0.0 copy-done.6
  29.9 0.1 iota_compare_fusion.10
  30.0 23.1 %fusion.8 = bf16[8192,128]{1,0:T(8,128)(2,1)} fusion(bf16[3584,128]{1,0:T(8,128)(2,1)} %reshape.59, s32[8192]{0:T(1024)S(1)} %broadcast_select_fusion), kind=kOutput, calls=%fused_computation.10 | convolution fusion | flops 7546601472 | bytes 3047424 | tf_op jit(solution)/shard_map/dot_general | solution.py:72
  53.1 3.7 %all-to-all-done = bf16[128,8,1152]{2,1,0:T(8,128)(2,1)} async-done(((bf16[128,8,1152]{2,1,0:T(8,128)(2,1)}), bf16[128,8,1152]{2,1,0:T(8,128)(2,1)}, u32[]{:S(2)}, u32[]{:S(2)}) %all-to-all-start) | async-done | bytes 2359328 | tf_op jit(solution)/shard_map/all_to_all | solution.py:57
  56.8 4.8 %all-to-all-start.1 = ((bf16[32,256,128]{2,1,0:T(8,128)(2,1)}), bf16[32,256,128]{2,1,0:T(8,128)(2,1)}, u32[]{:S(2)}, u32[]{:S(2)}) async-start(bf16[32,256,128]{2,1,0:T(8,128)(2,1)} %bitcast.20), calls=%async_computation.1 | async-start | bytes 4194304 | tf_op jit(solution)/shard_map/all_to_all | solution.py:76
  61.5 0.0 copy-start.4
  61.6 0.0 copy-start.9
  61.6 0.3 all-gather.2.cloned.1.call-start
  61.8 2.2 %fusion.14 = bf16[1,8,1152]{2,0,1:T(2,128)(2,1)S(1)} fusion(bf16[128,8,1152]{2,1,0:T(8,128)(2,1)} %all-to-all-done), kind=kOutput, calls=%fused_computation.19 | convolution fusion | flops 2359296 | bytes 2377728 | tf_op jit(solution)/shard_map/dot_general | solution.py:78
  64.0 0.6 copy.31
  64.6 0.0 all-gather.2.cloned.1.call-update
  64.6 0.0 copy-done.4
  64.7 27.0 %all-to-all-done.1 = bf16[32,256,128]{2,1,0:T(8,128)(2,1)} async-done(((bf16[32,256,128]{2,1,0:T(8,128)(2,1)}), bf16[32,256,128]{2,1,0:T(8,128)(2,1)}, u32[]{:S(2)}, u32[]{:S(2)}) %all-to-all-start.1) | async-done | bytes 2097184 | tf_op jit(solution)/shard_map/all_to_all | solution.py:76
  91.7 0.0 copy-done.9
  91.7 11.3 %fusion.11 = bf16[2048,128]{1,0:T(8,128)(2,1)S(1)} fusion(bf16[8192,128]{1,0:T(8,128)(2,1)} %bitcast.5, s32[8192]{0:T(1024)S(1)} %bitcast.27, s32[2048]{0:T(1024)S(1)} %bitcast.29), kind=kOutput, calls=%fused_computation.18 | convolution fusion | flops 4312006656 | bytes 2662400 | tf_op jit(solution)/shard_map/dot_general | solution.py:87
  103.0 11.3 %all_to_all.20 = bf16[4,512,128]{2,1,0:T(8,128)(2,1)S(1)} all-to-all(bf16[4,512,128]{2,1,0:T(8,128)(2,1)S(1)} %bitcast.22), channel_id=1, replica_groups=mesh['rep'=4,'shard'=32] {'rep'}, dimensions={0} | all-to-all | bytes 1048576 | tf_op jit(solution)/shard_map/all_to_all | solution.py:19
  114.4 0.1 reduce_sum.21
  114.4 0.9 broadcast_in_dim.17
  115.3 3.5 %all-to-all-start.3 = ((bf16[4,512,128]{2,1,0:T(8,128)(2,1)}), bf16[4,512,128]{2,1,0:T(8,128)(2,1)S(1)}, u32[]{:S(2)}, u32[]{:S(2)}) async-start(bf16[4,512,128]{2,1,0:T(8,128)(2,1)} %broadcast_in_dim.17), calls=%async_computation.3 | async-start | bytes 1048576 | tf_op jit(solution)/shard_map/all_to_all | solution.py:22
  118.8 1.6 %slice.29 = bf16[512,128]{1,0:T(8,128)(2,1)} slice(bf16[512,1024]{1,0:T(8,128)(2,1)} %copy-done.2), slice={[0:512], [0:128]} | slice | bytes 262144 | tf_op jit(solution)/shard_map/slice | solution.py:63
  120.4 2.9 %copy.21 = f32[4096,128]{0,1:T(8,128)} copy(f32[4096,128]{1,0:T(8,128)} %param.14) | data formatting | bytes 4194304 | tf_op args[4]
  123.3 4.3 %all-to-all-done.3 = bf16[4,512,128]{2,1,0:T(8,128)(2,1)S(1)} async-done(((bf16[4,512,128]{2,1,0:T(8,128)(2,1)}), bf16[4,512,128]{2,1,0:T(8,128)(2,1)S(1)}, u32[]{:S(2)}, u32[]{:S(2)}) %all-to-all-start.3) | async-done | bytes 524320 | tf_op jit(solution)/shard_map/all_to_all | solution.py:22
  127.6 7.0 %fusion.6 = f32[4096,256]{0,1:T(8,128)S(1)} fusion(s32[2048]{0:T(1024)S(1)} %bitcast.30, bf16[2048,128]{1,0:T(8,128)(2,1)S(1)} %bitcast.21), kind=kOutput, calls=%fused_computation.8 | convolution fusion | flops 4303355904 | bytes 4726784 | tf_op jit(solution)/shard_map/dot_general | solution.py:92
  134.6 0.0 copy-start.5
  134.6 0.0 copy-start.1
  134.6 0.1 compare_reduce_fusion
  134.7 0.2 multiply_reduce_fusion
  134.8 0.5 copy-done.5
  135.3 0.6 fusion.25
  135.9 0.3 copy-done.1
  136.2 1.8 %subtract_select_fusion = f32[4096,128]{0,1:T(8,128)} fusion(f32[4096,128]{0,1:T(8,128)S(1)} %copy-done.1, f32[4096,256]{0,1:T(8,128)S(1)} %fusion.6, f32[4096]{0:T(1024)S(1)} %get-tuple-element.25, pred[4096]{0:T(1024)(128)(4,1)S(1)} %compare_reduce_fusion), kind=kLoop, calls=%fused_computation.26 | loop fusion | flops 2621440 | bytes 6311936 | tf_op jit(solution)/shard_map/jit(_where)/select_n | solution.py:103
  138.0 2.9 %copy.23 = f32[4096,128]{1,0:T(8,128)} copy(f32[4096,128]{0,1:T(8,128)} %subtract_select_fusion) | data formatting | bytes 4194304
  140.9 0.0 all-gather.2.cloned.1.call-done
  140.9 6.0 %fusion.16 = f32[1024,1024]{1,0:T(8,128)} fusion(bf16[1024,1152]{1,0:T(8,128)(2,1)} %all-gather.2.cloned.1.call-done), kind=kOutput, calls=%fused_computation.21 | convolution fusion | flops 2149580800 | bytes 6291456 | tf_op jit(solution)/shard_map/dot_general | solution.py:97
  146.8 1.8 %multiply_reduce_fusion.1 = f32[1024]{0:T(1024)} fusion(bf16[1024,1152]{1,0:T(8,128)(2,1)} %all-gather.2.cloned.1.call-done), kind=kLoop, calls=%fused_computation.30 | loop fusion | flops 2048 | bytes 6144 | tf_op jit(solution)/shard_map/mul | solution.py:101
  (4 shorter events, 0.1 us)
Async XLA Ops:
  7.2 16.9 %copy-start = (bf16[1024,1024]{1,0:T(8,128)(2,1)S(1)}, bf16[1024,1024]{1,0:T(8,128)(2,1)}, u32[]{:S(2)}) copy-start(bf16[1024,1024]{1,0:T(8,128)(2,1)} %param.12) | copy-start | bytes 6291460
  12.2 11.9 %copy-start.7 = (bf16[512,1024]{1,0:T(8,128)(2,1)S(1)}, bf16[512,1024]{1,0:T(8,128)(2,1)}, u32[]{:S(2)}) copy-start(bf16[512,1024]{1,0:T(8,128)(2,1)} %param.10) | copy-start | bytes 3145732
  12.2 44.5 %all-to-all-start = ((bf16[128,8,1152]{2,1,0:T(8,128)(2,1)}), bf16[128,8,1152]{2,1,0:T(8,128)(2,1)}, u32[]{:S(2)}, u32[]{:S(2)}) async-start(bf16[128,8,1152]{2,1,0:T(8,128)(2,1)} %fusion.10), calls=%async_computation | async-start | bytes 4718592 | tf_op jit(solution)/shard_map/all_to_all | solution.py:57
  24.1 1.3 copy-start.8
  24.1 1.3 copy-start.10
  26.9 1.0 copy-start.2
  27.9 1.9 %copy-start.3 = (s32[1,32,256]{2,1,0:T(8,128)S(1)}, s32[1,32,256]{2,1,0:T(8,128)}, u32[]{:S(2)}) copy-start(s32[1,32,256]{2,1,0:T(8,128)} %param.16) | copy-start | bytes 98308
  27.9 1.9 %copy-start.6 = (s32[1,32]{1,0:T(1,128)S(1)}, s32[1,32]{1,0:T(1,128)}, u32[]{:S(2)}) copy-start(s32[1,32]{1,0:T(1,128)} %param.17) | copy-start | bytes 388
  56.8 34.9 %all-to-all-start.1 = ((bf16[32,256,128]{2,1,0:T(8,128)(2,1)}), bf16[32,256,128]{2,1,0:T(8,128)(2,1)}, u32[]{:S(2)}, u32[]{:S(2)}) async-start(bf16[32,256,128]{2,1,0:T(8,128)(2,1)} %bitcast.20), calls=%async_computation.1 | async-start | bytes 4194304 | tf_op jit(solution)/shard_map/all_to_all | solution.py:76
  61.5 3.1 %copy-start.4 = (s32[1,32,256]{2,1,0:T(8,128)S(1)}, s32[1,32,256]{2,1,0:T(8,128)}, u32[]{:S(2)}) copy-start(s32[1,32,256]{2,1,0:T(8,128)} %param.18) | copy-start | bytes 98308
  61.6 30.1 %copy-start.9 = (s32[1,2048]{1,0:T(1,128)S(1)}, s32[1,2048]{1,0:T(1,128)}, u32[]{:S(2)}) copy-start(s32[1,2048]{1,0:T(1,128)} %param.19) | copy-start | bytes 24580
  61.6 79.3 %all-gather.2.cloned.1.call-start = ((), (), s32[]{:S(2)}) async-start(), calls=%async_computation.4 | async-start | bytes 2377728 | tf_op jit(solution)/shard_map/all_gather | solution.py:81
  115.3 12.3 %all-to-all-start.3 = ((bf16[4,512,128]{2,1,0:T(8,128)(2,1)}), bf16[4,512,128]{2,1,0:T(8,128)(2,1)S(1)}, u32[]{:S(2)}, u32[]{:S(2)}) async-start(bf16[4,512,128]{2,1,0:T(8,128)(2,1)} %broadcast_in_dim.17), calls=%async_computation.3 | async-start | bytes 1048576 | tf_op jit(solution)/shard_map/all_to_all | solution.py:22
  134.6 0.7 copy-start.5
  134.6 1.6 %copy-start.1 = (f32[4096,128]{0,1:T(8,128)S(1)}, f32[4096,128]{0,1:T(8,128)}, u32[]{:S(2)}) copy-start(f32[4096,128]{0,1:T(8,128)} %copy.21) | copy-start | bytes 6291460
Sparse Core Ops, SparseCore 0:
  65.3 70.4 all-gather.1

commit v10 on v9

--- a/solution.py
+++ b/solution.py
@@ -73,11 +73,12 @@
     outgoing = picked.reshape(shard_count, slot_total, width)
 
     got_w, outgoing = lax.optimization_barrier((got_w, outgoing))
-    incoming = lax.all_to_all(outgoing, "shard", split_axis=0, concat_axis=0, tiled=True)
     ones = jnp.ones((devices,), jnp.bfloat16)
     mine_w = lax.dot_general(
         ones, got_w, (((0,), (0,)), ((), ())), preferred_element_type=jnp.float32
     ).astype(jnp.bfloat16)
+    mine_w, outgoing = lax.optimization_barrier((mine_w, outgoing))
+    incoming = lax.all_to_all(outgoing, "shard", split_axis=0, concat_axis=0, tiled=True)
     full_w = lax.all_gather(mine_w, axes, axis=0, tiled=True)
 
     incoming_rows = incoming.reshape(-1, width)
@@ -98,7 +99,7 @@
         full_w[:, :dim], eye, (((0,), (0,)), ((), ())), preferred_element_type=jnp.float32
     )
     weight_grad = weight_t * scale
-    bias_grad = full_w[:, dim].astype(jnp.float32) * scale
+    bias_grad = jnp.mean(full_w[:, dim:].astype(jnp.float32), axis=1) * scale
     upd_table, upd_accum = adagrad_rows(emb_table, row_accum, row_grads)
     new_table = jnp.where(marks[:, None], upd_table, emb_table)
     new_accum = jnp.where(marks, upd_accum, row_accum)

time: 158 us -> 160 us (1.013)
  waiting for transfers between devices: 35 us -> 37.9 us
    all_to_all x1, waiting for transfers between devices: 27 us -> 29.4 us  [per_device(): lax.all_to_all(outgoing, 'shard', split_axis=0, concat_axis=0, tiled=True)]
  transfers between devices with their start and end apart: 4 -> 4, of which waited for: 3 -> 3; matrix products, arithmetic and copies ran while one was open for 39% -> 36% of each run, Pallas kernels for 0% -> 0%
where the time goes in v10:
time: 160 us; the launch traced here: 158 us
  matrix products  57.4 us (36%)
  waiting for transfers between devices  37.9 us (24%)
  starting transfers between devices  20.5 us (13%)
  between operations  14.2 us (9%)
  local copies, waits for them, and re-layouts  12.6 us (8%)
  blocking collectives  11.3 us (7%)
  other arithmetic  4.47 us (3%)
    all_to_all x1, waiting for transfers between devices, per_device(): lax.all_to_all(outgoing, 'shard', split_axis=0, concat_axis=0, tiled=True)  29.4 us
    dot_general x1, matrix products, per_device(): jnp.dot(pick, pooled, preferred_element_type=jnp.float32)  23.1 us
    all_to_all x1, starting transfers between devices, per_device(): got_w = lax.all_to_all(packed, axes, 0, 0, tiled=True)  11.8 us
    all_to_all x1, blocking collectives, rep_sum(): got = lax.all_to_all(parts, 'rep', 0, 0, tiled=True)  11.3 us
    dot_general x1, matrix products, per_device(): jnp.dot(select, incoming_rows, preferred_element_type=jnp.float32)  11.3 us
    unnamed x26, local copies, waits for them, and re-layouts  7.58 us
    dot_general x1, matrix products, per_device(): spread_rows = jnp.dot(place, with_marks, preferred_element_type=jnp.float32)  6.96 us
    dot_general x1, matrix products, per_device(): lax.dot_general(full_w[:, :dim], eye, (((0,), (0,)), ((), ())), preferred...  5.99 us
  transfers between devices with their start and end apart: 4, of which 3 were waited for; matrix products, arithmetic and copies ran while one was open for 36% of the time, Pallas kernels for 0%

profile of v10, /device:TPU:0, one launch (start us, length us, event | category | flops | bytes accessed | tf_op | source)
XLA Modules:
  0.0 158.3 jit_solution(10994214610145396737)
XLA Ops:
  7.2 0.0 copy-start
  7.2 5.1 %fusion.10 = bf16[128,8,1152]{2,1,0:T(8,128)(2,1)} fusion(bf16[512,1024]{1,0:T(8,128)(2,1)} %param.10, bf16[512,1024]{1,0:T(8,128)(2,1)} %param.11), kind=kOutput, calls=%fused_computation.14 | convolution fusion | flops 1211236352 | bytes 4456448 | tf_op jit(solution)/shard_map/dot_general | solution.py:53
  12.2 0.0 copy-start.7
  12.2 11.8 %all-to-all-start = ((bf16[128,8,1152]{2,1,0:T(8,128)(2,1)}), bf16[128,8,1152]{2,1,0:T(8,128)(2,1)}, u32[]{:S(2)}, u32[]{:S(2)}) async-start(bf16[128,8,1152]{2,1,0:T(8,128)(2,1)} %fusion.10), calls=%async_computation | async-start | bytes 4718592 | tf_op jit(solution)/shard_map/all_to_all | solution.py:57
  24.1 0.0 copy-done
  24.1 0.0 copy-done.7
  24.1 0.0 copy-start.8
  24.1 0.0 copy-start.10
  24.1 1.2 fusion.31
  25.4 0.0 copy-done.8
  25.4 0.0 copy-done.10
  25.4 1.5 fusion.19
  26.9 0.0 copy-start.2
  26.9 1.0 copy-done.2
  27.9 0.0 copy-start.3
  27.9 0.0 copy-start.6
  27.9 0.1 slice.26
  28.0 1.8 %reshape.56 = bf16[3584,128]{1,0:T(8,128)(2,1)} reshape(bf16[512,896]{1,0:T(8,128)(2,1)S(1)} %slice.26) | data formatting | bytes 1835008 | tf_op jit(solution)/shard_map/reshape | solution.py:64
  29.8 0.0 copy-done.3
  29.8 0.0 copy-done.6
  29.9 0.1 iota_compare_fusion.10
  30.0 23.1 %fusion.8 = bf16[8192,128]{1,0:T(8,128)(2,1)} fusion(bf16[3584,128]{1,0:T(8,128)(2,1)} %reshape.56, s32[8192]{0:T(1024)S(1)} %broadcast_select_fusion), kind=kOutput, calls=%fused_computation.10 | convolution fusion | flops 7546601472 | bytes 3047424 | tf_op jit(solution)/shard_map/dot_general | solution.py:72
  53.1 3.7 %all-to-all-done = bf16[128,8,1152]{2,1,0:T(8,128)(2,1)} async-done(((bf16[128,8,1152]{2,1,0:T(8,128)(2,1)}), bf16[128,8,1152]{2,1,0:T(8,128)(2,1)}, u32[]{:S(2)}, u32[]{:S(2)}) %all-to-all-start) | async-done | bytes 2359328 | tf_op jit(solution)/shard_map/all_to_all | solution.py:57
  56.8 2.2 %fusion.14 = bf16[1,8,1152]{2,0,1:T(2,128)(2,1)S(1)} fusion(bf16[128,8,1152]{2,1,0:T(8,128)(2,1)} %all-to-all-done), kind=kOutput, calls=%fused_computation.19 | convolution fusion | flops 2359296 | bytes 2377728 | tf_op jit(solution)/shard_map/dot_general | solution.py:77
  58.9 0.6 copy.28
  59.5 0.0 copy-start.4
  59.5 0.0 copy-start.9
  59.5 4.9 %all-to-all-start.1 = ((bf16[32,256,128]{2,1,0:T(8,128)(2,1)}), bf16[32,256,128]{2,1,0:T(8,128)(2,1)}, u32[]{:S(2)}, u32[]{:S(2)}) async-start(bf16[32,256,128]{2,1,0:T(8,128)(2,1)} %bitcast.20), calls=%async_computation.1 | async-start | bytes 4194304 | tf_op jit(solution)/shard_map/all_to_all | solution.py:81
  64.5 0.3 all-gather.2.cloned.1.call-start
  64.7 0.5 all-gather.2.cloned.1.call-update
  65.2 0.0 copy-done.4
  65.2 29.4 %all-to-all-done.1 = bf16[32,256,128]{2,1,0:T(8,128)(2,1)} async-done(((bf16[32,256,128]{2,1,0:T(8,128)(2,1)}), bf16[32,256,128]{2,1,0:T(8,128)(2,1)}, u32[]{:S(2)}, u32[]{:S(2)}) %all-to-all-start.1) | async-done | bytes 2097184 | tf_op jit(solution)/shard_map/all_to_all | solution.py:81
  94.6 0.0 copy-done.9
  94.6 11.3 %fusion.11 = bf16[2048,128]{1,0:T(8,128)(2,1)S(1)} fusion(bf16[8192,128]{1,0:T(8,128)(2,1)} %bitcast.5, s32[8192]{0:T(1024)S(1)} %bitcast.27, s32[2048]{0:T(1024)S(1)} %bitcast.29), kind=kOutput, calls=%fused_computation.18 | convolution fusion | flops 4312006656 | bytes 2662400 | tf_op jit(solution)/shard_map/dot_general | solution.py:88
  105.9 11.3 %all_to_all.20 = bf16[4,512,128]{2,1,0:T(8,128)(2,1)S(1)} all-to-all(bf16[4,512,128]{2,1,0:T(8,128)(2,1)S(1)} %bitcast.22), channel_id=1, replica_groups=mesh['rep'=4,'shard'=32] {'rep'}, dimensions={0} | all-to-all | bytes 1048576 | tf_op jit(solution)/shard_map/all_to_all | solution.py:19
  117.3 0.1 reduce_sum.31
  117.4 0.9 broadcast_in_dim.17
  118.2 3.5 %all-to-all-start.3 = ((bf16[4,512,128]{2,1,0:T(8,128)(2,1)}), bf16[4,512,128]{2,1,0:T(8,128)(2,1)S(1)}, u32[]{:S(2)}, u32[]{:S(2)}) async-start(bf16[4,512,128]{2,1,0:T(8,128)(2,1)} %broadcast_in_dim.17), calls=%async_computation.3 | async-start | bytes 1048576 | tf_op jit(solution)/shard_map/all_to_all | solution.py:22
  121.7 1.6 %slice.29 = bf16[512,128]{1,0:T(8,128)(2,1)} slice(bf16[512,1024]{1,0:T(8,128)(2,1)} %copy-done.2), slice={[0:512], [0:128]} | slice | bytes 262144 | tf_op jit(solution)/shard_map/slice | solution.py:63
  123.3 2.9 %copy.18 = f32[4096,128]{0,1:T(8,128)} copy(f32[4096,128]{1,0:T(8,128)} %param.14) | data formatting | bytes 4194304 | tf_op args[4]
  126.2 4.4 %all-to-all-done.3 = bf16[4,512,128]{2,1,0:T(8,128)(2,1)S(1)} async-done(((bf16[4,512,128]{2,1,0:T(8,128)(2,1)}), bf16[4,512,128]{2,1,0:T(8,128)(2,1)S(1)}, u32[]{:S(2)}, u32[]{:S(2)}) %all-to-all-start.3) | async-done | bytes 524320 | tf_op jit(solution)/shard_map/all_to_all | solution.py:22
  130.6 7.0 %fusion.6 = f32[4096,256]{0,1:T(8,128)S(1)} fusion(s32[2048]{0:T(1024)S(1)} %bitcast.30, bf16[2048,128]{1,0:T(8,128)(2,1)S(1)} %bitcast.21), kind=kOutput, calls=%fused_computation.8 | convolution fusion | flops 4303355904 | bytes 4726784 | tf_op jit(solution)/shard_map/dot_general | solution.py:93
  137.5 0.0 copy-start.5
  137.5 0.0 copy-start.1
  137.5 0.1 compare_reduce_fusion
  137.6 0.2 multiply_reduce_fusion
  137.8 0.5 copy-done.5
  138.2 0.6 fusion.25
  138.9 0.3 copy-done.1
  139.1 1.8 %subtract_select_fusion = f32[4096,128]{0,1:T(8,128)} fusion(f32[4096,128]{0,1:T(8,128)S(1)} %copy-done.1, f32[4096,256]{0,1:T(8,128)S(1)} %fusion.6, f32[4096]{0:T(1024)S(1)} %get-tuple-element.24, pred[4096]{0:T(1024)(128)(4,1)S(1)} %compare_reduce_fusion), kind=kLoop, calls=%fused_computation.26 | loop fusion | flops 2621440 | bytes 6311936 | tf_op jit(solution)/shard_map/jit(_where)/select_n | solution.py:104
  140.9 2.9 %copy.20 = f32[4096,128]{1,0:T(8,128)} copy(f32[4096,128]{0,1:T(8,128)} %subtract_select_fusion) | data formatting | bytes 4194304
  143.8 0.0 all-gather.2.cloned.1.call-done
  143.8 1.1 convert_reduce_fusion
  144.9 0.6 broadcast_multiply_fusion
  145.5 6.0 %fusion.16 = f32[1024,1024]{1,0:T(8,128)} fusion(bf16[1024,1152]{1,0:T(8,128)(2,1)} %all-gather.2.cloned.1.call-done), kind=kOutput, calls=%fused_computation.21 | convolution fusion | flops 2149580800 | bytes 6291456 | tf_op jit(solution)/shard_map/dot_general | solution.py:98
  (4 shorter events, 0.1 us)
Async XLA Ops:
  7.2 16.9 %copy-start = (bf16[1024,1024]{1,0:T(8,128)(2,1)S(1)}, bf16[1024,1024]{1,0:T(8,128)(2,1)}, u32[]{:S(2)}) copy-start(bf16[1024,1024]{1,0:T(8,128)(2,1)} %param.12) | copy-start | bytes 6291460
  12.2 11.9 %copy-start.7 = (bf16[512,1024]{1,0:T(8,128)(2,1)S(1)}, bf16[512,1024]{1,0:T(8,128)(2,1)}, u32[]{:S(2)}) copy-start(bf16[512,1024]{1,0:T(8,128)(2,1)} %param.10) | copy-start | bytes 3145732
  12.2 44.5 %all-to-all-start = ((bf16[128,8,1152]{2,1,0:T(8,128)(2,1)}), bf16[128,8,1152]{2,1,0:T(8,128)(2,1)}, u32[]{:S(2)}, u32[]{:S(2)}) async-start(bf16[128,8,1152]{2,1,0:T(8,128)(2,1)} %fusion.10), calls=%async_computation | async-start | bytes 4718592 | tf_op jit(solution)/shard_map/all_to_all | solution.py:57
  24.1 1.3 copy-start.8
  24.1 1.3 copy-start.10
  26.9 1.0 copy-start.2
  27.9 1.9 %copy-start.3 = (s32[1,32,256]{2,1,0:T(8,128)S(1)}, s32[1,32,256]{2,1,0:T(8,128)}, u32[]{:S(2)}) copy-start(s32[1,32,256]{2,1,0:T(8,128)} %param.16) | copy-start | bytes 98308
  27.9 1.9 %copy-start.6 = (s32[1,32]{1,0:T(1,128)S(1)}, s32[1,32]{1,0:T(1,128)}, u32[]{:S(2)}) copy-start(s32[1,32]{1,0:T(1,128)} %param.17) | copy-start | bytes 388
  59.5 5.7 %copy-start.4 = (s32[1,32,256]{2,1,0:T(8,128)S(1)}, s32[1,32,256]{2,1,0:T(8,128)}, u32[]{:S(2)}) copy-start(s32[1,32,256]{2,1,0:T(8,128)} %param.18) | copy-start | bytes 98308
  59.5 35.0 %copy-start.9 = (s32[1,2048]{1,0:T(1,128)S(1)}, s32[1,2048]{1,0:T(1,128)}, u32[]{:S(2)}) copy-start(s32[1,2048]{1,0:T(1,128)} %param.19) | copy-start | bytes 24580
  59.5 35.0 %all-to-all-start.1 = ((bf16[32,256,128]{2,1,0:T(8,128)(2,1)}), bf16[32,256,128]{2,1,0:T(8,128)(2,1)}, u32[]{:S(2)}, u32[]{:S(2)}) async-start(bf16[32,256,128]{2,1,0:T(8,128)(2,1)} %bitcast.20), calls=%async_computation.1 | async-start | bytes 4194304 | tf_op jit(solution)/shard_map/all_to_all | solution.py:81
  64.5 79.4 %all-gather.2.cloned.1.call-start = ((), (), s32[]{:S(2)}) async-start(), calls=%async_computation.4 | async-start | bytes 2377728 | tf_op jit(solution)/shard_map/all_gather | solution.py:82
  118.2 12.3 %all-to-all-start.3 = ((bf16[4,512,128]{2,1,0:T(8,128)(2,1)}), bf16[4,512,128]{2,1,0:T(8,128)(2,1)S(1)}, u32[]{:S(2)}, u32[]{:S(2)}) async-start(bf16[4,512,128]{2,1,0:T(8,128)(2,1)} %broadcast_in_dim.17), calls=%async_computation.3 | async-start | bytes 1048576 | tf_op jit(solution)/shard_map/all_to_all | solution.py:22
  137.5 0.7 copy-start.5
  137.5 1.6 %copy-start.1 = (f32[4096,128]{0,1:T(8,128)S(1)}, f32[4096,128]{0,1:T(8,128)}, u32[]{:S(2)}) copy-start(f32[4096,128]{0,1:T(8,128)} %copy.18) | copy-start | bytes 6291460
Sparse Core Ops, SparseCore 0:
  68.2 70.4 all-gather.1

commit v11 on v10

--- a/solution.py
+++ b/solution.py
@@ -73,19 +73,24 @@
     outgoing = picked.reshape(shard_count, slot_total, width)
 
     got_w, outgoing = lax.optimization_barrier((got_w, outgoing))
+    half = slot_total // 2
+    incoming_a = lax.all_to_all(outgoing[:, :half], "shard", 0, 0, tiled=True)
+    incoming_b = lax.all_to_all(outgoing[:, half:], "shard", 0, 0, tiled=True)
     ones = jnp.ones((devices,), jnp.bfloat16)
     mine_w = lax.dot_general(
         ones, got_w, (((0,), (0,)), ((), ())), preferred_element_type=jnp.float32
     ).astype(jnp.bfloat16)
-    mine_w, outgoing = lax.optimization_barrier((mine_w, outgoing))
-    incoming = lax.all_to_all(outgoing, "shard", split_axis=0, concat_axis=0, tiled=True)
     full_w = lax.all_gather(mine_w, axes, axis=0, tiled=True)
 
-    incoming_rows = incoming.reshape(-1, width)
-    slot_rows = recv_rows[0].reshape(-1)
     touched = touched_rows[0]
-    select = (touched[:, None] == slot_rows[None, :]).astype(jnp.bfloat16)
-    local_sums = jnp.dot(select, incoming_rows, preferred_element_type=jnp.float32)
+
+    def touched_sums(slots, rows):
+        select = (touched[:, None] == rows.reshape(-1)[None, :]).astype(jnp.bfloat16)
+        return jnp.dot(select, slots.reshape(-1, width), preferred_element_type=jnp.float32)
+
+    local_sums = touched_sums(incoming_a, recv_rows[0][:, :half]) + touched_sums(
+        incoming_b, recv_rows[0][:, half:]
+    )
     touched_grads = rep_sum(local_sums, rep).astype(jnp.bfloat16)
     row_range = jnp.arange(shard_rows, dtype=jnp.int32)
     place = (row_range[:, None] == touched[None, :]).astype(jnp.bfloat16)

time: 160 us -> 171 us (1.069)
  blocking collectives: 11.3 us -> 34.2 us
  waiting for transfers between devices: 37.9 us -> 21.8 us
  local copies, waits for them, and re-layouts: 12.6 us -> 15.2 us
  matrix products: 57.4 us -> 59.4 us
    all_to_all x1, waiting for transfers between devices: 29.4 us -> 7.07 us  [per_device(): incoming_a = lax.all_to_all(outgoing[:, :half], 'shard', 0, 0, tiled=True)]
    all_to_all x0 -> x1, blocking collectives: none -> 21 us  [per_device(): incoming_b = lax.all_to_all(outgoing[:, half:], 'shard', 0, 0, tiled=True)]
    all_gather x1, waiting for transfers between devices: 0.01 us -> 6.87 us  [per_device(): full_w = lax.all_gather(mine_w, axes, axis=0, tiled=True)]
    slice x0 -> x1, local copies, waits for them, and re-layouts: none -> 2.7 us  [per_device(): incoming_a = lax.all_to_all(outgoing[:, :half], 'shard', 0, 0, tiled=True)]
    dot_general x1 -> x2, matrix products: 11.3 us -> 13.4 us  [touched_sums(): jnp.dot(select, slots.reshape(-1, width), preferred_element_type=jnp.floa...]
    all_to_all x1, blocking collectives: 11.3 us -> 13.2 us  [rep_sum(): got = lax.all_to_all(parts, 'rep', 0, 0, tiled=True)]
    unnamed x26 -> x25, local copies, waits for them, and re-layouts: 7.58 us -> 7.55 us
  transfers between devices with their start and end apart: 4 -> 4, of which waited for: 3 -> 4; matrix products, arithmetic and copies ran while one was open for 36% -> 37% of each run, Pallas kernels for 0% -> 0%
where the time goes in v11:
time: 171 us; the launch traced here: 169 us
  matrix products  59.4 us (35%)
  blocking collectives  34.2 us (20%)
  waiting for transfers between devices  21.8 us (13%)
  starting transfers between devices  19.9 us (12%)
  local copies, waits for them, and re-layouts  15.2 us (9%)
  between operations  14.2 us (8%)
  other arithmetic  4.47 us (3%)
    dot_general x1, matrix products, per_device(): jnp.dot(pick, pooled, preferred_element_type=jnp.float32)  23.1 us
    all_to_all x1, blocking collectives, per_device(): incoming_b = lax.all_to_all(outgoing[:, half:], 'shard', 0, 0, tiled=True)  21 us
    dot_general x2, matrix products, touched_sums(): jnp.dot(select, slots.reshape(-1, width), preferred_element_type=jnp.floa...  13.4 us
    all_to_all x1, blocking collectives, rep_sum(): got = lax.all_to_all(parts, 'rep', 0, 0, tiled=True)  13.2 us
    all_to_all x1, starting transfers between devices, per_device(): got_w = lax.all_to_all(packed, axes, 0, 0, tiled=True)  11.8 us
    unnamed x25, local copies, waits for them, and re-layouts  7.55 us
    all_to_all x1, waiting for transfers between devices, per_device(): incoming_a = lax.all_to_all(outgoing[:, :half], 'shard', 0, 0, tiled=True)  7.07 us
    dot_general x1, matrix products, per_device(): spread_rows = jnp.dot(place, with_marks, preferred_element_type=jnp.float32)  6.96 us
  transfers between devices with their start and end apart: 4, of which 4 were waited for; matrix products, arithmetic and copies ran while one was open for 37% of the time, Pallas kernels for 0%

profile of v11, /device:TPU:0, one launch (start us, length us, event | category | flops | bytes accessed | tf_op | source)
XLA Modules:
  0.0 169.2 jit_solution(6199874053545898506)
XLA Ops:
  7.2 0.0 copy-start
  7.2 5.1 %fusion.14 = bf16[128,8,1152]{2,1,0:T(8,128)(2,1)} fusion(bf16[512,1024]{1,0:T(8,128)(2,1)} %param.10, bf16[512,1024]{1,0:T(8,128)(2,1)} %param.11), kind=kOutput, calls=%fused_computation.18 | convolution fusion | flops 1211236352 | bytes 4456448 | tf_op jit(solution)/shard_map/dot_general | solution.py:53
  12.2 0.0 copy-start.7
  12.2 11.8 %all-to-all-start = ((bf16[128,8,1152]{2,1,0:T(8,128)(2,1)}), bf16[128,8,1152]{2,1,0:T(8,128)(2,1)}, u32[]{:S(2)}, u32[]{:S(2)}) async-start(bf16[128,8,1152]{2,1,0:T(8,128)(2,1)} %fusion.14), calls=%async_computation | async-start | bytes 4718592 | tf_op jit(solution)/shard_map/all_to_all | solution.py:57
  24.1 0.0 copy-done
  24.1 0.0 copy-done.7
  24.1 0.0 copy-start.8
  24.1 0.0 copy-start.10
  24.1 1.2 fusion.39
  25.4 0.0 copy-done.8
  25.4 0.0 copy-done.10
  25.4 1.5 fusion.26
  26.9 0.0 copy-start.2
  26.9 1.0 copy-done.2
  27.9 0.0 copy-start.3
  27.9 0.0 copy-start.6
  27.9 0.1 slice.42
  28.0 1.8 %reshape.60 = bf16[3584,128]{1,0:T(8,128)(2,1)} reshape(bf16[512,896]{1,0:T(8,128)(2,1)S(1)} %slice.42) | data formatting | bytes 1835008 | tf_op jit(solution)/shard_map/reshape | solution.py:64
  29.8 0.0 copy-done.3
  29.8 0.0 copy-done.6
  29.9 0.1 iota_compare_fusion.10
  30.0 23.1 %fusion.12 = bf16[8192,128]{1,0:T(8,128)(2,1)} fusion(bf16[3584,128]{1,0:T(8,128)(2,1)} %reshape.60, s32[8192]{0:T(1024)S(1)} %broadcast_select_fusion), kind=kOutput, calls=%fused_computation.14 | convolution fusion | flops 7546601472 | bytes 3047424 | tf_op jit(solution)/shard_map/dot_general | solution.py:72
  53.1 3.7 %all-to-all-done = bf16[128,8,1152]{2,1,0:T(8,128)(2,1)} async-done(((bf16[128,8,1152]{2,1,0:T(8,128)(2,1)}), bf16[128,8,1152]{2,1,0:T(8,128)(2,1)}, u32[]{:S(2)}, u32[]{:S(2)}) %all-to-all-start) | async-done | bytes 2359328 | tf_op jit(solution)/shard_map/all_to_all | solution.py:57
  56.8 2.7 %fusion.38 = (bf16[32,128,128]{2,1,0:T(8,128)(2,1)}, bf16[32,128,128]{2,1,0:T(8,128)(2,1)S(1)}) fusion(bf16[32,256,128]{2,1,0:T(8,128)(2,1)} %bitcast.25), kind=kLoop, calls=%fused_computation.50 | loop fusion | bytes 4194304 | tf_op jit(solution)/shard_map/slice | solution.py:77
  59.5 0.0 copy-start.4
  59.5 21.0 %all_to_all.25 = bf16[32,128,128]{2,1,0:T(8,128)(2,1)} all-to-all(bf16[32,128,128]{2,1,0:T(8,128)(2,1)S(1)} %get-tuple-element.20), channel_id=1, replica_groups=mesh['rep'=4,'shard'=32] {'shard'}, dimensions={0} | all-to-all | bytes 2097152 | tf_op jit(solution)/shard_map/all_to_all | solution.py:78
  80.5 0.0 copy-start.9
  80.5 4.1 %all-to-all-start.1 = ((bf16[32,128,128]{2,1,0:T(8,128)(2,1)}), bf16[32,128,128]{2,1,0:T(8,128)(2,1)S(1)}, u32[]{:S(2)}, u32[]{:S(2)}) async-start(bf16[32,128,128]{2,1,0:T(8,128)(2,1)} %get-tuple-element.19), calls=%async_computation.1 | async-start | bytes 2097152 | tf_op jit(solution)/shard_map/all_to_all | solution.py:77
  84.5 0.3 all-gather.2.cloned.1.call-start
  84.8 0.0 copy-done.4
  84.8 2.2 %fusion.21 = bf16[1,8,1152]{2,0,1:T(2,128)(2,1)S(1)} fusion(bf16[128,8,1152]{2,1,0:T(8,128)(2,1)} %all-to-all-done), kind=kOutput, calls=%fused_computation.24 | convolution fusion | flops 2359296 | bytes 2377728 | tf_op jit(solution)/shard_map/dot_general | solution.py:80
  87.0 0.6 copy.27
  87.6 0.0 all-gather.2.cloned.1.call-update
  87.6 0.0 copy-done.9
  87.6 7.0 %fusion.3 = f32[2048,128]{1,0:T(8,128)} fusion(bf16[4096,128]{1,0:T(8,128)(2,1)} %bitcast.27, s32[4096]{0:T(1024)S(1)} %get-tuple-element.24, s32[2048]{0:T(1024)S(1)} %bitcast.35), kind=kOutput, calls=%fused_computation.5 | convolution fusion | flops 2155872256 | bytes 2121728 | tf_op jit(solution)/shard_map/dot_general | solution.py:89
  94.7 7.1 %all-to-all-done.1 = bf16[32,128,128]{2,1,0:T(8,128)(2,1)S(1)} async-done(((bf16[32,128,128]{2,1,0:T(8,128)(2,1)}), bf16[32,128,128]{2,1,0:T(8,128)(2,1)S(1)}, u32[]{:S(2)}, u32[]{:S(2)}) %all-to-all-start.1) | async-done | bytes 1048608 | tf_op jit(solution)/shard_map/all_to_all | solution.py:77
  101.7 6.3 %fusion.18 = bf16[2048,128]{1,0:T(8,128)(2,1)S(1)} fusion(f32[2048,128]{1,0:T(8,128)} %fusion.3, bf16[4096,128]{1,0:T(8,128)(2,1)S(1)} %bitcast.26, s32[4096]{0:T(1024)S(1)} %get-tuple-element.23, s32[2048]{0:T(1024)S(1)} %bitcast.36), kind=kOutput, calls=%fused_computation.23 | convolution fusion | flops 2156396544 | bytes 2646016 | tf_op jit(solution)/shard_map/dot_general | solution.py:89
  108.1 13.2 %all_to_all.26 = bf16[4,512,128]{2,1,0:T(8,128)(2,1)S(1)} all-to-all(bf16[4,512,128]{2,1,0:T(8,128)(2,1)S(1)} %bitcast.29), channel_id=1, replica_groups=mesh['rep'=4,'shard'=32] {'rep'}, dimensions={0} | all-to-all | bytes 1048576 | tf_op jit(solution)/shard_map/all_to_all | solution.py:19
  121.3 0.1 reduce_sum.31
  121.4 0.9 broadcast_in_dim.17
  122.2 3.7 %all-to-all-start.4 = ((bf16[4,512,128]{2,1,0:T(8,128)(2,1)}), bf16[4,512,128]{2,1,0:T(8,128)(2,1)S(1)}, u32[]{:S(2)}, u32[]{:S(2)}) async-start(bf16[4,512,128]{2,1,0:T(8,128)(2,1)} %broadcast_in_dim.17), calls=%async_computation.4 | async-start | bytes 1048576 | tf_op jit(solution)/shard_map/all_to_all | solution.py:22
  126.0 1.6 slice.45
  127.5 2.9 %copy.18 = f32[4096,128]{0,1:T(8,128)} copy(f32[4096,128]{1,0:T(8,128)} %param.14) | data formatting | bytes 4194304 | tf_op args[4]
  130.4 4.1 %all-to-all-done.4 = bf16[4,512,128]{2,1,0:T(8,128)(2,1)S(1)} async-done(((bf16[4,512,128]{2,1,0:T(8,128)(2,1)}), bf16[4,512,128]{2,1,0:T(8,128)(2,1)S(1)}, u32[]{:S(2)}, u32[]{:S(2)}) %all-to-all-start.4) | async-done | bytes 524320 | tf_op jit(solution)/shard_map/all_to_all | solution.py:22
  134.5 7.0 %fusion.2 = f32[4096,256]{0,1:T(8,128)S(1)} fusion(s32[2048]{0:T(1024)S(1)} %bitcast.37, bf16[2048,128]{1,0:T(8,128)(2,1)S(1)} %bitcast.28), kind=kOutput, calls=%fused_computation.4 | convolution fusion | flops 4303355904 | bytes 4726784 | tf_op jit(solution)/shard_map/dot_general | solution.py:98
  141.5 0.0 copy-start.5
  141.5 0.0 copy-start.1
  141.5 0.1 compare_reduce_fusion
  141.6 0.2 multiply_reduce_fusion
  141.8 0.5 copy-done.5
  142.2 0.6 fusion.32
  142.8 0.3 copy-done.1
  143.1 1.8 %subtract_select_fusion = f32[4096,128]{0,1:T(8,128)} fusion(f32[4096,128]{0,1:T(8,128)S(1)} %copy-done.1, f32[4096,256]{0,1:T(8,128)S(1)} %fusion.2, f32[4096]{0:T(1024)S(1)} %get-tuple-element.22, pred[4096]{0:T(1024)(128)(4,1)S(1)} %compare_reduce_fusion), kind=kLoop, calls=%fused_computation.31 | loop fusion | flops 2621440 | bytes 6311936 | tf_op jit(solution)/shard_map/jit(_where)/select_n | solution.py:109
  144.9 2.9 %copy.20 = f32[4096,128]{1,0:T(8,128)} copy(f32[4096,128]{0,1:T(8,128)} %subtract_select_fusion) | data formatting | bytes 4194304
  147.8 6.9 %all-gather.2.cloned.1.call-done = bf16[1024,1152]{1,0:T(8,128)(2,1)} async-done(((bf16[8,1152]{1,0:T(8,128)(2,1)}), bf16[1024,1152]{1,0:T(8,128)(2,1)}) %all-gather.2.cloned.1.call-update) | async-done | bytes 2359312 | tf_op jit(solution)/shard_map/all_gather | solution.py:83
  154.7 1.1 convert_reduce_fusion
  155.7 0.6 broadcast_multiply_fusion
  156.3 6.0 %fusion.23 = f32[1024,1024]{1,0:T(8,128)} fusion(bf16[1024,1152]{1,0:T(8,128)(2,1)} %all-gather.2.cloned.1.call-done), kind=kOutput, calls=%fused_computation.26 | convolution fusion | flops 2149580800 | bytes 6291456 | tf_op jit(solution)/shard_map/dot_general | solution.py:103
  (4 shorter events, 0.0 us)
Async XLA Ops:
  7.2 16.9 %copy-start = (bf16[1024,1024]{1,0:T(8,128)(2,1)S(1)}, bf16[1024,1024]{1,0:T(8,128)(2,1)}, u32[]{:S(2)}) copy-start(bf16[1024,1024]{1,0:T(8,128)(2,1)} %param.12) | copy-start | bytes 6291460
  12.2 11.9 %copy-start.7 = (bf16[512,1024]{1,0:T(8,128)(2,1)S(1)}, bf16[512,1024]{1,0:T(8,128)(2,1)}, u32[]{:S(2)}) copy-start(bf16[512,1024]{1,0:T(8,128)(2,1)} %param.10) | copy-start | bytes 3145732
  12.2 44.5 %all-to-all-start = ((bf16[128,8,1152]{2,1,0:T(8,128)(2,1)}), bf16[128,8,1152]{2,1,0:T(8,128)(2,1)}, u32[]{:S(2)}, u32[]{:S(2)}) async-start(bf16[128,8,1152]{2,1,0:T(8,128)(2,1)} %fusion.14), calls=%async_computation | async-start | bytes 4718592 | tf_op jit(solution)/shard_map/all_to_all | solution.py:57
  24.1 1.3 copy-start.8
  24.1 1.3 copy-start.10
  26.9 1.0 copy-start.2
  27.9 1.9 %copy-start.3 = (s32[1,32,256]{2,1,0:T(8,128)S(1)}, s32[1,32,256]{2,1,0:T(8,128)}, u32[]{:S(2)}) copy-start(s32[1,32,256]{2,1,0:T(8,128)} %param.16) | copy-start | bytes 98308
  27.9 1.9 %copy-start.6 = (s32[1,32]{1,0:T(1,128)S(1)}, s32[1,32]{1,0:T(1,128)}, u32[]{:S(2)}) copy-start(s32[1,32]{1,0:T(1,128)} %param.17) | copy-start | bytes 388
  59.5 25.3 %copy-start.4 = (s32[1,32,256]{2,1,0:T(8,128)S(1)}, s32[1,32,256]{2,1,0:T(8,128)}, u32[]{:S(2)}) copy-start(s32[1,32,256]{2,1,0:T(8,128)} %param.18) | copy-start | bytes 98308
  80.5 7.2 %copy-start.9 = (s32[1,2048]{1,0:T(1,128)S(1)}, s32[1,2048]{1,0:T(1,128)}, u32[]{:S(2)}) copy-start(s32[1,2048]{1,0:T(1,128)} %param.19) | copy-start | bytes 24580
  80.5 21.3 %all-to-all-start.1 = ((bf16[32,128,128]{2,1,0:T(8,128)(2,1)}), bf16[32,128,128]{2,1,0:T(8,128)(2,1)S(1)}, u32[]{:S(2)}, u32[]{:S(2)}) async-start(bf16[32,128,128]{2,1,0:T(8,128)(2,1)} %get-tuple-element.19), calls=%async_computation.1 | async-start | bytes 2097152 | tf_op jit(solution)/shard_map/all_to_all | solution.py:77
  84.5 70.1 %all-gather.2.cloned.1.call-start = ((), (), s32[]{:S(2)}) async-start(), calls=%async_computation.5 | async-start | bytes 2377728 | tf_op jit(solution)/shard_map/all_gather | solution.py:83
  122.2 12.3 %all-to-all-start.4 = ((bf16[4,512,128]{2,1,0:T(8,128)(2,1)}), bf16[4,512,128]{2,1,0:T(8,128)(2,1)S(1)}, u32[]{:S(2)}, u32[]{:S(2)}) async-start(bf16[4,512,128]{2,1,0:T(8,128)(2,1)} %broadcast_in_dim.17), calls=%async_computation.4 | async-start | bytes 1048576 | tf_op jit(solution)/shard_map/all_to_all | solution.py:22
  141.5 0.7 copy-start.5
  141.5 1.6 copy-start.1
Sparse Core Ops, SparseCore 0:
  88.3 66.3 all-gather.1

commit v12 on v9

--- a/solution.py
+++ b/solution.py
@@ -98,7 +98,7 @@
         full_w[:, :dim], eye, (((0,), (0,)), ((), ())), preferred_element_type=jnp.float32
     )
     weight_grad = weight_t * scale
-    bias_grad = full_w[:, dim].astype(jnp.float32) * scale
+    bias_grad = jnp.mean(full_w[:, dim:].astype(jnp.float32), axis=1) * scale
     upd_table, upd_accum = adagrad_rows(emb_table, row_accum, row_grads)
     new_table = jnp.where(marks[:, None], upd_table, emb_table)
     new_accum = jnp.where(marks, upd_accum, row_accum)

time: 158 us -> 158 us (level)
  no operation moved by 1% of the time
where the time goes in v12:
time: 158 us; the launch traced here: 155 us
  matrix products  57.4 us (36%)
  waiting for transfers between devices  35 us (22%)
  starting transfers between devices  20.3 us (13%)
  between operations  14.2 us (9%)
  local copies, waits for them, and re-layouts  12.6 us (8%)
  blocking collectives  11.3 us (7%)
  other arithmetic  4.47 us (3%)
    all_to_all x1, waiting for transfers between devices, per_device(): lax.all_to_all(outgoing, 'shard', split_axis=0, concat_axis=0, tiled=True)  27 us
    dot_general x1, matrix products, per_device(): jnp.dot(pick, pooled, preferred_element_type=jnp.float32)  23.1 us
    all_to_all x1, starting transfers between devices, per_device(): got_w = lax.all_to_all(packed, axes, 0, 0, tiled=True)  11.8 us
    all_to_all x1, blocking collectives, rep_sum(): got = lax.all_to_all(parts, 'rep', 0, 0, tiled=True)  11.3 us
    dot_general x1, matrix products, per_device(): jnp.dot(select, incoming_rows, preferred_element_type=jnp.float32)  11.3 us
    unnamed x26, local copies, waits for them, and re-layouts  7.59 us
    dot_general x1, matrix products, per_device(): spread_rows = jnp.dot(place, with_marks, preferred_element_type=jnp.float32)  6.96 us
    dot_general x1, matrix products, per_device(): lax.dot_general(full_w[:, :dim], eye, (((0,), (0,)), ((), ())), preferred...  6 us
  transfers between devices with their start and end apart: 4, of which 3 were waited for; matrix products, arithmetic and copies ran while one was open for 39% of the time, Pallas kernels for 0%

profile of v12, /device:TPU:0, one launch (start us, length us, event | category | flops | bytes accessed | tf_op | source)
XLA Modules:
  0.0 155.4 jit_solution(3606669258622472331)
XLA Ops:
  7.2 0.0 copy-start
  7.2 5.1 %fusion.10 = bf16[128,8,1152]{2,1,0:T(8,128)(2,1)} fusion(bf16[512,1024]{1,0:T(8,128)(2,1)} %param.10, bf16[512,1024]{1,0:T(8,128)(2,1)} %param.11), kind=kOutput, calls=%fused_computation.14 | convolution fusion | flops 1211236352 | bytes 4456448 | tf_op jit(solution)/shard_map/dot_general | solution.py:53
  12.2 0.0 copy-start.7
  12.2 11.8 %all-to-all-start = ((bf16[128,8,1152]{2,1,0:T(8,128)(2,1)}), bf16[128,8,1152]{2,1,0:T(8,128)(2,1)}, u32[]{:S(2)}, u32[]{:S(2)}) async-start(bf16[128,8,1152]{2,1,0:T(8,128)(2,1)} %fusion.10), calls=%async_computation | async-start | bytes 4718592 | tf_op jit(solution)/shard_map/all_to_all | solution.py:57
  24.1 0.0 copy-done
  24.1 0.0 copy-done.7
  24.1 0.0 copy-start.8
  24.1 0.0 copy-start.10
  24.1 1.2 fusion.31
  25.4 0.0 copy-done.8
  25.4 0.0 copy-done.10
  25.4 1.5 fusion.19
  26.9 0.0 copy-start.2
  26.9 1.0 copy-done.2
  27.9 0.0 copy-start.3
  27.9 0.0 copy-start.6
  27.9 0.1 slice.26
  28.0 1.8 %reshape.56 = bf16[3584,128]{1,0:T(8,128)(2,1)} reshape(bf16[512,896]{1,0:T(8,128)(2,1)S(1)} %slice.26) | data formatting | bytes 1835008 | tf_op jit(solution)/shard_map/reshape | solution.py:64
  29.8 0.0 copy-done.3
  29.8 0.0 copy-done.6
  29.9 0.1 iota_compare_fusion.10
  30.0 23.1 %fusion.8 = bf16[8192,128]{1,0:T(8,128)(2,1)} fusion(bf16[3584,128]{1,0:T(8,128)(2,1)} %reshape.56, s32[8192]{0:T(1024)S(1)} %broadcast_select_fusion), kind=kOutput, calls=%fused_computation.10 | convolution fusion | flops 7546601472 | bytes 3047424 | tf_op jit(solution)/shard_map/dot_general | solution.py:72
  53.1 3.7 %all-to-all-done = bf16[128,8,1152]{2,1,0:T(8,128)(2,1)} async-done(((bf16[128,8,1152]{2,1,0:T(8,128)(2,1)}), bf16[128,8,1152]{2,1,0:T(8,128)(2,1)}, u32[]{:S(2)}, u32[]{:S(2)}) %all-to-all-start) | async-done | bytes 2359328 | tf_op jit(solution)/shard_map/all_to_all | solution.py:57
  56.8 4.8 %all-to-all-start.1 = ((bf16[32,256,128]{2,1,0:T(8,128)(2,1)}), bf16[32,256,128]{2,1,0:T(8,128)(2,1)}, u32[]{:S(2)}, u32[]{:S(2)}) async-start(bf16[32,256,128]{2,1,0:T(8,128)(2,1)} %bitcast.20), calls=%async_computation.1 | async-start | bytes 4194304 | tf_op jit(solution)/shard_map/all_to_all | solution.py:76
  61.5 0.0 copy-start.4
  61.6 0.0 copy-start.9
  61.6 0.3 all-gather.2.cloned.1.call-start
  61.8 2.2 %fusion.14 = bf16[1,8,1152]{2,0,1:T(2,128)(2,1)S(1)} fusion(bf16[128,8,1152]{2,1,0:T(8,128)(2,1)} %all-to-all-done), kind=kOutput, calls=%fused_computation.19 | convolution fusion | flops 2359296 | bytes 2377728 | tf_op jit(solution)/shard_map/dot_general | solution.py:78
  64.0 0.6 copy.28
  64.6 0.0 all-gather.2.cloned.1.call-update
  64.6 0.0 copy-done.4
  64.7 27.0 %all-to-all-done.1 = bf16[32,256,128]{2,1,0:T(8,128)(2,1)} async-done(((bf16[32,256,128]{2,1,0:T(8,128)(2,1)}), bf16[32,256,128]{2,1,0:T(8,128)(2,1)}, u32[]{:S(2)}, u32[]{:S(2)}) %all-to-all-start.1) | async-done | bytes 2097184 | tf_op jit(solution)/shard_map/all_to_all | solution.py:76
  91.7 0.0 copy-done.9
  91.7 11.3 %fusion.11 = bf16[2048,128]{1,0:T(8,128)(2,1)S(1)} fusion(bf16[8192,128]{1,0:T(8,128)(2,1)} %bitcast.5, s32[8192]{0:T(1024)S(1)} %bitcast.27, s32[2048]{0:T(1024)S(1)} %bitcast.29), kind=kOutput, calls=%fused_computation.18 | convolution fusion | flops 4312006656 | bytes 2662400 | tf_op jit(solution)/shard_map/dot_general | solution.py:87
  103.0 11.3 %all_to_all.20 = bf16[4,512,128]{2,1,0:T(8,128)(2,1)S(1)} all-to-all(bf16[4,512,128]{2,1,0:T(8,128)(2,1)S(1)} %bitcast.22), channel_id=1, replica_groups=mesh['rep'=4,'shard'=32] {'rep'}, dimensions={0} | all-to-all | bytes 1048576 | tf_op jit(solution)/shard_map/all_to_all | solution.py:19
  114.4 0.1 reduce_sum.31
  114.4 0.9 broadcast_in_dim.17
  115.3 3.5 %all-to-all-start.3 = ((bf16[4,512,128]{2,1,0:T(8,128)(2,1)}), bf16[4,512,128]{2,1,0:T(8,128)(2,1)S(1)}, u32[]{:S(2)}, u32[]{:S(2)}) async-start(bf16[4,512,128]{2,1,0:T(8,128)(2,1)} %broadcast_in_dim.17), calls=%async_computation.3 | async-start | bytes 1048576 | tf_op jit(solution)/shard_map/all_to_all | solution.py:22
  118.8 1.6 %slice.29 = bf16[512,128]{1,0:T(8,128)(2,1)} slice(bf16[512,1024]{1,0:T(8,128)(2,1)} %copy-done.2), slice={[0:512], [0:128]} | slice | bytes 262144 | tf_op jit(solution)/shard_map/slice | solution.py:63
  120.4 2.9 %copy.18 = f32[4096,128]{0,1:T(8,128)} copy(f32[4096,128]{1,0:T(8,128)} %param.14) | data formatting | bytes 4194304 | tf_op args[4]
  123.3 4.3 %all-to-all-done.3 = bf16[4,512,128]{2,1,0:T(8,128)(2,1)S(1)} async-done(((bf16[4,512,128]{2,1,0:T(8,128)(2,1)}), bf16[4,512,128]{2,1,0:T(8,128)(2,1)S(1)}, u32[]{:S(2)}, u32[]{:S(2)}) %all-to-all-start.3) | async-done | bytes 524320 | tf_op jit(solution)/shard_map/all_to_all | solution.py:22
  127.6 7.0 %fusion.6 = f32[4096,256]{0,1:T(8,128)S(1)} fusion(s32[2048]{0:T(1024)S(1)} %bitcast.30, bf16[2048,128]{1,0:T(8,128)(2,1)S(1)} %bitcast.21), kind=kOutput, calls=%fused_computation.8 | convolution fusion | flops 4303355904 | bytes 4726784 | tf_op jit(solution)/shard_map/dot_general | solution.py:92
  134.6 0.0 copy-start.5
  134.6 0.0 copy-start.1
  134.6 0.1 compare_reduce_fusion
  134.7 0.2 multiply_reduce_fusion
  134.8 0.5 copy-done.5
  135.3 0.6 fusion.25
  135.9 0.3 copy-done.1
  136.2 1.8 %subtract_select_fusion = f32[4096,128]{0,1:T(8,128)} fusion(f32[4096,128]{0,1:T(8,128)S(1)} %copy-done.1, f32[4096,256]{0,1:T(8,128)S(1)} %fusion.6, f32[4096]{0:T(1024)S(1)} %get-tuple-element.20, pred[4096]{0:T(1024)(128)(4,1)S(1)} %compare_reduce_fusion), kind=kLoop, calls=%fused_computation.26 | loop fusion | flops 2621440 | bytes 6311936 | tf_op jit(solution)/shard_map/jit(_where)/select_n | solution.py:103
  138.0 2.9 %copy.20 = f32[4096,128]{1,0:T(8,128)} copy(f32[4096,128]{0,1:T(8,128)} %subtract_select_fusion) | data formatting | bytes 4194304
  140.9 0.0 all-gather.2.cloned.1.call-done
  140.9 1.1 convert_reduce_fusion
  142.0 0.6 broadcast_multiply_fusion
  142.6 6.0 %fusion.16 = f32[1024,1024]{1,0:T(8,128)} fusion(bf16[1024,1152]{1,0:T(8,128)(2,1)} %all-gather.2.cloned.1.call-done), kind=kOutput, calls=%fused_computation.21 | convolution fusion | flops 2149580800 | bytes 6291456 | tf_op jit(solution)/shard_map/dot_general | solution.py:97
  (4 shorter events, 0.1 us)
Async XLA Ops:
  7.2 16.9 %copy-start = (bf16[1024,1024]{1,0:T(8,128)(2,1)S(1)}, bf16[1024,1024]{1,0:T(8,128)(2,1)}, u32[]{:S(2)}) copy-start(bf16[1024,1024]{1,0:T(8,128)(2,1)} %param.12) | copy-start | bytes 6291460
  12.2 11.9 %copy-start.7 = (bf16[512,1024]{1,0:T(8,128)(2,1)S(1)}, bf16[512,1024]{1,0:T(8,128)(2,1)}, u32[]{:S(2)}) copy-start(bf16[512,1024]{1,0:T(8,128)(2,1)} %param.10) | copy-start | bytes 3145732
  12.2 44.5 %all-to-all-start = ((bf16[128,8,1152]{2,1,0:T(8,128)(2,1)}), bf16[128,8,1152]{2,1,0:T(8,128)(2,1)}, u32[]{:S(2)}, u32[]{:S(2)}) async-start(bf16[128,8,1152]{2,1,0:T(8,128)(2,1)} %fusion.10), calls=%async_computation | async-start | bytes 4718592 | tf_op jit(solution)/shard_map/all_to_all | solution.py:57
  24.1 1.3 copy-start.8
  24.1 1.3 copy-start.10
  26.9 1.0 copy-start.2
  27.9 1.9 %copy-start.3 = (s32[1,32,256]{2,1,0:T(8,128)S(1)}, s32[1,32,256]{2,1,0:T(8,128)}, u32[]{:S(2)}) copy-start(s32[1,32,256]{2,1,0:T(8,128)} %param.16) | copy-start | bytes 98308
  27.9 1.9 %copy-start.6 = (s32[1,32]{1,0:T(1,128)S(1)}, s32[1,32]{1,0:T(1,128)}, u32[]{:S(2)}) copy-start(s32[1,32]{1,0:T(1,128)} %param.17) | copy-start | bytes 388
  56.8 34.9 %all-to-all-start.1 = ((bf16[32,256,128]{2,1,0:T(8,128)(2,1)}), bf16[32,256,128]{2,1,0:T(8,128)(2,1)}, u32[]{:S(2)}, u32[]{:S(2)}) async-start(bf16[32,256,128]{2,1,0:T(8,128)(2,1)} %bitcast.20), calls=%async_computation.1 | async-start | bytes 4194304 | tf_op jit(solution)/shard_map/all_to_all | solution.py:76
  61.5 3.1 %copy-start.4 = (s32[1,32,256]{2,1,0:T(8,128)S(1)}, s32[1,32,256]{2,1,0:T(8,128)}, u32[]{:S(2)}) copy-start(s32[1,32,256]{2,1,0:T(8,128)} %param.18) | copy-start | bytes 98308
  61.6 30.1 %copy-start.9 = (s32[1,2048]{1,0:T(1,128)S(1)}, s32[1,2048]{1,0:T(1,128)}, u32[]{:S(2)}) copy-start(s32[1,2048]{1,0:T(1,128)} %param.19) | copy-start | bytes 24580
  61.6 79.3 %all-gather.2.cloned.1.call-start = ((), (), s32[]{:S(2)}) async-start(), calls=%async_computation.4 | async-start | bytes 2377728 | tf_op jit(solution)/shard_map/all_gather | solution.py:81
  115.3 12.3 %all-to-all-start.3 = ((bf16[4,512,128]{2,1,0:T(8,128)(2,1)}), bf16[4,512,128]{2,1,0:T(8,128)(2,1)S(1)}, u32[]{:S(2)}, u32[]{:S(2)}) async-start(bf16[4,512,128]{2,1,0:T(8,128)(2,1)} %broadcast_in_dim.17), calls=%async_computation.3 | async-start | bytes 1048576 | tf_op jit(solution)/shard_map/all_to_all | solution.py:22
  134.6 0.7 copy-start.5
  134.6 1.6 %copy-start.1 = (f32[4096,128]{0,1:T(8,128)S(1)}, f32[4096,128]{0,1:T(8,128)}, u32[]{:S(2)}) copy-start(f32[4096,128]{0,1:T(8,128)} %copy.18) | copy-start | bytes 6291460
Sparse Core Ops, SparseCore 0:
  65.3 70.4 all-gather.1

commit v13 on v12

--- a/solution.py
+++ b/solution.py
@@ -80,6 +80,8 @@
     ).astype(jnp.bfloat16)
     full_w = lax.all_gather(mine_w, axes, axis=0, tiled=True)
 
+    marks = jnp.zeros((shard_rows,), jnp.bool_).at[touched_rows[0]].set(True, unique_indices=True)
+    marks, incoming = lax.optimization_barrier((marks, incoming))
     incoming_rows = incoming.reshape(-1, width)
     slot_rows = recv_rows[0].reshape(-1)
     touched = touched_rows[0]
@@ -88,10 +90,7 @@
     touched_grads = rep_sum(local_sums, rep).astype(jnp.bfloat16)
     row_range = jnp.arange(shard_rows, dtype=jnp.int32)
     place = (row_range[:, None] == touched[None, :]).astype(jnp.bfloat16)
-    with_marks = jnp.concatenate([touched_grads, jnp.ones_like(touched_grads)], axis=1)
-    spread_rows = jnp.dot(place, with_marks, preferred_element_type=jnp.float32)
-    row_grads = spread_rows[:, :width]
-    marks = spread_rows[:, width] > 0.5
+    row_grads = jnp.dot(place, touched_grads, preferred_element_type=jnp.float32)
 
     eye = (lax.broadcasted_iota(jnp.int32, (dim, dim), 0) == lax.broadcasted_iota(jnp.int32, (dim, dim), 1)).astype(jnp.bfloat16)
     weight_t = lax.dot_general(

time: 158 us -> 158 us (level)
  waiting for transfers between devices: 35 us -> 24.3 us
  local copies, waits for them, and re-layouts: 12.6 us -> 20.9 us
  matrix products: 57.4 us -> 59.1 us
    all_to_all x1, waiting for transfers between devices: 27 us -> 17.8 us  [per_device(): lax.all_to_all(outgoing, 'shard', split_axis=0, concat_axis=0, tiled=True)]
    scatter x0 -> x1, local copies, waits for them, and re-layouts: none -> 9.13 us  [per_device(): jnp.zeros((shard_rows,), jnp.bool_).at[touched_rows[0]]]
  transfers between devices with their start and end apart: 4 -> 4, of which waited for: 3 -> 3; matrix products, arithmetic and copies ran while one was open for 39% -> 45% of each run, Pallas kernels for 0% -> 0%
where the time goes in v13:
time: 158 us; the launch traced here: 156 us
  matrix products  59.1 us (37%)
  waiting for transfers between devices  24.3 us (15%)
  local copies, waits for them, and re-layouts  20.9 us (13%)
  starting transfers between devices  20.6 us (13%)
  between operations  14.3 us (9%)
  blocking collectives  12.8 us (8%)
  other arithmetic  4.22 us (3%)
    dot_general x1, matrix products, per_device(): jnp.dot(pick, pooled, preferred_element_type=jnp.float32)  23.1 us
    all_to_all x1, waiting for transfers between devices, per_device(): lax.all_to_all(outgoing, 'shard', split_axis=0, concat_axis=0, tiled=True)  17.8 us
    all_to_all x1, blocking collectives, rep_sum(): got = lax.all_to_all(parts, 'rep', 0, 0, tiled=True)  12.8 us
    all_to_all x1, starting transfers between devices, per_device(): got_w = lax.all_to_all(packed, axes, 0, 0, tiled=True)  11.8 us
    dot_general x1, matrix products, per_device(): jnp.dot(select, incoming_rows, preferred_element_type=jnp.float32)  11.3 us
    scatter x1, local copies, waits for them, and re-layouts, per_device(): jnp.zeros((shard_rows,), jnp.bool_).at[touched_rows[0]]  9.13 us
    dot_general x1, matrix products, per_device(): jnp.dot(place, touched_grads, preferred_element_type=jnp.float32)  7.3 us
    unnamed x26, local copies, waits for them, and re-layouts  6.84 us
  transfers between devices with their start and end apart: 4, of which 3 were waited for; matrix products, arithmetic and copies ran while one was open for 45% of the time, Pallas kernels for 0%

profile of v13, /device:TPU:0, one launch (start us, length us, event | category | flops | bytes accessed | tf_op | source)
XLA Modules:
  0.0 156.2 jit_solution(10778949886386760598)
XLA Ops:
  7.2 0.0 copy-start
  7.2 5.1 %fusion.10 = bf16[128,8,1152]{2,1,0:T(8,128)(2,1)} fusion(bf16[512,1024]{1,0:T(8,128)(2,1)} %param.10, bf16[512,1024]{1,0:T(8,128)(2,1)} %param.11), kind=kOutput, calls=%fused_computation.15 | convolution fusion | flops 1211236352 | bytes 4456448 | tf_op jit(solution)/shard_map/dot_general | solution.py:53
  12.2 0.0 copy-start.7
  12.2 0.0 copy-start.3
  12.2 11.8 %all-to-all-start = ((bf16[128,8,1152]{2,1,0:T(8,128)(2,1)}), bf16[128,8,1152]{2,1,0:T(8,128)(2,1)}, u32[]{:S(2)}, u32[]{:S(2)}) async-start(bf16[128,8,1152]{2,1,0:T(8,128)(2,1)} %fusion.10), calls=%async_computation | async-start | bytes 4718592 | tf_op jit(solution)/shard_map/all_to_all | solution.py:57
  24.1 0.0 copy-done.7
  24.1 0.1 iota_compare_fusion.10
  24.2 0.0 copy-done.3
  24.2 0.0 copy-done
  24.2 0.0 copy-start.8
  24.2 0.0 copy-start.9
  24.3 0.0 copy-start.10
  24.3 2.6 %fusion.31 = f32[512,1024]{1,0:T(8,128)S(1)} fusion(bf16[512,1024]{1,0:T(8,128)(2,1)} %param.10, bf16[1024,1024]{1,0:T(8,128)(2,1)S(1)} %copy-done), kind=kOutput, calls=%fused_computation.44 | convolution fusion | flops 1073741824 | bytes 5242880 | tf_op jit(solution)/shard_map/dot_general | solution.py:46
  26.9 0.0 copy-done.8
  26.9 0.0 copy-done.9
  26.9 0.0 copy-done.10
  26.9 1.6 %fusion.19 = bf16[512,1024]{1,0:T(8,128)(2,1)S(1)} fusion(bf16[512,1024]{1,0:T(8,128)(2,1)S(1)} %copy-done.9, f32[512,1024]{1,0:T(8,128)S(1)} %fusion.31, bf16[1024,1024]{1,0:T(8,128)(2,1)S(1)} %copy-done, f32[1024]{0:T(1024)S(1)} %copy-done.10, bf16[512,1024]{1,0:T(8,128)(2,1)S(1)} %copy-done.8), kind=kOutput, calls=%fused_computation.25 | convolution fusion | flops 1078984704 | bytes 7344128 | tf_op jit(solution)/shard_map/dot_general | solution.py:59
  28.5 0.0 copy-start.2
  28.5 1.0 copy-done.2
  29.5 0.1 slice.18
  29.6 1.8 %reshape.83 = bf16[3584,128]{1,0:T(8,128)(2,1)} reshape(bf16[512,896]{1,0:T(8,128)(2,1)S(1)} %slice.18) | data formatting | bytes 1835008 | tf_op jit(solution)/shard_map/reshape | solution.py:64
  31.4 23.1 %fusion.8 = bf16[8192,128]{1,0:T(8,128)(2,1)} fusion(bf16[3584,128]{1,0:T(8,128)(2,1)} %reshape.83, s32[8192]{0:T(1024)S(1)} %broadcast_select_fusion), kind=kOutput, calls=%fused_computation.11 | convolution fusion | flops 7546601472 | bytes 3047424 | tf_op jit(solution)/shard_map/dot_general | solution.py:72
  54.5 2.3 %all-to-all-done = bf16[128,8,1152]{2,1,0:T(8,128)(2,1)} async-done(((bf16[128,8,1152]{2,1,0:T(8,128)(2,1)}), bf16[128,8,1152]{2,1,0:T(8,128)(2,1)}, u32[]{:S(2)}, u32[]{:S(2)}) %all-to-all-start) | async-done | bytes 2359328 | tf_op jit(solution)/shard_map/all_to_all | solution.py:57
  56.8 4.8 %all-to-all-start.1 = ((bf16[32,256,128]{2,1,0:T(8,128)(2,1)}), bf16[32,256,128]{2,1,0:T(8,128)(2,1)}, u32[]{:S(2)}, u32[]{:S(2)}) async-start(bf16[32,256,128]{2,1,0:T(8,128)(2,1)} %bitcast.25), calls=%async_computation.1 | async-start | bytes 4194304 | tf_op jit(solution)/shard_map/all_to_all | solution.py:76
  61.5 0.0 copy-start.4
  61.5 0.0 copy-start.6
  61.6 0.3 all-gather.2.cloned.1.call-start
  61.8 2.2 %fusion.14 = bf16[1,8,1152]{2,0,1:T(2,128)(2,1)S(1)} fusion(bf16[128,8,1152]{2,1,0:T(8,128)(2,1)} %all-to-all-done), kind=kOutput, calls=%fused_computation.20 | convolution fusion | flops 2359296 | bytes 2377728 | tf_op jit(solution)/shard_map/dot_general | solution.py:78
  64.0 0.6 copy.31
  64.6 0.0 all-gather.2.cloned.1.call-update
  64.6 0.0 copy-done.4
  64.7 0.0 copy-done.6
  64.7 9.1 %scatter_custom_fusion = pred[4096]{0:T(1024)(128)(4,1)S(1)} fusion(s32[2048]{0:T(1024)S(1)} %bitcast.35, pred[2048]{0:T(1024)(128)(4,1)S(1)} %broadcast.31, pred[]{:T(512)} %constant.8.clone.1), kind=kCustom, calls=%fused_computation.38 | custom fusion | bytes 4097 | tf_op jit(solution)/shard_map/scatter | solution.py:83
  73.8 17.8 %all-to-all-done.1 = bf16[32,256,128]{2,1,0:T(8,128)(2,1)} async-done(((bf16[32,256,128]{2,1,0:T(8,128)(2,1)}), bf16[32,256,128]{2,1,0:T(8,128)(2,1)}, u32[]{:S(2)}, u32[]{:S(2)}) %all-to-all-start.1) | async-done | bytes 2097184 | tf_op jit(solution)/shard_map/all_to_all | solution.py:76
  91.6 11.3 %fusion.11 = bf16[2048,128]{1,0:T(8,128)(2,1)S(1)} fusion(bf16[8192,128]{1,0:T(8,128)(2,1)} %bitcast.7, s32[8192]{0:T(1024)S(1)} %bitcast.32, s32[2048]{0:T(1024)S(1)} %bitcast.33), kind=kOutput, calls=%fused_computation.19 | convolution fusion | flops 4312006656 | bytes 2662400 | tf_op jit(solution)/shard_map/dot_general | solution.py:89
  103.0 12.8 %all_to_all.20 = bf16[4,512,128]{2,1,0:T(8,128)(2,1)S(1)} all-to-all(bf16[4,512,128]{2,1,0:T(8,128)(2,1)S(1)} %bitcast.27), channel_id=1, replica_groups=mesh['rep'=4,'shard'=32] {'rep'}, dimensions={0} | all-to-all | bytes 1048576 | tf_op jit(solution)/shard_map/all_to_all | solution.py:19
  115.8 0.1 reduce_sum.31
  115.9 0.9 broadcast_in_dim.40
  116.7 3.7 %all-to-all-start.3 = ((bf16[4,512,128]{2,1,0:T(8,128)(2,1)}), bf16[4,512,128]{2,1,0:T(8,128)(2,1)S(1)}, u32[]{:S(2)}, u32[]{:S(2)}) async-start(bf16[4,512,128]{2,1,0:T(8,128)(2,1)} %broadcast_in_dim.40), calls=%async_computation.3 | async-start | bytes 1048576 | tf_op jit(solution)/shard_map/all_to_all | solution.py:22
  120.5 1.6 %slice.21 = bf16[512,128]{1,0:T(8,128)(2,1)} slice(bf16[512,1024]{1,0:T(8,128)(2,1)} %copy-done.2), slice={[0:512], [0:128]} | slice | bytes 262144 | tf_op jit(solution)/shard_map/slice | solution.py:63
  122.0 2.9 %copy.21 = f32[4096,128]{0,1:T(8,128)} copy(f32[4096,128]{1,0:T(8,128)} %param.14) | data formatting | bytes 4194304 | tf_op args[4]
  124.9 4.2 %all-to-all-done.3 = bf16[4,512,128]{2,1,0:T(8,128)(2,1)S(1)} async-done(((bf16[4,512,128]{2,1,0:T(8,128)(2,1)}), bf16[4,512,128]{2,1,0:T(8,128)(2,1)S(1)}, u32[]{:S(2)}, u32[]{:S(2)}) %all-to-all-start.3) | async-done | bytes 524320 | tf_op jit(solution)/shard_map/all_to_all | solution.py:22
  129.1 0.0 copy-start.5
  129.1 0.0 copy-start.1
  129.1 7.3 %multiply_reduce_fusion = (f32[4096]{0:T(1024)S(1)}, f32[4096,128]{0,1:T(8,128)S(1)}) fusion(bf16[2048,128]{1,0:T(8,128)(2,1)S(1)} %bitcast.26, s32[2048]{0:T(1024)S(1)} %bitcast.34), kind=kOutput, calls=%fused_computation.28 | convolution fusion | flops 2156916736 | bytes 2646016 | tf_op jit(solution)/shard_map/dot_general | solution.py:93
  136.4 0.0 copy-done.5
  136.4 0.6 fusion.24
  137.1 0.0 copy-done.1
  137.1 1.7 %subtract_select_fusion = f32[4096,128]{0,1:T(8,128)} fusion(f32[4096,128]{0,1:T(8,128)S(1)} %copy-done.1, f32[4096,128]{0,1:T(8,128)S(1)} %get-tuple-element.31, f32[4096]{0:T(1024)S(1)} %get-tuple-element.29, pred[4096]{0:T(1024)(128)(4,1)S(1)} %scatter_custom_fusion), kind=kLoop, calls=%fused_computation.27 | loop fusion | flops 2621440 | bytes 6311936 | tf_op jit(solution)/shard_map/jit(_where)/select_n | solution.py:102
  138.8 2.9 %copy.23 = f32[4096,128]{1,0:T(8,128)} copy(f32[4096,128]{0,1:T(8,128)} %subtract_select_fusion) | data formatting | bytes 4194304
  141.7 0.0 all-gather.2.cloned.1.call-done
  141.7 1.1 convert_reduce_fusion
  142.8 0.6 broadcast_multiply_fusion
  143.4 6.0 %fusion.16 = f32[1024,1024]{1,0:T(8,128)} fusion(bf16[1024,1152]{1,0:T(8,128)(2,1)} %all-gather.2.cloned.1.call-done), kind=kOutput, calls=%fused_computation.22 | convolution fusion | flops 2149580800 | bytes 6291456 | tf_op jit(solution)/shard_map/dot_general | solution.py:96
  (6 shorter events, 0.1 us)
Async XLA Ops:
  7.2 17.1 %copy-start = (bf16[1024,1024]{1,0:T(8,128)(2,1)S(1)}, bf16[1024,1024]{1,0:T(8,128)(2,1)}, u32[]{:S(2)}) copy-start(bf16[1024,1024]{1,0:T(8,128)(2,1)} %param.12) | copy-start | bytes 6291460
  12.2 11.8 %copy-start.7 = (s32[1,32]{1,0:T(1,128)S(1)}, s32[1,32]{1,0:T(1,128)}, u32[]{:S(2)}) copy-start(s32[1,32]{1,0:T(1,128)} %param.17) | copy-start | bytes 388
  12.2 11.9 %copy-start.3 = (s32[1,32,256]{2,1,0:T(8,128)S(1)}, s32[1,32,256]{2,1,0:T(8,128)}, u32[]{:S(2)}) copy-start(s32[1,32,256]{2,1,0:T(8,128)} %param.16) | copy-start | bytes 98308
  12.2 44.5 %all-to-all-start = ((bf16[128,8,1152]{2,1,0:T(8,128)(2,1)}), bf16[128,8,1152]{2,1,0:T(8,128)(2,1)}, u32[]{:S(2)}, u32[]{:S(2)}) async-start(bf16[128,8,1152]{2,1,0:T(8,128)(2,1)} %fusion.10), calls=%async_computation | async-start | bytes 4718592 | tf_op jit(solution)/shard_map/all_to_all | solution.py:57
  24.2 2.7 %copy-start.8 = (bf16[512,1024]{1,0:T(8,128)(2,1)S(1)}, bf16[512,1024]{1,0:T(8,128)(2,1)}, u32[]{:S(2)}) copy-start(bf16[512,1024]{1,0:T(8,128)(2,1)} %param.10) | copy-start | bytes 3145732
  24.2 2.7 %copy-start.9 = (bf16[512,1024]{1,0:T(8,128)(2,1)S(1)}, bf16[512,1024]{1,0:T(8,128)(2,1)}, u32[]{:S(2)}) copy-start(bf16[512,1024]{1,0:T(8,128)(2,1)} %param.11) | copy-start | bytes 3145732
  24.3 2.7 %copy-start.10 = (f32[1024]{0:T(1024)S(1)}, f32[1024]{0:T(1024)}, u32[]{:S(2)}) copy-start(f32[1024]{0:T(1024)} %param.13) | copy-start | bytes 12292
  28.5 1.0 copy-start.2
  56.8 34.9 %all-to-all-start.1 = ((bf16[32,256,128]{2,1,0:T(8,128)(2,1)}), bf16[32,256,128]{2,1,0:T(8,128)(2,1)}, u32[]{:S(2)}, u32[]{:S(2)}) async-start(bf16[32,256,128]{2,1,0:T(8,128)(2,1)} %bitcast.25), calls=%async_computation.1 | async-start | bytes 4194304 | tf_op jit(solution)/shard_map/all_to_all | solution.py:76
  61.5 3.1 %copy-start.4 = (s32[1,32,256]{2,1,0:T(8,128)S(1)}, s32[1,32,256]{2,1,0:T(8,128)}, u32[]{:S(2)}) copy-start(s32[1,32,256]{2,1,0:T(8,128)} %param.18) | copy-start | bytes 98308
  61.5 3.1 %copy-start.6 = (s32[1,2048]{1,0:T(1,128)S(1)}, s32[1,2048]{1,0:T(1,128)}, u32[]{:S(2)}) copy-start(s32[1,2048]{1,0:T(1,128)} %param.19) | copy-start | bytes 24580
  61.6 80.1 %all-gather.2.cloned.1.call-start = ((), (), s32[]{:S(2)}) async-start(), calls=%async_computation.4 | async-start | bytes 2377728 | tf_op jit(solution)/shard_map/all_gather | solution.py:81
  116.7 12.4 %all-to-all-start.3 = ((bf16[4,512,128]{2,1,0:T(8,128)(2,1)}), bf16[4,512,128]{2,1,0:T(8,128)(2,1)S(1)}, u32[]{:S(2)}, u32[]{:S(2)}) async-start(bf16[4,512,128]{2,1,0:T(8,128)(2,1)} %broadcast_in_dim.40), calls=%async_computation.3 | async-start | bytes 1048576 | tf_op jit(solution)/shard_map/all_to_all | solution.py:22
  129.1 7.3 %copy-start.5 = (f32[4096]{0:T(1024)S(1)}, f32[4096]{0:T(1024)}, u32[]{:S(2)}) copy-start(f32[4096]{0:T(1024)} %param.15) | copy-start | bytes 49156
  129.1 7.9 %copy-start.1 = (f32[4096,128]{0,1:T(8,128)S(1)}, f32[4096,128]{0,1:T(8,128)}, u32[]{:S(2)}) copy-start(f32[4096,128]{0,1:T(8,128)} %copy.21) | copy-start | bytes 6291460
Sparse Core Ops, SparseCore 0:
  65.3 71.6 all-gather.1

commit v14 on v12

--- a/solution.py
+++ b/solution.py
@@ -83,8 +83,10 @@
     incoming_rows = incoming.reshape(-1, width)
     slot_rows = recv_rows[0].reshape(-1)
     touched = touched_rows[0]
-    select = (touched[:, None] == slot_rows[None, :]).astype(jnp.bfloat16)
-    local_sums = jnp.dot(select, incoming_rows, preferred_element_type=jnp.float32)
+    select = (slot_rows[:, None] == touched[None, :]).astype(jnp.bfloat16)
+    local_sums = lax.dot_general(
+        select, incoming_rows, (((0,), (0,)), ((), ())), preferred_element_type=jnp.float32
+    )
     touched_grads = rep_sum(local_sums, rep).astype(jnp.bfloat16)
     row_range = jnp.arange(shard_rows, dtype=jnp.int32)
     place = (row_range[:, None] == touched[None, :]).astype(jnp.bfloat16)

time: 158 us -> 166 us (1.051); the launches traced: 155 us -> 165 us
  matrix products: 57.4 us -> 67.2 us
    dot_general x1, matrix products: 11.3 us -> 21.2 us  [per_device(): lax.dot_general(select, incoming_rows, (((0,), (0,)), ((), ())), preferre...]
  transfers between devices with their start and end apart: 4 -> 4, of which waited for: 3 -> 3; matrix products, arithmetic and copies ran while one was open for 39% -> 42% of each run, Pallas kernels for 0% -> 0%
where the time goes in v14:
time: 166 us; the launch traced here: 165 us
  matrix products  67.2 us (40%)
  waiting for transfers between devices  34.3 us (21%)
  starting transfers between devices  20.3 us (12%)
  between operations  14.2 us (9%)
  local copies, waits for them, and re-layouts  12.5 us (8%)
  blocking collectives  12 us (7%)
  other arithmetic  4.47 us (3%)
    all_to_all x1, waiting for transfers between devices, per_device(): lax.all_to_all(outgoing, 'shard', split_axis=0, concat_axis=0, tiled=True)  27 us
    dot_general x1, matrix products, per_device(): jnp.dot(pick, pooled, preferred_element_type=jnp.float32)  23.1 us
    dot_general x1, matrix products, per_device(): lax.dot_general(select, incoming_rows, (((0,), (0,)), ((), ())), preferre...  21.2 us
    all_to_all x1, blocking collectives, rep_sum(): got = lax.all_to_all(parts, 'rep', 0, 0, tiled=True)  12 us
    all_to_all x1, starting transfers between devices, per_device(): got_w = lax.all_to_all(packed, axes, 0, 0, tiled=True)  11.8 us
    unnamed x26, local copies, waits for them, and re-layouts  7.58 us
    dot_general x1, matrix products, per_device(): spread_rows = jnp.dot(place, with_marks, preferred_element_type=jnp.float32)  6.96 us
    dot_general x1, matrix products, per_device(): lax.dot_general(full_w[:, :dim], eye, (((0,), (0,)), ((), ())), preferred...  5.99 us
  transfers between devices with their start and end apart: 4, of which 3 were waited for; matrix products, arithmetic and copies ran while one was open for 42% of the time, Pallas kernels for 0%

profile of v14, /device:TPU:0, one launch (start us, length us, event | category | flops | bytes accessed | tf_op | source)
XLA Modules:
  0.0 165.1 jit_solution(18252179450764580696)
XLA Ops:
  7.2 0.0 copy-start
  7.2 5.1 %fusion.10 = bf16[128,8,1152]{2,1,0:T(8,128)(2,1)} fusion(bf16[512,1024]{1,0:T(8,128)(2,1)} %param.10, bf16[512,1024]{1,0:T(8,128)(2,1)} %param.11), kind=kOutput, calls=%fused_computation.14 | convolution fusion | flops 1211236352 | bytes 4456448 | tf_op jit(solution)/shard_map/dot_general | solution.py:53
  12.2 0.0 copy-start.7
  12.2 11.8 %all-to-all-start = ((bf16[128,8,1152]{2,1,0:T(8,128)(2,1)}), bf16[128,8,1152]{2,1,0:T(8,128)(2,1)}, u32[]{:S(2)}, u32[]{:S(2)}) async-start(bf16[128,8,1152]{2,1,0:T(8,128)(2,1)} %fusion.10), calls=%async_computation | async-start | bytes 4718592 | tf_op jit(solution)/shard_map/all_to_all | solution.py:57
  24.1 0.0 copy-done
  24.1 0.0 copy-done.7
  24.1 0.0 copy-start.8
  24.1 0.0 copy-start.10
  24.1 1.2 fusion.31
  25.4 0.0 copy-done.8
  25.4 0.0 copy-done.10
  25.4 1.5 fusion.19
  26.9 0.0 copy-start.2
  26.9 1.0 copy-done.2
  27.9 0.0 copy-start.3
  27.9 0.0 copy-start.6
  27.9 0.1 slice.26
  28.0 1.8 %reshape.55 = bf16[3584,128]{1,0:T(8,128)(2,1)} reshape(bf16[512,896]{1,0:T(8,128)(2,1)S(1)} %slice.26) | data formatting | bytes 1835008 | tf_op jit(solution)/shard_map/reshape | solution.py:64
  29.8 0.0 copy-done.3
  29.8 0.0 copy-done.6
  29.9 0.1 iota_compare_fusion.10
  30.0 23.1 %fusion.8 = bf16[8192,128]{1,0:T(8,128)(2,1)} fusion(bf16[3584,128]{1,0:T(8,128)(2,1)} %reshape.55, s32[8192]{0:T(1024)S(1)} %broadcast_select_fusion), kind=kOutput, calls=%fused_computation.10 | convolution fusion | flops 7546601472 | bytes 3047424 | tf_op jit(solution)/shard_map/dot_general | solution.py:72
  53.1 3.7 %all-to-all-done = bf16[128,8,1152]{2,1,0:T(8,128)(2,1)} async-done(((bf16[128,8,1152]{2,1,0:T(8,128)(2,1)}), bf16[128,8,1152]{2,1,0:T(8,128)(2,1)}, u32[]{:S(2)}, u32[]{:S(2)}) %all-to-all-start) | async-done | bytes 2359328 | tf_op jit(solution)/shard_map/all_to_all | solution.py:57
  56.8 4.8 %all-to-all-start.1 = ((bf16[32,256,128]{2,1,0:T(8,128)(2,1)}), bf16[32,256,128]{2,1,0:T(8,128)(2,1)}, u32[]{:S(2)}, u32[]{:S(2)}) async-start(bf16[32,256,128]{2,1,0:T(8,128)(2,1)} %bitcast.20), calls=%async_computation.1 | async-start | bytes 4194304 | tf_op jit(solution)/shard_map/all_to_all | solution.py:76
  61.5 0.0 copy-start.4
  61.6 0.0 copy-start.9
  61.6 0.3 all-gather.2.cloned.1.call-start
  61.8 2.2 %fusion.14 = bf16[1,8,1152]{2,0,1:T(2,128)(2,1)S(1)} fusion(bf16[128,8,1152]{2,1,0:T(8,128)(2,1)} %all-to-all-done), kind=kOutput, calls=%fused_computation.19 | convolution fusion | flops 2359296 | bytes 2377728 | tf_op jit(solution)/shard_map/dot_general | solution.py:78
  64.0 0.6 copy.28
  64.6 0.0 all-gather.2.cloned.1.call-update
  64.6 0.0 copy-done.4
  64.7 27.0 %all-to-all-done.1 = bf16[32,256,128]{2,1,0:T(8,128)(2,1)} async-done(((bf16[32,256,128]{2,1,0:T(8,128)(2,1)}), bf16[32,256,128]{2,1,0:T(8,128)(2,1)}, u32[]{:S(2)}, u32[]{:S(2)}) %all-to-all-start.1) | async-done | bytes 2097184 | tf_op jit(solution)/shard_map/all_to_all | solution.py:76
  91.7 0.0 copy-done.9
  91.7 21.2 %fusion.11 = bf16[2048,128]{1,0:T(8,128)(2,1)S(1)} fusion(bf16[8192,128]{1,0:T(8,128)(2,1)} %bitcast.5, s32[2048]{0:T(1024)S(1)} %bitcast.29, s32[8192]{0:T(1024)S(1)} %bitcast.27), kind=kOutput, calls=%fused_computation.18 | convolution fusion | flops 4312006656 | bytes 2662400 | tf_op jit(solution)/shard_map/dot_general | solution.py:87
  112.8 12.0 %all_to_all.20 = bf16[4,512,128]{2,1,0:T(8,128)(2,1)S(1)} all-to-all(bf16[4,512,128]{2,1,0:T(8,128)(2,1)S(1)} %bitcast.22), channel_id=1, replica_groups=mesh['rep'=4,'shard'=32] {'rep'}, dimensions={0} | all-to-all | bytes 1048576 | tf_op jit(solution)/shard_map/all_to_all | solution.py:19
  124.8 0.1 reduce_sum.31
  124.9 0.9 broadcast_in_dim.17
  125.8 3.5 %all-to-all-start.3 = ((bf16[4,512,128]{2,1,0:T(8,128)(2,1)}), bf16[4,512,128]{2,1,0:T(8,128)(2,1)S(1)}, u32[]{:S(2)}, u32[]{:S(2)}) async-start(bf16[4,512,128]{2,1,0:T(8,128)(2,1)} %broadcast_in_dim.17), calls=%async_computation.3 | async-start | bytes 1048576 | tf_op jit(solution)/shard_map/all_to_all | solution.py:22
  129.3 1.6 slice.29
  130.8 2.9 %copy.18 = f32[4096,128]{0,1:T(8,128)} copy(f32[4096,128]{1,0:T(8,128)} %param.14) | data formatting | bytes 4194304 | tf_op args[4]
  133.7 3.6 %all-to-all-done.3 = bf16[4,512,128]{2,1,0:T(8,128)(2,1)S(1)} async-done(((bf16[4,512,128]{2,1,0:T(8,128)(2,1)}), bf16[4,512,128]{2,1,0:T(8,128)(2,1)S(1)}, u32[]{:S(2)}, u32[]{:S(2)}) %all-to-all-start.3) | async-done | bytes 524320 | tf_op jit(solution)/shard_map/all_to_all | solution.py:22
  137.3 7.0 %fusion.6 = f32[4096,256]{0,1:T(8,128)S(1)} fusion(s32[2048]{0:T(1024)S(1)} %bitcast.30, bf16[2048,128]{1,0:T(8,128)(2,1)S(1)} %bitcast.21), kind=kOutput, calls=%fused_computation.8 | convolution fusion | flops 4303355904 | bytes 4726784 | tf_op jit(solution)/shard_map/dot_general | solution.py:94
  144.3 0.0 copy-start.5
  144.3 0.0 copy-start.1
  144.3 0.1 compare_reduce_fusion
  144.4 0.2 multiply_reduce_fusion
  144.5 0.5 copy-done.5
  145.0 0.6 fusion.25
  145.6 0.3 copy-done.1
  145.9 1.8 %subtract_select_fusion = f32[4096,128]{0,1:T(8,128)} fusion(f32[4096,128]{0,1:T(8,128)S(1)} %copy-done.1, f32[4096,256]{0,1:T(8,128)S(1)} %fusion.6, f32[4096]{0:T(1024)S(1)} %get-tuple-element.20, pred[4096]{0:T(1024)(128)(4,1)S(1)} %compare_reduce_fusion), kind=kLoop, calls=%fused_computation.26 | loop fusion | flops 2621440 | bytes 6311936 | tf_op jit(solution)/shard_map/jit(_where)/select_n | solution.py:105
  147.7 2.9 %copy.20 = f32[4096,128]{1,0:T(8,128)} copy(f32[4096,128]{0,1:T(8,128)} %subtract_select_fusion) | data formatting | bytes 4194304
  150.6 0.0 all-gather.2.cloned.1.call-done
  150.6 1.1 convert_reduce_fusion
  151.7 0.6 broadcast_multiply_fusion
  152.2 6.0 %fusion.16 = f32[1024,1024]{1,0:T(8,128)} fusion(bf16[1024,1152]{1,0:T(8,128)(2,1)} %all-gather.2.cloned.1.call-done), kind=kOutput, calls=%fused_computation.21 | convolution fusion | flops 2149580800 | bytes 6291456 | tf_op jit(solution)/shard_map/dot_general | solution.py:99
  (4 shorter events, 0.1 us)
Async XLA Ops:
  7.2 16.9 %copy-start = (bf16[1024,1024]{1,0:T(8,128)(2,1)S(1)}, bf16[1024,1024]{1,0:T(8,128)(2,1)}, u32[]{:S(2)}) copy-start(bf16[1024,1024]{1,0:T(8,128)(2,1)} %param.12) | copy-start | bytes 6291460
  12.2 11.9 %copy-start.7 = (bf16[512,1024]{1,0:T(8,128)(2,1)S(1)}, bf16[512,1024]{1,0:T(8,128)(2,1)}, u32[]{:S(2)}) copy-start(bf16[512,1024]{1,0:T(8,128)(2,1)} %param.10) | copy-start | bytes 3145732
  12.2 44.5 %all-to-all-start = ((bf16[128,8,1152]{2,1,0:T(8,128)(2,1)}), bf16[128,8,1152]{2,1,0:T(8,128)(2,1)}, u32[]{:S(2)}, u32[]{:S(2)}) async-start(bf16[128,8,1152]{2,1,0:T(8,128)(2,1)} %fusion.10), calls=%async_computation | async-start | bytes 4718592 | tf_op jit(solution)/shard_map/all_to_all | solution.py:57
  24.1 1.3 copy-start.8
  24.1 1.3 copy-start.10
  26.9 1.0 copy-start.2
  27.9 1.9 %copy-start.3 = (s32[1,32,256]{2,1,0:T(8,128)S(1)}, s32[1,32,256]{2,1,0:T(8,128)}, u32[]{:S(2)}) copy-start(s32[1,32,256]{2,1,0:T(8,128)} %param.16) | copy-start | bytes 98308
  27.9 1.9 %copy-start.6 = (s32[1,32]{1,0:T(1,128)S(1)}, s32[1,32]{1,0:T(1,128)}, u32[]{:S(2)}) copy-start(s32[1,32]{1,0:T(1,128)} %param.17) | copy-start | bytes 388
  56.8 34.9 %all-to-all-start.1 = ((bf16[32,256,128]{2,1,0:T(8,128)(2,1)}), bf16[32,256,128]{2,1,0:T(8,128)(2,1)}, u32[]{:S(2)}, u32[]{:S(2)}) async-start(bf16[32,256,128]{2,1,0:T(8,128)(2,1)} %bitcast.20), calls=%async_computation.1 | async-start | bytes 4194304 | tf_op jit(solution)/shard_map/all_to_all | solution.py:76
  61.5 3.1 %copy-start.4 = (s32[1,32,256]{2,1,0:T(8,128)S(1)}, s32[1,32,256]{2,1,0:T(8,128)}, u32[]{:S(2)}) copy-start(s32[1,32,256]{2,1,0:T(8,128)} %param.18) | copy-start | bytes 98308
  61.6 30.1 %copy-start.9 = (s32[1,2048]{1,0:T(1,128)S(1)}, s32[1,2048]{1,0:T(1,128)}, u32[]{:S(2)}) copy-start(s32[1,2048]{1,0:T(1,128)} %param.19) | copy-start | bytes 24580
  61.6 89.0 %all-gather.2.cloned.1.call-start = ((), (), s32[]{:S(2)}) async-start(), calls=%async_computation.4 | async-start | bytes 2377728 | tf_op jit(solution)/shard_map/all_gather | solution.py:81
  125.8 11.5 %all-to-all-start.3 = ((bf16[4,512,128]{2,1,0:T(8,128)(2,1)}), bf16[4,512,128]{2,1,0:T(8,128)(2,1)S(1)}, u32[]{:S(2)}, u32[]{:S(2)}) async-start(bf16[4,512,128]{2,1,0:T(8,128)(2,1)} %broadcast_in_dim.17), calls=%async_computation.3 | async-start | bytes 1048576 | tf_op jit(solution)/shard_map/all_to_all | solution.py:22
  144.3 0.7 copy-start.5
  144.3 1.6 copy-start.1
Sparse Core Ops, SparseCore 0:
  65.3 69.9 all-gather.1
